TPU v7x, 128 devices: a whole 4x4x4 slice. The times are simulated.
128 devices in a mesh: lat: 8 (over z, x_lo), lon: 16 (over y, x_hi, core).
Axes of the slice: x: 4 (x_hi: 2, x_lo: 2; x = x_hi * 2 + x_lo), y: 4, z: 4, core: 2. Of those that a mesh axis runs over, the one named last changes fastest.
Arguments:
- radiances: bfloat16 [131072, 8461], P(('lat', 'lon')), may hold values from -6 to 6
- project_weight: bfloat16 [8461, 256], replicated, may hold values from -0.0625 to 0.0625
- tile_ids: int32 [131072], P(('lat', 'lon')), may hold values from 0 to 127, as said below
- slot_offsets: int32 [131072], P(('lat', 'lon')), may hold values from 0 to 2559, as said below
- tile_counts: int32 [8, 16], P('lat', 'lon'), may hold values from 512 to 2560, as said below
- setconv_weights: bfloat16 [512, 512, 2560], P('lat', 'lon'), may hold values from 0.049804688 to 1
- conv1_weight: bfloat16 [3, 3, 256, 256], replicated, may hold values from -0.125 to 0.125
- conv2_weight: bfloat16 [3, 3, 256, 256], replicated, may hold values from -0.125 to 0.125
Outputs:
- encoded: bfloat16 [128, 128, 256], P('lat', 'lon')
Inputs may be any that keep to these rules, and one draw needn't show every extreme that they name: `tile_ids`: A device's observations bound for one tile stand next to each other; one device sends at most 28 observations to one tile, a number reached in every draw. `slot_offsets`: the observations bound for one tile hold the offsets 0 to its count minus 1, each once. `tile_counts`: each entry is the number of observations whose tile_ids name that tile; 2560 is reached in every draw.
All inputs are finite; a program needn't handle non-finite values.
Results may differ from a plain program's by a relative error of at most 0.009.
Values may be sent and summed in bfloat16 or wider, within the bound.
No kernel may reach another device: no remote copies, remote signals or barrier semaphores. Data moves between devices by JAX's collectives and lax.ppermute only.
A program may use at most 512 MiB of HBM per device.

v0:
```python
import jax
import jax.numpy as jnp
from jax import lax
from jax.sharding import PartitionSpec as P


def shifted_2(value, axis, by):
    peers = lax.axis_size(axis)
    pairs = [(i, i + by) for i in range(peers) if 0 <= i + by < peers]
    return lax.ppermute(value, axis, pairs)


def passed_along(value, axis, steps):
    count = lax.axis_size(axis)
    pairs = [(source, (source + steps) % count) for source in range(count)]
    return lax.ppermute(value, axis, pairs)


def stride_conv(field, kernel):
    height, breadth, depth = field.shape
    half_rows, half_cols = (height // 2, breadth // 2)
    upper_rim = shifted_2(field[-1:], "lat", 1)
    west_column = jnp.concatenate([upper_rim[:, -1:], field[:, -1:]], axis=0)
    west_rim = passed_along(west_column, "lon", 1)[:, 0]
    paired = field.reshape(half_rows, 2, half_cols, 2 * depth)
    even_rows = paired[:, 0]
    odd_rows = paired[:, 1]
    upper_paired = upper_rim.reshape(1, half_cols, 2 * depth)
    above_rows = jnp.concatenate([upper_paired, odd_rows[:-1]], axis=0)
    tap_rows = (above_rows, even_rows, odd_rows)
    zero_block = jnp.zeros((depth, depth), kernel.dtype)
    summed = jnp.zeros((half_rows * half_cols, 2 * depth), jnp.float32)
    west_sum = jnp.zeros((half_rows, depth), jnp.float32)
    for row_tap in range(3):
        upper_half = jnp.concatenate([kernel[row_tap, 1], zero_block], axis=1)
        lower_half = jnp.concatenate([kernel[row_tap, 2], kernel[row_tap, 0]], axis=1)
        stacked = jnp.concatenate([upper_half, lower_half], axis=0)
        rows_flat = tap_rows[row_tap].reshape(-1, 2 * depth)
        summed = summed + jnp.dot(rows_flat, stacked, preferred_element_type=jnp.float32)
        west_rows = west_rim[row_tap : row_tap + height : 2]
        west_sum = west_sum + jnp.dot(
            west_rows, kernel[row_tap, 0], preferred_element_type=jnp.float32
        )
    summed = summed.reshape(half_rows, half_cols, 2 * depth)
    central = summed[:, :, :depth]
    westward = summed[:, :, depth:]
    shifted = jnp.concatenate([west_sum[:, None, :], westward[:, :-1]], axis=1)
    return central + shifted


def body(
    radiances,
    project_weight,
    tile_ids,
    slot_offsets,
    tile_counts,
    setconv_weights,
    conv1_weight,
    conv2_weight,
):
    lat_size = lax.axis_size("lat")
    lon_size = lax.axis_size("lon")
    peer_count = lat_size * lon_size
    obs_count = radiances.shape[0]
    capacity = 7 * (obs_count // peer_count) // 2
    slot_count = setconv_weights.shape[2]
    channel_count = project_weight.shape[1]
    targets = jnp.arange(peer_count, dtype=jnp.int32)
    row_index = jnp.arange(obs_count, dtype=jnp.int32)
    matches = tile_ids[:, None] == targets[None, :]
    run_counts = jnp.sum(matches.astype(jnp.int32), axis=0)
    run_starts = jnp.min(jnp.where(matches, row_index[:, None], obs_count), axis=0)
    within = jnp.arange(capacity, dtype=jnp.int32)
    source_rows = jnp.minimum(run_starts[:, None] + within[None, :], obs_count - 1).reshape(-1)
    valid_slot = (within[None, :] < run_counts[:, None]).reshape(-1)
    payload = jnp.dot(radiances, project_weight, preferred_element_type=jnp.float32).astype(
        jnp.bfloat16
    )
    row_width = payload.shape[1]
    packed = jnp.where(
        valid_slot[:, None], jnp.take(payload, source_rows, axis=0), jnp.zeros((), jnp.bfloat16)
    )
    offsets_out = jnp.where(valid_slot, jnp.take(slot_offsets, source_rows, axis=0), slot_count)
    arrived, arrived_offsets = (
        lax.all_to_all(
            packed.reshape(peer_count, capacity, row_width),
            ("lat", "lon"),
            split_axis=0,
            concat_axis=0,
            tiled=True,
        ),
        lax.all_to_all(
            offsets_out.reshape(peer_count, capacity),
            ("lat", "lon"),
            split_axis=0,
            concat_axis=0,
            tiled=True,
        ),
    )
    arrived = arrived.reshape(-1, row_width)
    arrived_offsets = arrived_offsets.reshape(-1)
    slot_table = (
        jnp.arange(slot_count, dtype=jnp.int32)[:, None] == arrived_offsets[None, :]
    ).astype(jnp.bfloat16)
    obs_block = jnp.dot(slot_table, arrived, preferred_element_type=jnp.float32).astype(
        jnp.bfloat16
    )
    tile_rows, tile_cols = (setconv_weights.shape[0], setconv_weights.shape[1])
    weights_flat = setconv_weights.reshape(-1, slot_count)
    live_mask = jnp.arange(slot_count, dtype=jnp.int32) < tile_counts.reshape(-1)[0]
    masked = jnp.where(live_mask[None, :], weights_flat, jnp.zeros((), jnp.bfloat16))
    numerator = jnp.dot(masked, obs_block, preferred_element_type=jnp.float32)
    density = jnp.sum(masked, axis=1, dtype=jnp.float32)
    grid = (
        (numerator / jnp.sqrt(density)[:, None])
        .astype(jnp.bfloat16)
        .reshape(tile_rows, tile_cols, channel_count)
    )
    hidden = jax.nn.gelu(stride_conv(grid, conv1_weight)).astype(jnp.bfloat16)
    return stride_conv(hidden, conv2_weight).astype(jnp.bfloat16)


def solution(mesh):
    in_specs = (
        P(("lat", "lon"), None),
        P(),
        P(("lat", "lon")),
        P(("lat", "lon")),
        P("lat", "lon"),
        P("lat", "lon", None),
        P(),
        P(),
    )
    out_specs = P("lat", "lon", None)
    return jax.shard_map(body, mesh=mesh, in_specs=in_specs, out_specs=out_specs, check_vma=False)
```

profile of v0, /device:TPU:0, one launch (start us, length us, event | category | flops | bytes accessed | tf_op | source)
XLA Modules:
  0.0 156.7 jit_solution(283561641565456429)
XLA Ops:
  1.2 12.9 %gather_fusion = s32[3584]{0:T(1024)S(1)} fusion(s32[1024]{0:T(1024)S(1)} %copy-done, s32[4096]{0:T(1024)S(1)} %pad_clamp_fusion), kind=kCustom, calls=%fused_computation | custom fusion | bytes 43008 | tf_op jit(solution)/shard_map/jit(_take)/gather | solution.py:83
  15.0 11.2 %all-to-all-start = ((s32[128,1,28]{2,1,0:T(1,128)}), s32[128,1,28]{2,1,0:T(1,128)S(1)}, u32[]{:S(2)}, u32[]{:S(2)}) async-start(s32[128,1,28]{2,1,0:T(1,128)} %bitcast.2), calls=%async_computation | async-start | bytes 131072 | tf_op jit(solution)/shard_map/all_to_all | solution.py:92
  26.3 12.0 %convolution_convert_fusion = bf16[1024,256]{1,0:T(8,128)(2,1)S(1)} fusion(bf16[1024,8461]{0,1:T(8,128)(2,1)} %param.8, bf16[8461,256]{1,0:T(8,128)(2,1)} %param.9), kind=kOutput, calls=%fused_computation.13 | convolution fusion | flops 4436262912 | bytes 22184448 | tf_op jit(solution)/shard_map/dot_general | solution.py:76
  38.3 10.9 %gather_fusion.1 = bf16[3584,256]{1,0:T(8,128)(2,1)} fusion(bf16[1024,256]{1,0:T(8,128)(2,1)S(1)} %convolution_convert_fusion, s32[4096]{0:T(1024)S(1)} %pad_clamp_fusion), kind=kCustom, calls=%fused_computation.1 | custom fusion | bytes 3684352 | tf_op jit(solution)/shard_map/jit(_take)/gather | solution.py:81
  49.2 2.5 %gather.15 = bf16[128,28,256]{2,1,0:T(8,128)(2,1)S(1)} reshape(bf16[3584,256]{1,0:T(8,128)(2,1)} %gather_fusion.1) | data formatting | bytes 3670016 | tf_op jit(solution)/shard_map/jit(_take)/gather | solution.py:81
  52.4 1.0 slice_bitcast_fusion.15
  53.4 6.3 %convert_reduce_fusion = f32[64,32]{1,0:T(8,128)S(1)} fusion(bf16[64,32,2560]{2,1,0:T(8,128)(2,1)} %param.13, pred[2560]{0:T(1024)(128)(4,1)S(1)} %iota_compare_fusion.8), kind=kLoop, calls=%fused_computation.4 | loop fusion | flops 15726592 | bytes 10496512 | tf_op jit(solution)/shard_map/reduce_sum | solution.py:113
  59.7 3.5 %select_select_fusion = bf16[128,28,256]{2,1,0:T(8,128)(2,1)} fusion(bf16[128,28,256]{2,1,0:T(8,128)(2,1)S(1)} %gather.15, pred[128,28]{1,0:T(8,128)(4,1)S(1)} %get-tuple-element.28, pred[128,28]{1,0:T(8,128)(4,1)S(1)} %get-tuple-element.27), kind=kLoop, calls=%fused_computation.10 | loop fusion | flops 1835008 | bytes 3677184 | tf_op jit(solution)/shard_map/jit(_where)/select_n | solution.py:80
  63.2 1.0 slice_bitcast_fusion.6
  64.3 9.8 %all-to-all-start.1 = ((bf16[128,28,256]{2,1,0:T(8,128)(2,1)}), bf16[128,28,256]{2,1,0:T(8,128)(2,1)S(1)}, u32[]{:S(2)}, u32[]{:S(2)}) async-start(bf16[128,28,256]{2,1,0:T(8,128)(2,1)} %select_select_fusion), calls=%async_computation.1 | async-start | bytes 4194304 | tf_op jit(solution)/shard_map/all_to_all | solution.py:85
  74.1 10.0 %bitcast_select_fusion = bf16[2048,2560]{1,0:T(8,128)(2,1)} fusion(bf16[64,32,2560]{2,1,0:T(8,128)(2,1)} %param.13, pred[2560]{0:T(1024)(128)(4,1)S(1)} %iota_compare_fusion.8), kind=kLoop, calls=%fused_computation.6 | loop fusion | flops 5242880 | bytes 20974080 | tf_op jit(solution)/shard_map/jit(_where)/select_n | solution.py:111
  85.5 18.1 %all-to-all-done.1 = bf16[128,28,256]{2,1,0:T(8,128)(2,1)S(1)} async-done(((bf16[128,28,256]{2,1,0:T(8,128)(2,1)}), bf16[128,28,256]{2,1,0:T(8,128)(2,1)S(1)}, u32[]{:S(2)}, u32[]{:S(2)}) %all-to-all-start.1) | async-done | bytes 1835040 | tf_op jit(solution)/shard_map/all_to_all | solution.py:85
  103.6 1.4 reshape.214
  105.0 18.0 %fusion.3 = bf16[2048,256]{1,0:T(8,128)(2,1)S(1)} fusion(bf16[2048,2560]{1,0:T(8,128)(2,1)} %bitcast_select_fusion, f32[2048]{0:T(1024)S(1)} %sqrt.11, bf16[3584,256]{1,0:T(8,128)(2,1)} %reshape.214, s32[3584]{0:T(1024)S(1)} %eq.32), kind=kOutput, calls=%fused_computation.9 | convolution fusion | flops 7392854016 | bytes 13391872 | tf_op jit(solution)/shard_map/dot_general | solution.py:112
  123.4 2.7 %collective-permute-start = (bf16[1,32,256]{2,1,0:T(8,128)(2,1)S(1)}, bf16[1,32,256]{2,1,0:T(8,128)(2,1)S(1)}, u32[]{:S(2)}, u32[]{:S(2)}) collective-permute-start(bf16[1,32,256]{2,1,0:T(8,128)(2,1)S(1)} %slice_bitcast_fusion.24), channel_id=1, source_target_pairs={{0,16},{16,32},{32,48},{48,64},{64,80},{80,96},{96,112},{1,17},{17... | collective-permute-start | bytes 49160 | tf_op jit(solution)/shard_map/ppermute | solution.py:10
  127.1 1.4 fusion.26
  130.3 1.8 %convolution_add_fusion.1 = f32[512,512]{1,0:T(8,128)S(1)} fusion(f32[512,512]{1,0:T(8,128)} %fusion.26, bf16[512,512]{1,0:T(8,128)(2,1)S(1)} %bitcast.98, bf16[256,256]{1,0:T(8,128)(2,1)} %get-tuple-element.23, bf16[256,256]{1,0:T(8,128)(2,1)S(1)} %copy-done.17, bf16[256,256]{1,0:T(8,128)(2,1)S(1)} %copy-done.18), kind=kOutput, calls=%fused_computation.12 | convolution fusion | flops 270794752 | bytes 3014656 | tf_op jit(solution)/shard_map/dot_general | solution.py:39
  133.0 4.5 %collective-permute-done.1 = bf16[65,1,256]{2,0,1:T(8,128)(2,1)} collective-permute-done((bf16[65,1,256]{2,0,1:T(8,128)(2,1)}, bf16[65,1,256]{2,0,1:T(8,128)(2,1)}, u32[]{:S(2)}, u32[]{:S(2)}) %collective-permute-start.1) | collective-permute-done | bytes 33312 | tf_op jit(solution)/shard_map/ppermute | solution.py:16
  141.0 3.5 %collective-permute-start.2 = (bf16[1,16,256]{2,0,1:T(2,128)(2,1)S(1)}, bf16[1,16,256]{2,0,1:T(2,128)(2,1)S(1)}, u32[]{:S(2)}, u32[]{:S(2)}) collective-permute-start(bf16[1,16,256]{2,0,1:T(2,128)(2,1)S(1)} %slice.196), channel_id=1, source_target_pairs={{0,16},{16,32},{32,48},{48,64},{64,80},{80,96},{96,112},{1,17},{17... | collective-permute-start | bytes 24584 | tf_op jit(solution)/shard_map/ppermute | solution.py:10
  144.6 1.3 collective-permute-done.2
  147.3 5.5 %collective-permute-done.3 = bf16[33,1,256]{2,0,1:T(8,128)(2,1)S(1)} collective-permute-done((bf16[33,1,256]{2,0,1:T(8,128)(2,1)S(1)}, bf16[33,1,256]{2,0,1:T(8,128)(2,1)S(1)}, u32[]{:S(2)}, u32[]{:S(2)}) %collective-permute-start.3) | collective-permute-done | bytes 16928 | tf_op jit(solution)/shard_map/ppermute | solution.py:16
  152.9 1.0 fusion.100
  153.9 1.1 fusion.101
  155.0 1.1 fusion.8
  (101 shorter events, 13.1 us)
Async XLA Ops:
  15.0 49.3 %all-to-all-start = ((s32[128,1,28]{2,1,0:T(1,128)}), s32[128,1,28]{2,1,0:T(1,128)S(1)}, u32[]{:S(2)}, u32[]{:S(2)}) async-start(s32[128,1,28]{2,1,0:T(1,128)} %bitcast.2), calls=%async_computation | async-start | bytes 131072 | tf_op jit(solution)/shard_map/all_to_all | solution.py:92
  49.2 3.2 %copy-start.2 = (bf16[3,3,256,256]{3,2,1,0:T(8,128)(2,1)S(1)}, bf16[3,3,256,256]{3,2,1,0:T(8,128)(2,1)}, u32[]{:S(2)}) copy-start(bf16[3,3,256,256]{3,2,1,0:T(8,128)(2,1)} %param.14) | copy-start | bytes 3538948
  59.7 3.5 %copy-start.3 = (bf16[3,3,256,256]{3,2,1,0:T(8,128)(2,1)S(1)}, bf16[3,3,256,256]{3,2,1,0:T(8,128)(2,1)}, u32[]{:S(2)}) copy-start(bf16[3,3,256,256]{3,2,1,0:T(8,128)(2,1)} %param.15) | copy-start | bytes 3538948
  64.3 39.2 %all-to-all-start.1 = ((bf16[128,28,256]{2,1,0:T(8,128)(2,1)}), bf16[128,28,256]{2,1,0:T(8,128)(2,1)S(1)}, u32[]{:S(2)}, u32[]{:S(2)}) async-start(bf16[128,28,256]{2,1,0:T(8,128)(2,1)} %select_select_fusion), calls=%async_computation.1 | async-start | bytes 4194304 | tf_op jit(solution)/shard_map/all_to_all | solution.py:85
  123.0 4.1 %copy-start.4 = (bf16[2048,256]{1,0:T(8,128)(2,1)}, bf16[2048,256]{1,0:T(8,128)(2,1)S(1)}, u32[]{:S(2)}) copy-start(bf16[2048,256]{1,0:T(8,128)(2,1)S(1)} %fusion.3) | copy-start | bytes 3145732
  123.4 3.7 %copy-start.19 = (bf16[256,256]{1,0:T(8,128)(2,1)S(1)}, bf16[256,256]{1,0:T(8,128)(2,1)}, u32[]{:S(2)}) copy-start(bf16[256,256]{1,0:T(8,128)(2,1)} %get-tuple-element.18) | copy-start | bytes 393220
  123.4 3.7 %copy-start.20 = (bf16[256,256]{1,0:T(8,128)(2,1)S(1)}, bf16[256,256]{1,0:T(8,128)(2,1)}, u32[]{:S(2)}) copy-start(bf16[256,256]{1,0:T(8,128)(2,1)} %get-tuple-element.19) | copy-start | bytes 393220
  123.4 3.6 %copy-start.21 = (bf16[256,256]{1,0:T(8,128)(2,1)S(1)}, bf16[256,256]{1,0:T(8,128)(2,1)}, u32[]{:S(2)}) copy-start(bf16[256,256]{1,0:T(8,128)(2,1)} %get-tuple-element.20) | copy-start | bytes 393220
  123.4 6.2 %collective-permute-start = (bf16[1,32,256]{2,1,0:T(8,128)(2,1)S(1)}, bf16[1,32,256]{2,1,0:T(8,128)(2,1)S(1)}, u32[]{:S(2)}, u32[]{:S(2)}) collective-permute-start(bf16[1,32,256]{2,1,0:T(8,128)(2,1)S(1)} %slice_bitcast_fusion.24), channel_id=1, source_target_pairs={{0,16},{16,32},{32,48},{48,64},{64,80},{80,96},{96,112},{1,17},{17... | collective-permute-start | bytes 49160 | tf_op jit(solution)/shard_map/ppermute | solution.py:10
  127.0 3.3 %copy-start.17 = (bf16[256,256]{1,0:T(8,128)(2,1)S(1)}, bf16[256,256]{1,0:T(8,128)(2,1)}, u32[]{:S(2)}) copy-start(bf16[256,256]{1,0:T(8,128)(2,1)} %get-tuple-element.21) | copy-start | bytes 393220
  127.0 3.3 %copy-start.18 = (bf16[256,256]{1,0:T(8,128)(2,1)S(1)}, bf16[256,256]{1,0:T(8,128)(2,1)}, u32[]{:S(2)}) copy-start(bf16[256,256]{1,0:T(8,128)(2,1)} %get-tuple-element.22) | copy-start | bytes 393220
  130.2 7.3 %collective-permute-start.1 = (bf16[65,1,256]{2,0,1:T(8,128)(2,1)}, bf16[65,1,256]{2,0,1:T(8,128)(2,1)}, u32[]{:S(2)}, u32[]{:S(2)}) collective-permute-start(bf16[65,1,256]{2,0,1:T(8,128)(2,1)} %pad_maximum_fusion.1), channel_id=1, source_target_pairs={{0,1},{1,2},{2,3},{3,4},{4,5},{5,6},{6,7},{7,8},{8,9},{9,10},{10,1... | collective-permute-start | bytes 99848 | tf_op jit(solution)/shard_map/ppermute | solution.py:16
  130.2 1.9 %copy-start.5 = (bf16[32,1,16,512]{3,2,1,0:T(8,128)(2,1)S(1)}, bf16[32,1,16,512]{3,2,1,0:T(8,128)(2,1)}, u32[]{:S(2)}) copy-start(bf16[32,1,16,512]{3,2,1,0:T(8,128)(2,1)} %get-tuple-element.25) | copy-start | bytes 1572868
  130.2 1.9 %copy-start.14 = (bf16[256,256]{1,0:T(8,128)(2,1)S(1)}, bf16[256,256]{1,0:T(8,128)(2,1)}, u32[]{:S(2)}) copy-start(bf16[256,256]{1,0:T(8,128)(2,1)} %get-tuple-element.16) | copy-start | bytes 393220
  130.2 1.9 %copy-start.15 = (bf16[256,256]{1,0:T(8,128)(2,1)S(1)}, bf16[256,256]{1,0:T(8,128)(2,1)}, u32[]{:S(2)}) copy-start(bf16[256,256]{1,0:T(8,128)(2,1)} %get-tuple-element.17) | copy-start | bytes 393220
  132.7 13.4 %copy-start.11 = (bf16[256,256]{1,0:T(8,128)(2,1)S(1)}, bf16[256,256]{1,0:T(8,128)(2,1)}, u32[]{:S(2)}) copy-start(bf16[256,256]{1,0:T(8,128)(2,1)} %get-tuple-element.12) | copy-start | bytes 393220
  132.7 13.4 %copy-start.12 = (bf16[256,256]{1,0:T(8,128)(2,1)S(1)}, bf16[256,256]{1,0:T(8,128)(2,1)}, u32[]{:S(2)}) copy-start(bf16[256,256]{1,0:T(8,128)(2,1)} %get-tuple-element.13) | copy-start | bytes 393220
  132.7 13.4 %copy-start.13 = (bf16[256,256]{1,0:T(8,128)(2,1)S(1)}, bf16[256,256]{1,0:T(8,128)(2,1)}, u32[]{:S(2)}) copy-start(bf16[256,256]{1,0:T(8,128)(2,1)} %get-tuple-element.14) | copy-start | bytes 393220
  140.7 5.6 %copy-start.8 = (bf16[256,256]{1,0:T(8,128)(2,1)S(1)}, bf16[256,256]{1,0:T(8,128)(2,1)}, u32[]{:S(2)}) copy-start(bf16[256,256]{1,0:T(8,128)(2,1)} %get-tuple-element.9) | copy-start | bytes 393220
  140.7 5.6 %copy-start.9 = (bf16[256,256]{1,0:T(8,128)(2,1)S(1)}, bf16[256,256]{1,0:T(8,128)(2,1)}, u32[]{:S(2)}) copy-start(bf16[256,256]{1,0:T(8,128)(2,1)} %get-tuple-element.10) | copy-start | bytes 393220
  140.8 5.6 %copy-start.10 = (bf16[256,256]{1,0:T(8,128)(2,1)S(1)}, bf16[256,256]{1,0:T(8,128)(2,1)}, u32[]{:S(2)}) copy-start(bf16[256,256]{1,0:T(8,128)(2,1)} %get-tuple-element.11) | copy-start | bytes 393220
  141.0 5.0 %collective-permute-start.2 = (bf16[1,16,256]{2,0,1:T(2,128)(2,1)S(1)}, bf16[1,16,256]{2,0,1:T(2,128)(2,1)S(1)}, u32[]{:S(2)}, u32[]{:S(2)}) collective-permute-start(bf16[1,16,256]{2,0,1:T(2,128)(2,1)S(1)} %slice.196), channel_id=1, source_target_pairs={{0,16},{16,32},{32,48},{48,64},{64,80},{80,96},{96,112},{1,17},{17... | collective-permute-start | bytes 24584 | tf_op jit(solution)/shard_map/ppermute | solution.py:10
  145.9 6.9 %collective-permute-start.3 = (bf16[33,1,256]{2,0,1:T(8,128)(2,1)S(1)}, bf16[33,1,256]{2,0,1:T(8,128)(2,1)S(1)}, u32[]{:S(2)}, u32[]{:S(2)}) collective-permute-start(bf16[33,1,256]{2,0,1:T(8,128)(2,1)S(1)} %pad_maximum_fusion.2), channel_id=1, source_target_pairs={{0,1},{1,2},{2,3},{3,4},{4,5},{5,6},{6,7},{7,8},{8,9},{9,10},{10,1... | collective-permute-start | bytes 50696 | tf_op jit(solution)/shard_map/ppermute | solution.py:16
  146.4 10.3 %copy-start.1 = (s32[1024]{0:T(1024)S(1)}, s32[1024]{0:T(1024)}, u32[]{:S(2)}) copy-start(s32[1024]{0:T(1024)} %param.11) | copy-start | bytes 12292
  (4 other events, 5.0 us)
where the time goes:
time: 158 us; the launch traced here: 157 us
  matrix products  37.8 us (24%)
  local copies, waits for them, and re-layouts  36.7 us (23%)
  waiting for transfers between devices  29.4 us (19%)
  starting transfers between devices  27.2 us (17%)
  other arithmetic  24.3 us (15%)
    all_to_all x1, waiting for transfers between devices, body(): lax.all_to_all(packed.reshape(peer_count, capacity, row_width), ('lat', '...  18.1 us
    dot_general x1, matrix products, body(): numerator = jnp.dot(masked, obs_block, preferred_element_type=jnp.float32)  18 us
    gather x2, local copies, waits for them, and re-layouts, body(): jnp.take(payload, source_rows, axis=0)  13.4 us
    gather x2, local copies, waits for them, and re-layouts, body(): jnp.take(slot_offsets, source_rows, axis=0)  13 us
    dot_general x1, matrix products, body(): jnp.dot(radiances, project_weight, preferred_element_type=jnp.float32)  12 us
    all_to_all x1, starting transfers between devices, body(): lax.all_to_all(offsets_out.reshape(peer_count, capacity), ('lat', 'lon'),...  11.2 us
    ppermute x2, waiting for transfers between devices, passed_along(): return lax.ppermute(value, axis, pairs)  9.99 us
    select_n x1, other arithmetic, body(): jnp.where(live_mask[None, :], weights_flat, jnp.zeros((), jnp.bfloat16))  9.95 us
  transfers between devices with their start and end apart: 6, of which 4 were waited for; matrix products, arithmetic and copies ran while one was open for 36% of the time, Pallas kernels for 0%

commit v1 on v0

--- a/solution.py
+++ b/solution.py
@@ -16,12 +16,24 @@
     return lax.ppermute(value, axis, pairs)
 
 
+def diagonal(value):
+    lat_size = lax.axis_size("lat")
+    lon_size = lax.axis_size("lon")
+    pairs = [
+        (l * lon_size + n, (l + 1) * lon_size + (n + 1) % lon_size)
+        for l in range(lat_size - 1)
+        for n in range(lon_size)
+    ]
+    return lax.ppermute(value, ("lat", "lon"), pairs)
+
+
 def stride_conv(field, kernel):
     height, breadth, depth = field.shape
     half_rows, half_cols = (height // 2, breadth // 2)
     upper_rim = shifted_2(field[-1:], "lat", 1)
-    west_column = jnp.concatenate([upper_rim[:, -1:], field[:, -1:]], axis=0)
-    west_rim = passed_along(west_column, "lon", 1)[:, 0]
+    west_col = passed_along(field[:, -1:], "lon", 1)
+    corner = diagonal(field[-1:, -1:])
+    west_rim = jnp.concatenate([corner, west_col], axis=0)[:, 0]
     paired = field.reshape(half_rows, 2, half_cols, 2 * depth)
     even_rows = paired[:, 0]
     odd_rows = paired[:, 1]
@@ -63,53 +75,62 @@
     peer_count = lat_size * lon_size
     obs_count = radiances.shape[0]
     capacity = 7 * (obs_count // peer_count) // 2
+    chunk_rows = ((capacity + 1 + 15) // 16) * 16
     slot_count = setconv_weights.shape[2]
     channel_count = project_weight.shape[1]
+    digit = 64
     targets = jnp.arange(peer_count, dtype=jnp.int32)
     row_index = jnp.arange(obs_count, dtype=jnp.int32)
     matches = tile_ids[:, None] == targets[None, :]
     run_counts = jnp.sum(matches.astype(jnp.int32), axis=0)
     run_starts = jnp.min(jnp.where(matches, row_index[:, None], obs_count), axis=0)
     within = jnp.arange(capacity, dtype=jnp.int32)
-    source_rows = jnp.minimum(run_starts[:, None] + within[None, :], obs_count - 1).reshape(-1)
+    source_rows = (run_starts[:, None] + within[None, :]).reshape(-1)
     valid_slot = (within[None, :] < run_counts[:, None]).reshape(-1)
+    selector = (
+        (source_rows[:, None] == row_index[None, :]) & valid_slot[:, None]
+    ).astype(jnp.bfloat16)
     payload = jnp.dot(radiances, project_weight, preferred_element_type=jnp.float32).astype(
         jnp.bfloat16
     )
-    row_width = payload.shape[1]
-    packed = jnp.where(
-        valid_slot[:, None], jnp.take(payload, source_rows, axis=0), jnp.zeros((), jnp.bfloat16)
+    packed = jnp.dot(selector, payload, preferred_element_type=jnp.float32).astype(jnp.bfloat16)
+    key = slot_offsets + 1
+    digits = jnp.stack([key // digit, key % digit], axis=1).astype(jnp.bfloat16)
+    packed_digits = jnp.dot(selector, digits, preferred_element_type=jnp.float32)
+    packed_digits = packed_digits.reshape(peer_count, capacity, 2)
+    digit_row = jnp.concatenate(
+        [
+            packed_digits[:, :, 0],
+            packed_digits[:, :, 1],
+            jnp.zeros((peer_count, channel_count - 2 * capacity), jnp.float32),
+        ],
+        axis=1,
+    ).astype(jnp.bfloat16)
+    outgoing = jnp.concatenate(
+        [
+            packed.reshape(peer_count, capacity, channel_count),
+            digit_row[:, None, :],
+            jnp.zeros((peer_count, chunk_rows - capacity - 1, channel_count), jnp.bfloat16),
+        ],
+        axis=1,
     )
-    offsets_out = jnp.where(valid_slot, jnp.take(slot_offsets, source_rows, axis=0), slot_count)
-    arrived, arrived_offsets = (
-        lax.all_to_all(
-            packed.reshape(peer_count, capacity, row_width),
-            ("lat", "lon"),
-            split_axis=0,
-            concat_axis=0,
-            tiled=True,
-        ),
-        lax.all_to_all(
-            offsets_out.reshape(peer_count, capacity),
-            ("lat", "lon"),
-            split_axis=0,
-            concat_axis=0,
-            tiled=True,
-        ),
-    )
-    arrived = arrived.reshape(-1, row_width)
-    arrived_offsets = arrived_offsets.reshape(-1)
+    arrived = lax.all_to_all(outgoing, ("lat", "lon"), split_axis=0, concat_axis=0, tiled=True)
+    arrived_rows = arrived[:, :capacity].reshape(-1, channel_count)
+    arrived_digits = arrived[:, capacity].astype(jnp.int32)
+    arrived_key = arrived_digits[:, :capacity] * digit + arrived_digits[:, capacity : 2 * capacity]
+    arrived_offsets = arrived_key.reshape(-1) - 1
     slot_table = (
         jnp.arange(slot_count, dtype=jnp.int32)[:, None] == arrived_offsets[None, :]
     ).astype(jnp.bfloat16)
-    obs_block = jnp.dot(slot_table, arrived, preferred_element_type=jnp.float32).astype(
+    obs_block = jnp.dot(slot_table, arrived_rows, preferred_element_type=jnp.float32).astype(
         jnp.bfloat16
     )
     tile_rows, tile_cols = (setconv_weights.shape[0], setconv_weights.shape[1])
     weights_flat = setconv_weights.reshape(-1, slot_count)
     live_mask = jnp.arange(slot_count, dtype=jnp.int32) < tile_counts.reshape(-1)[0]
+    obs_masked = jnp.where(live_mask[:, None], obs_block, jnp.zeros((), jnp.bfloat16))
+    numerator = jnp.dot(weights_flat, obs_masked, preferred_element_type=jnp.float32)
     masked = jnp.where(live_mask[None, :], weights_flat, jnp.zeros((), jnp.bfloat16))
-    numerator = jnp.dot(masked, obs_block, preferred_element_type=jnp.float32)
     density = jnp.sum(masked, axis=1, dtype=jnp.float32)
     grid = (
         (numerator / jnp.sqrt(density)[:, None])

time: 158 us -> 123 us (0.78)
  local copies, waits for them, and re-layouts: 36.7 us -> 14.1 us
  other arithmetic: 24.3 us -> 14 us
  waiting for transfers between devices: 29.4 us -> 20.2 us
  matrix products: 37.8 us -> 44.9 us
    gather x4 -> x0, local copies, waits for them, and re-layouts: 26.4 us -> none  [the longest x2 13.4 us: body(): jnp.take(payload, source_rows, axis=0)]
    select_n x4 -> x0, other arithmetic: 14.2 us -> none  [the longest x1 9.95 us: body(): jnp.where(live_mask[None, :], weights_flat, jnp.zeros((), jnp.bfloat16))]
    ppermute x2, waiting for transfers between devices: 9.99 us -> 0.01 us  [passed_along(): return lax.ppermute(value, axis, pairs)]
    all_to_all x2 -> x1, starting transfers between devices: 20.9 us -> 11.3 us  [body(): lax.all_to_all(outgoing, ('lat', 'lon'), split_axis=0, concat_axis=0, til...]
    dot_general x1 -> x3, matrix products: 18 us -> 26.4 us  [the longest x1 17.4 us: body(): jnp.dot(weights_flat, obs_masked, preferred_element_type=jnp.float32)]
    ppermute x0 -> x2, starting transfers between devices: none -> 7.97 us  [diagonal(): return lax.ppermute(value, ('lat', 'lon'), pairs)]
    concatenate x2, other arithmetic: 0.64 us -> 3.24 us  [the longest x1 2.31 us: body(): jnp.concatenate([packed.reshape(peer_count, capacity, channel_count), dig...]
    reshape x1 -> x2, local copies, waits for them, and re-layouts: 1.4 us -> 3.83 us  [the longest x1 2.39 us: body(): packed.reshape(peer_count, capacity, channel_count)]
  transfers between devices with their start and end apart: 6 -> 7, of which waited for: 4 -> 2; matrix products, arithmetic and copies ran while one was open for 36% -> 15% of each run, Pallas kernels for 0% -> 0%
where the time goes in v1:
time: 123 us; the launch traced here: 122 us
  matrix products  44.9 us (37%)
  starting transfers between devices  27.2 us (22%)
  waiting for transfers between devices  20.2 us (16%)
  local copies, waits for them, and re-layouts  14.1 us (11%)
  other arithmetic  14 us (11%)
  between operations  1.27 us (1%)
    all_to_all x1, waiting for transfers between devices, body(): lax.all_to_all(outgoing, ('lat', 'lon'), split_axis=0, concat_axis=0, til...  18.8 us
    dot_general x1, matrix products, body(): jnp.dot(weights_flat, obs_masked, preferred_element_type=jnp.float32)  17.4 us
    dot_general x1, matrix products, body(): jnp.dot(radiances, project_weight, preferred_element_type=jnp.float32)  12 us
    all_to_all x1, starting transfers between devices, body(): lax.all_to_all(outgoing, ('lat', 'lon'), split_axis=0, concat_axis=0, til...  11.3 us
    ppermute x2, starting transfers between devices, diagonal(): return lax.ppermute(value, ('lat', 'lon'), pairs)  7.97 us
    ppermute x2, starting transfers between devices, shifted_2(): return lax.ppermute(value, axis, pairs)  7.74 us
    reduce_sum x1, other arithmetic, body(): density = jnp.sum(masked, axis=1, dtype=jnp.float32)  6.38 us
    dot_general x1, matrix products, body(): jnp.dot(selector, payload, preferred_element_type=jnp.float32)  5.22 us
  transfers between devices with their start and end apart: 7, of which 2 were waited for; matrix products, arithmetic and copies ran while one was open for 15% of the time, Pallas kernels for 0%

profile of v1, /device:TPU:0, one launch (start us, length us, event | category | flops | bytes accessed | tf_op | source)
XLA Modules:
  0.0 121.7 jit_solution(724885027921698754)
XLA Ops:
  2.0 3.8 %fusion.14 = bf16[3584,2]{0,1:T(2,128)(2,1)S(1)} fusion(s32[3584]{0:T(1024)S(1)} %add.98, pred[3584]{0:T(1024)(128)(4,1)S(1)} %lt.42, bf16[1024,1]{0,1:T(2,128)(2,1)S(1)} %stack.13, bf16[1024,1]{0,1:T(2,128)(2,1)S(1)} %stack.12), kind=kOutput, calls=%fused_computation.13 | convolution fusion | flops 22035456 | bytes 36352 | tf_op jit(solution)/shard_map/dot_general | solution.py:99
  6.1 12.0 %convolution_convert_fusion = bf16[1024,256]{1,0:T(8,128)(2,1)S(1)} fusion(bf16[1024,8461]{0,1:T(8,128)(2,1)} %param.8, bf16[8461,256]{1,0:T(8,128)(2,1)} %param.9), kind=kOutput, calls=%fused_computation.22 | convolution fusion | flops 4436262912 | bytes 22184448 | tf_op jit(solution)/shard_map/dot_general | solution.py:93
  18.1 5.2 %fusion.11 = bf16[3584,256]{1,0:T(8,128)(2,1)} fusion(bf16[1024,256]{1,0:T(8,128)(2,1)S(1)} %convolution_convert_fusion, s32[3584]{0:T(1024)S(1)} %add.98, pred[3584]{0:T(1024)(128)(4,1)S(1)} %lt.42), kind=kOutput, calls=%fused_computation.12 | convolution fusion | flops 1887305728 | bytes 2377216 | tf_op jit(solution)/shard_map/dot_general | solution.py:96
  23.3 2.4 %reshape.141 = bf16[128,28,256]{2,1,0:T(8,128)(2,1)S(1)} reshape(bf16[3584,256]{1,0:T(8,128)(2,1)} %fusion.11) | data formatting | bytes 3670016 | tf_op jit(solution)/shard_map/reshape | solution.py:111
  25.9 2.3 %maximum_maximum_fusion = bf16[128,32,256]{2,1,0:T(8,128)(2,1)} fusion(bf16[128,1,28]{2,1,0:T(2,128)(2,1)S(1)} %copy.34, bf16[128,1,28]{2,1,0:T(2,128)(2,1)S(1)} %copy.33, bf16[128,28,256]{2,1,0:T(8,128)(2,1)S(1)} %reshape.141, bf16[32]{0:T(256)(128)(2,1)S(1)} %pad.40.clone, bf16[32,256]{1,0:T(8,128)(2,1)S(1)} %pad.39.clone), kind=kLoop, calls=%fused_computation.19 | loop fusion | flops 10485760 | bytes 3962944 | tf_op jit(solution)/shard_map/concatenate | solution.py:109
  28.2 11.3 %all-to-all-start = ((bf16[128,32,256]{2,1,0:T(8,128)(2,1)}), bf16[128,32,256]{2,1,0:T(8,128)(2,1)S(1)}, u32[]{:S(2)}, u32[]{:S(2)}) async-start(bf16[128,32,256]{2,1,0:T(8,128)(2,1)} %maximum_maximum_fusion), calls=%async_computation | async-start | bytes 4194304 | tf_op jit(solution)/shard_map/all_to_all | solution.py:117
  40.3 6.4 %convert_reduce_fusion = f32[64,32]{1,0:T(8,128)S(1)} fusion(bf16[64,32,2560]{2,1,0:T(8,128)(2,1)} %param.13, pred[2560]{0:T(1024)(128)(4,1)S(1)} %iota_compare_fusion.12), kind=kLoop, calls=%fused_computation.2 | loop fusion | flops 15726592 | bytes 10496512 | tf_op jit(solution)/shard_map/reduce_sum | solution.py:134
  46.7 1.1 slice_bitcast_fusion.15
  47.8 2.3 %slice_bitcast_fusion.6 = (bf16[256,256]{1,0:T(8,128)(2,1)S(1)}, bf16[256,256]{1,0:T(8,128)(2,1)S(1)}, bf16[256,256]{1,0:T(8,128)(2,1)}, bf16[256,256]{1,0:T(8,1...) fusion(bf16[3,3,256,256]{3,2,1,0:T(8,128)(2,1)} %param.15), kind=kLoop, calls=%fused_computation.109 | loop fusion | bytes 2359296 | tf_op jit(solution)/shard_map/squeeze | solution.py:48
  50.1 18.8 %all-to-all-done = bf16[128,32,256]{2,1,0:T(8,128)(2,1)S(1)} async-done(((bf16[128,32,256]{2,1,0:T(8,128)(2,1)}), bf16[128,32,256]{2,1,0:T(8,128)(2,1)S(1)}, u32[]{:S(2)}, u32[]{:S(2)}) %all-to-all-start) | async-done | bytes 2097184 | tf_op jit(solution)/shard_map/all_to_all | solution.py:117
  68.9 1.4 %reshape.143 = bf16[3584,256]{1,0:T(8,128)(2,1)} reshape(bf16[128,28,256]{2,1,0:T(8,128)(2,1)S(1)} %bitcast.103) | data formatting | bytes 3670016 | tf_op jit(solution)/shard_map/reshape | solution.py:118
  70.7 17.4 %fusion.20 = bf16[2048,256]{0,1:T(8,128)(2,1)S(1)} fusion(bf16[2048,2560]{1,0:T(8,128)(2,1)} %bitcast.102, bf16[3584,256]{1,0:T(8,128)(2,1)} %reshape.143, s32[3584]{0:T(1024)S(1)} %sub.14, pred[2560]{0:T(1024)(128)(4,1)S(1)} %iota_compare_fusion.12, f32[2048]{0:T(1024)S(1)} %sqrt.11), kind=kOutput, calls=%fused_computation.18 | convolution fusion | flops 7393509376 | bytes 13394432 | tf_op jit(solution)/shard_map/dot_general | solution.py:132
  89.7 3.2 %collective-permute-start = (bf16[1,32,256]{1,2,0:T(8,128)(2,1)}, bf16[1,32,256]{1,2,0:T(8,128)(2,1)}, u32[]{:S(2)}, u32[]{:S(2)}) collective-permute-start(bf16[1,32,256]{1,2,0:T(8,128)(2,1)} %slice_bitcast_fusion.24), channel_id=1, source_target_pairs={{0,16},{16,32},{32,48},{48,64},{64,80},{80,96},{96,112},{1,17},{17... | collective-permute-start | bytes 49160 | tf_op jit(solution)/shard_map/ppermute | solution.py:10
  93.0 1.1 fusion.122
  95.7 4.0 %collective-permute-start.1 = (bf16[1,1,256]{2,1,0:T(2,128)(2,1)S(1)}, bf16[1,1,256]{2,1,0:T(2,128)(2,1)S(1)}, u32[]{:S(2)}, u32[]{:S(2)}) collective-permute-start(bf16[1,1,256]{2,1,0:T(2,128)(2,1)S(1)} %slice.221), channel_id=1, source_target_pairs={{0,17},{1,18},{2,19},{3,20},{4,21},{5,22},{6,23},{7,24},{8,25},{9,... | collective-permute-start | bytes 1544 | tf_op jit(solution)/shard_map/ppermute | solution.py:27
  100.7 1.2 pad_maximum_fusion
  101.8 1.5 %fusion.40 = f32[512,512]{1,0:T(8,128)S(1)} fusion(bf16[512,512]{1,0:T(8,128)(2,1)S(1)} %bitcast.108, bf16[256,256]{1,0:T(8,128)(2,1)} %get-tuple-element.23, bf16[256,256]{1,0:T(8,128)(2,1)} %get-tuple-element.21, bf16[256,256]{1,0:T(8,128)(2,1)} %get-tuple-element.22), kind=kOutput, calls=%fused_computation.50 | convolution fusion | flops 270532608 | bytes 1966080 | tf_op jit(solution)/shard_map/dot_general | solution.py:51
  104.7 0.9 pad_maximum_fusion.1
  106.9 4.0 %collective-permute-start.4 = (bf16[1,1,256]{2,0,1:T(2,128)(2,1)S(1)}, bf16[1,1,256]{2,0,1:T(2,128)(2,1)S(1)}, u32[]{:S(2)}, u32[]{:S(2)}) collective-permute-start(bf16[1,1,256]{2,0,1:T(2,128)(2,1)S(1)} %slice.229), channel_id=1, source_target_pairs={{0,17},{1,18},{2,19},{3,20},{4,21},{5,22},{6,23},{7,24},{8,25},{9,... | collective-permute-start | bytes 1544 | tf_op jit(solution)/shard_map/ppermute | solution.py:27
  111.0 4.5 %collective-permute-start.3 = (bf16[1,16,256]{2,0,1:T(2,128)(2,1)S(1)}, bf16[1,16,256]{2,0,1:T(2,128)(2,1)S(1)}, u32[]{:S(2)}, u32[]{:S(2)}) collective-permute-start(bf16[1,16,256]{2,0,1:T(2,128)(2,1)S(1)} %slice.224), channel_id=1, source_target_pairs={{0,16},{16,32},{32,48},{48,64},{64,80},{80,96},{96,112},{1,17},{17... | collective-permute-start | bytes 24584 | tf_op jit(solution)/shard_map/ppermute | solution.py:10
  115.5 1.4 %collective-permute-done.3 = bf16[1,16,256]{2,0,1:T(2,128)(2,1)S(1)} collective-permute-done((bf16[1,16,256]{2,0,1:T(2,128)(2,1)S(1)}, bf16[1,16,256]{2,0,1:T(2,128)(2,1)S(1)}, u32[]{:S(2)}, u32[]{:S(2)}) %collective-permute-start.3) | collective-permute-done | bytes 8224 | tf_op jit(solution)/shard_map/ppermute | solution.py:10
  117.9 1.0 fusion.121
  118.9 1.1 convolution_add_fusion.7
  120.0 1.1 fusion.23
  (101 shorter events, 11.2 us)
Async XLA Ops:
  28.2 40.6 %all-to-all-start = ((bf16[128,32,256]{2,1,0:T(8,128)(2,1)}), bf16[128,32,256]{2,1,0:T(8,128)(2,1)S(1)}, u32[]{:S(2)}, u32[]{:S(2)}) async-start(bf16[128,32,256]{2,1,0:T(8,128)(2,1)} %maximum_maximum_fusion), calls=%async_computation | async-start | bytes 4194304 | tf_op jit(solution)/shard_map/all_to_all | solution.py:117
  40.2 6.5 %copy-start = (bf16[3,3,256,256]{3,2,1,0:T(8,128)(2,1)S(1)}, bf16[3,3,256,256]{3,2,1,0:T(8,128)(2,1)}, u32[]{:S(2)}) copy-start(bf16[3,3,256,256]{3,2,1,0:T(8,128)(2,1)} %param.14) | copy-start | bytes 3538948
  89.7 9.9 %collective-permute-start = (bf16[1,32,256]{1,2,0:T(8,128)(2,1)}, bf16[1,32,256]{1,2,0:T(8,128)(2,1)}, u32[]{:S(2)}, u32[]{:S(2)}) collective-permute-start(bf16[1,32,256]{1,2,0:T(8,128)(2,1)} %slice_bitcast_fusion.24), channel_id=1, source_target_pairs={{0,16},{16,32},{32,48},{48,64},{64,80},{80,96},{96,112},{1,17},{17... | collective-permute-start | bytes 49160 | tf_op jit(solution)/shard_map/ppermute | solution.py:10
  94.9 8.4 %copy-start.2 = (bf16[32,1,16,512]{3,2,1,0:T(8,128)(2,1)S(1)}, bf16[32,1,16,512]{3,2,1,0:T(8,128)(2,1)}, u32[]{:S(2)}) copy-start(bf16[32,1,16,512]{3,2,1,0:T(8,128)(2,1)} %get-tuple-element.26) | copy-start | bytes 1572868
  94.9 8.4 %copy-start.13 = (bf16[256,256]{1,0:T(8,128)(2,1)S(1)}, bf16[256,256]{1,0:T(8,128)(2,1)}, u32[]{:S(2)}) copy-start(bf16[256,256]{1,0:T(8,128)(2,1)} %get-tuple-element.18) | copy-start | bytes 393220
  95.6 7.7 %copy-start.14 = (bf16[256,256]{1,0:T(8,128)(2,1)S(1)}, bf16[256,256]{1,0:T(8,128)(2,1)}, u32[]{:S(2)}) copy-start(bf16[256,256]{1,0:T(8,128)(2,1)} %get-tuple-element.19) | copy-start | bytes 393220
  95.6 7.7 %copy-start.15 = (bf16[256,256]{1,0:T(8,128)(2,1)S(1)}, bf16[256,256]{1,0:T(8,128)(2,1)}, u32[]{:S(2)}) copy-start(bf16[256,256]{1,0:T(8,128)(2,1)} %get-tuple-element.20) | copy-start | bytes 393220
  95.6 9.1 %collective-permute-start.2 = (bf16[64,1,256]{2,1,0:T(2,128)(2,1)}, bf16[64,1,256]{2,1,0:T(2,128)(2,1)}, u32[]{:S(2)}, u32[]{:S(2)}) collective-permute-start(bf16[64,1,256]{2,1,0:T(2,128)(2,1)} %slice.222), channel_id=1, source_target_pairs={{0,1},{1,2},{2,3},{3,4},{4,5},{5,6},{6,7},{7,8},{8,9},{9,10},{10,1... | collective-permute-start | bytes 98312 | tf_op jit(solution)/shard_map/ppermute | solution.py:16
  95.7 9.0 %collective-permute-start.1 = (bf16[1,1,256]{2,1,0:T(2,128)(2,1)S(1)}, bf16[1,1,256]{2,1,0:T(2,128)(2,1)S(1)}, u32[]{:S(2)}, u32[]{:S(2)}) collective-permute-start(bf16[1,1,256]{2,1,0:T(2,128)(2,1)S(1)} %slice.221), channel_id=1, source_target_pairs={{0,17},{1,18},{2,19},{3,20},{4,21},{5,22},{6,23},{7,24},{8,25},{9,... | collective-permute-start | bytes 1544 | tf_op jit(solution)/shard_map/ppermute | solution.py:27
  100.6 3.1 %copy-start.1 = (bf16[32,1,16,512]{3,2,1,0:T(8,128)(2,1)S(1)}, bf16[32,1,16,512]{3,2,1,0:T(8,128)(2,1)}, u32[]{:S(2)}) copy-start(bf16[32,1,16,512]{3,2,1,0:T(8,128)(2,1)} %get-tuple-element.25) | copy-start | bytes 1572868
  100.6 3.1 %copy-start.10 = (bf16[256,256]{1,0:T(8,128)(2,1)S(1)}, bf16[256,256]{1,0:T(8,128)(2,1)}, u32[]{:S(2)}) copy-start(bf16[256,256]{1,0:T(8,128)(2,1)} %get-tuple-element.16) | copy-start | bytes 393220
  100.6 3.1 %copy-start.11 = (bf16[256,256]{1,0:T(8,128)(2,1)S(1)}, bf16[256,256]{1,0:T(8,128)(2,1)}, u32[]{:S(2)}) copy-start(bf16[256,256]{1,0:T(8,128)(2,1)} %get-tuple-element.17) | copy-start | bytes 393220
  100.7 3.1 %copy-start.12 = (bf16[256,256]{1,0:T(8,128)(2,1)S(1)}, bf16[256,256]{1,0:T(8,128)(2,1)}, u32[]{:S(2)}) copy-start(bf16[256,256]{1,0:T(8,128)(2,1)} %get-tuple-element.24) | copy-start | bytes 393220
  104.2 12.8 %copy-start.7 = (bf16[256,256]{1,0:T(8,128)(2,1)S(1)}, bf16[256,256]{1,0:T(8,128)(2,1)}, u32[]{:S(2)}) copy-start(bf16[256,256]{1,0:T(8,128)(2,1)} %get-tuple-element.12) | copy-start | bytes 393220
  104.2 12.8 %copy-start.8 = (bf16[256,256]{1,0:T(8,128)(2,1)S(1)}, bf16[256,256]{1,0:T(8,128)(2,1)}, u32[]{:S(2)}) copy-start(bf16[256,256]{1,0:T(8,128)(2,1)} %get-tuple-element.13) | copy-start | bytes 393220
  104.2 12.8 %copy-start.9 = (bf16[256,256]{1,0:T(8,128)(2,1)S(1)}, bf16[256,256]{1,0:T(8,128)(2,1)}, u32[]{:S(2)}) copy-start(bf16[256,256]{1,0:T(8,128)(2,1)} %get-tuple-element.14) | copy-start | bytes 393220
  104.4 12.9 %copy-start.4 = (bf16[256,256]{1,0:T(8,128)(2,1)S(1)}, bf16[256,256]{1,0:T(8,128)(2,1)}, u32[]{:S(2)}) copy-start(bf16[256,256]{1,0:T(8,128)(2,1)} %get-tuple-element.9) | copy-start | bytes 393220
  104.4 12.9 %copy-start.5 = (bf16[256,256]{1,0:T(8,128)(2,1)S(1)}, bf16[256,256]{1,0:T(8,128)(2,1)}, u32[]{:S(2)}) copy-start(bf16[256,256]{1,0:T(8,128)(2,1)} %get-tuple-element.10) | copy-start | bytes 393220
  104.4 12.9 %copy-start.6 = (bf16[256,256]{1,0:T(8,128)(2,1)S(1)}, bf16[256,256]{1,0:T(8,128)(2,1)}, u32[]{:S(2)}) copy-start(bf16[256,256]{1,0:T(8,128)(2,1)} %get-tuple-element.11) | copy-start | bytes 393220
  106.2 11.3 %copy-start.3 = (bf16[256,256]{1,0:T(8,128)(2,1)S(1)}, bf16[256,256]{1,0:T(8,128)(2,1)}, u32[]{:S(2)}) copy-start(bf16[256,256]{1,0:T(8,128)(2,1)} %get-tuple-element.15) | copy-start | bytes 393220
  106.8 11.0 %collective-permute-start.5 = (bf16[32,1,256]{2,0,1:T(8,128)(2,1)S(1)}, bf16[32,1,256]{2,0,1:T(8,128)(2,1)S(1)}, u32[]{:S(2)}, u32[]{:S(2)}) collective-permute-start(bf16[32,1,256]{2,0,1:T(8,128)(2,1)S(1)} %slice.230), channel_id=1, source_target_pairs={{0,1},{1,2},{2,3},{3,4},{4,5},{5,6},{6,7},{7,8},{8,9},{9,10},{10,1... | collective-permute-start | bytes 49160 | tf_op jit(solution)/shard_map/ppermute | solution.py:16
  106.9 10.9 %collective-permute-start.4 = (bf16[1,1,256]{2,0,1:T(2,128)(2,1)S(1)}, bf16[1,1,256]{2,0,1:T(2,128)(2,1)S(1)}, u32[]{:S(2)}, u32[]{:S(2)}) collective-permute-start(bf16[1,1,256]{2,0,1:T(2,128)(2,1)S(1)} %slice.229), channel_id=1, source_target_pairs={{0,17},{1,18},{2,19},{3,20},{4,21},{5,22},{6,23},{7,24},{8,25},{9,... | collective-permute-start | bytes 1544 | tf_op jit(solution)/shard_map/ppermute | solution.py:27
  111.0 6.0 %collective-permute-start.3 = (bf16[1,16,256]{2,0,1:T(2,128)(2,1)S(1)}, bf16[1,16,256]{2,0,1:T(2,128)(2,1)S(1)}, u32[]{:S(2)}, u32[]{:S(2)}) collective-permute-start(bf16[1,16,256]{2,0,1:T(2,128)(2,1)S(1)} %slice.224), channel_id=1, source_target_pairs={{0,16},{16,32},{32,48},{48,64},{64,80},{80,96},{96,112},{1,17},{17... | collective-permute-start | bytes 24584 | tf_op jit(solution)/shard_map/ppermute | solution.py:10

commit v2 on v1

v2 whole, which is shorter than its diff:
```python
import jax
import jax.numpy as jnp
from jax import lax
from jax.sharding import PartitionSpec as P


def cyclic(value, axes, shifts):
    sizes = [lax.axis_size(a) for a in axes]
    pairs = []
    for l in range(sizes[0]):
        for n in range(sizes[-1] if len(axes) > 1 else 1):
            if len(axes) == 1:
                pairs.append((l, (l + shifts[0]) % sizes[0]))
            else:
                src = l * sizes[1] + n
                dst = ((l + shifts[0]) % sizes[0]) * sizes[1] + (n + shifts[1]) % sizes[1]
                pairs.append((src, dst))
    return lax.ppermute(value, axes if len(axes) > 1 else axes[0], pairs)


def strided_valid(field, kernel):
    height, breadth, depth = field.shape
    out_rows, out_cols = ((height - 3) // 2 + 1, (breadth - 3) // 2 + 1)
    summed = jnp.zeros((out_rows * out_cols, kernel.shape[3]), jnp.float32)
    for row_tap in range(3):
        for col_tap in range(3):
            window = lax.slice(
                field,
                (row_tap, col_tap, 0),
                (row_tap + 2 * out_rows - 1, col_tap + 2 * out_cols - 1, depth),
                (2, 2, 1),
            )
            summed = summed + jnp.dot(
                window.reshape(-1, depth),
                kernel[row_tap, col_tap],
                preferred_element_type=jnp.float32,
            )
    return summed.reshape(out_rows, out_cols, kernel.shape[3])


def encode_tile(grid, conv1_weight, conv2_weight):
    rim = 3
    north = cyclic(grid[-rim:], ("lat",), (1,))
    west = cyclic(grid[:, -rim:], ("lon",), (1,))
    north_west = cyclic(grid[-rim:, -rim:], ("lat", "lon"), (1, 1))
    top = jnp.concatenate([north_west, north], axis=1)
    top = jnp.where(lax.axis_index("lat") == 0, jnp.zeros((), top.dtype), top)
    body_rows = jnp.concatenate([west, grid], axis=1)
    extended = jnp.concatenate([top, body_rows], axis=0)
    hidden = jax.nn.gelu(strided_valid(extended, conv1_weight)).astype(jnp.bfloat16)
    return strided_valid(hidden, conv2_weight).astype(jnp.bfloat16)


def body(
    radiances,
    project_weight,
    tile_ids,
    slot_offsets,
    tile_counts,
    setconv_weights,
    conv1_weight,
    conv2_weight,
):
    lat_size = lax.axis_size("lat")
    lon_size = lax.axis_size("lon")
    peer_count = lat_size * lon_size
    obs_count = radiances.shape[0]
    capacity = 7 * (obs_count // peer_count) // 2
    chunk_rows = ((capacity + 1 + 15) // 16) * 16
    slot_count = setconv_weights.shape[2]
    channel_count = project_weight.shape[1]
    digit = 64
    targets = jnp.arange(peer_count, dtype=jnp.int32)
    row_index = jnp.arange(obs_count, dtype=jnp.int32)
    matches = tile_ids[:, None] == targets[None, :]
    run_counts = jnp.sum(matches.astype(jnp.int32), axis=0)
    run_starts = jnp.min(jnp.where(matches, row_index[:, None], obs_count), axis=0)
    within = jnp.arange(chunk_rows, dtype=jnp.int32)
    source_rows = (run_starts[:, None] + within[None, :]).reshape(-1)
    valid_slot = (
        (within[None, :] < run_counts[:, None]) & (within[None, :] < capacity)
    ).reshape(-1)
    selector = (
        (source_rows[:, None] == row_index[None, :]) & valid_slot[:, None]
    ).astype(jnp.bfloat16)
    payload = jnp.dot(radiances, project_weight, preferred_element_type=jnp.float32).astype(
        jnp.bfloat16
    )
    packed = jnp.dot(selector, payload, preferred_element_type=jnp.float32).astype(jnp.bfloat16)
    packed = packed.reshape(peer_count, chunk_rows, channel_count)
    key = jnp.concatenate([slot_offsets + 1, jnp.zeros((capacity,), jnp.int32)])
    hi_cols = jnp.stack([key[c : c + obs_count] // digit for c in range(capacity)], axis=1)
    lo_cols = jnp.stack([key[c : c + obs_count] % digit for c in range(capacity)], axis=1)
    windows = jnp.concatenate(
        [hi_cols, lo_cols, jnp.zeros((obs_count, channel_count - 2 * capacity), jnp.int32)],
        axis=1,
    ).astype(jnp.bfloat16)
    run_head = (run_starts[:, None] == row_index[None, :]).astype(jnp.bfloat16)
    digit_row = jnp.dot(run_head, windows, preferred_element_type=jnp.float32)
    column = jnp.arange(channel_count, dtype=jnp.int32)
    digit_live = (column[None, :] % capacity < run_counts[:, None]) & (
        column[None, :] < 2 * capacity
    )
    digit_row = jnp.where(digit_live, digit_row, 0.0).astype(jnp.bfloat16)
    outgoing = packed.at[:, capacity, :].set(digit_row)
    arrived = lax.all_to_all(outgoing, ("lat", "lon"), split_axis=0, concat_axis=0, tiled=True)
    arrived_rows = arrived[:, :capacity].reshape(-1, channel_count)
    arrived_digits = arrived[:, capacity].astype(jnp.int32)
    arrived_key = arrived_digits[:, :capacity] * digit + arrived_digits[:, capacity : 2 * capacity]
    arrived_offsets = arrived_key.reshape(-1) - 1
    slot_table = (
        jnp.arange(slot_count, dtype=jnp.int32)[:, None] == arrived_offsets[None, :]
    ).astype(jnp.bfloat16)
    obs_block = jnp.dot(slot_table, arrived_rows, preferred_element_type=jnp.float32).astype(
        jnp.bfloat16
    )
    tile_rows, tile_cols = (setconv_weights.shape[0], setconv_weights.shape[1])
    weights_flat = setconv_weights.reshape(-1, slot_count)
    live_mask = jnp.arange(slot_count, dtype=jnp.int32) < tile_counts.reshape(-1)[0]
    obs_masked = jnp.where(live_mask[:, None], obs_block, jnp.zeros((), jnp.bfloat16))
    numerator = jnp.dot(weights_flat, obs_masked, preferred_element_type=jnp.float32)
    masked = jnp.where(live_mask[None, :], weights_flat, jnp.zeros((), jnp.bfloat16))
    density = jnp.sum(masked, axis=1, dtype=jnp.float32)
    grid = (
        (numerator / jnp.sqrt(density)[:, None])
        .astype(jnp.bfloat16)
        .reshape(tile_rows, tile_cols, channel_count)
    )
    return encode_tile(grid, conv1_weight, conv2_weight)


def solution(mesh):
    in_specs = (
        P(("lat", "lon"), None),
        P(),
        P(("lat", "lon")),
        P(("lat", "lon")),
        P("lat", "lon"),
        P("lat", "lon", None),
        P(),
        P(),
    )
    out_specs = P("lat", "lon", None)
    return jax.shard_map(body, mesh=mesh, in_specs=in_specs, out_specs=out_specs, check_vma=False)
```

time: 123 us -> 244 us (1.98)
  local copies, waits for them, and re-layouts: 14.1 us -> 137 us
  starting transfers between devices: 27.2 us -> 14.3 us
  waiting for transfers between devices: 20.2 us -> 28.6 us
  matrix products: 44.9 us -> 52.8 us
  other arithmetic: 14 us -> 9.01 us
    slice x18 -> x22, local copies, waits for them, and re-layouts: 3.59 us -> 63 us  [the longest x18 62.7 us: strided_valid(): lax.slice(field, (row_tap, col_tap, 0), (row_tap + 2 * out_rows - 1, col_...]
    another operation x4 -> x57, local copies, waits for them, and re-layouts: 0.56 us -> 43 us  [the longest x28 25.4 us: body(): jnp.stack([key[c:c + obs_count] % digit for c in range(capacity)], axis=1)]
    concatenate x5 -> x1, local copies, waits for them, and re-layouts: 0.27 us -> 13.6 us  [body(): jnp.concatenate([hi_cols, lo_cols, jnp.zeros((obs_count, channel_count -...]
    ppermute x6 -> x3, starting transfers between devices: 15.9 us -> 2.92 us  [cyclic(): return lax.ppermute(value, axes if len(axes) > 1 else axes[0], pairs)]
    reshape x4 -> x10, local copies, waits for them, and re-layouts: 2.52 us -> 10.9 us  [the longest x9 9.66 us: strided_valid(): window.reshape(-1, depth)]
    dot_general x13 -> x19, matrix products: 10.4 us -> 17.5 us  [the longest x18 16.2 us: strided_valid(): jnp.dot(window.reshape(-1, depth), kernel[row_tap, col_tap], preferred_el...]
    ppermute x6 -> x3, waiting for transfers between devices: 1.42 us -> 6.4 us  [cyclic(): return lax.ppermute(value, axes if len(axes) > 1 else axes[0], pairs)]
    scatter x0 -> x1, local copies, waits for them, and re-layouts: none -> 3.92 us  [body(): outgoing = packed.at[:, capacity, :].set(digit_row)]
  transfers between devices with their start and end apart: 7 -> 4, of which waited for: 2 -> 3; matrix products, arithmetic and copies ran while one was open for 15% -> 3% of each run, Pallas kernels for 0% -> 0%
where the time goes in v2:
time: 244 us; the launch traced here: 243 us
  local copies, waits for them, and re-layouts  137 us (56%)
  matrix products  52.8 us (22%)
  waiting for transfers between devices  28.6 us (12%)
  starting transfers between devices  14.3 us (6%)
  other arithmetic  9.01 us (4%)
    slice x18, local copies, waits for them, and re-layouts, strided_valid(): lax.slice(field, (row_tap, col_tap, 0), (row_tap + 2 * out_rows - 1, col_...  62.7 us
    another operation x28, local copies, waits for them, and re-layouts, body(): jnp.stack([key[c:c + obs_count] % digit for c in range(capacity)], axis=1)  25.4 us
    all_to_all x1, waiting for transfers between devices, body(): lax.all_to_all(outgoing, ('lat', 'lon'), split_axis=0, concat_axis=0, til...  22.2 us
    another operation x28, local copies, waits for them, and re-layouts, body(): jnp.stack([key[c:c + obs_count] // digit for c in range(capacity)], axis=1)  17.5 us
    dot_general x1, matrix products, body(): jnp.dot(weights_flat, obs_masked, preferred_element_type=jnp.float32)  17.4 us
    dot_general x18, matrix products, strided_valid(): jnp.dot(window.reshape(-1, depth), kernel[row_tap, col_tap], preferred_el...  16.2 us
    concatenate x1, local copies, waits for them, and re-layouts, body(): jnp.concatenate([hi_cols, lo_cols, jnp.zeros((obs_count, channel_count -...  13.6 us
    dot_general x1, matrix products, body(): jnp.dot(radiances, project_weight, preferred_element_type=jnp.float32)  12 us
  transfers between devices with their start and end apart: 4, of which 3 were waited for; matrix products, arithmetic and copies ran while one was open for 3% of the time, Pallas kernels for 0%

profile of v2, /device:TPU:0, one launch (start us, length us, event | category | flops | bytes accessed | tf_op | source)
XLA Modules:
  0.0 242.6 jit_solution(2375905039393573813)
XLA Ops:
  44.4 13.6 %concatenate.19 = bf16[1024,256]{1,0:T(8,128)(2,1)} concatenate(bf16[1024,1]{1,0:T(8,128)(2,1)} %stack.280, bf16[1024,1]{1,0:T(8,128)(2,1)} %stack.281, bf16[1024,1]{1,0:T(8,128)(2,1)} %stack.282, bf16[1024,1]{1,0:T(8,128)(2,1)} %stack.283, bf16[1024,1]{1,0:T(8,128)(2,1)S(1)} %stack.284, bf16[1024,1]{1,0:T(8,128)(2,1)S(1)} %stack.285, bf16[1024,1]{1,0:T(8,128)(2,1)S(1)} %stack.286, ...), dimensions={1} | concatenate | bytes 1048576 | tf_op jit(solution)/shard_map/concatenate | solution.py:94
  59.7 12.0 %fusion.214 = bf16[1024,256]{1,0:T(8,128)(2,1)S(1)} fusion(bf16[8461,256]{1,0:T(8,128)(2,1)} %param.11, bf16[1024,8461]{0,1:T(8,128)(2,1)} %param.10), kind=kOutput, calls=%bitcast_fusion.10.clone.2 | convolution fusion | flops 4436262912 | bytes 22184448 | tf_op jit(solution)/shard_map/dot_general | solution.py:86
  71.7 5.9 %fusion.7 = bf16[4096,256]{1,0:T(8,128)(2,1)} fusion(s32[4096]{0:T(1024)S(1)} %add.254, pred[4096]{0:T(1024)(128)(4,1)S(1)} %and.272, bf16[1024,256]{1,0:T(8,128)(2,1)S(1)} %fusion.214), kind=kOutput, calls=%fused_computation.9 | convolution fusion | flops 2156920832 | bytes 2641920 | tf_op jit(solution)/shard_map/dot_general | solution.py:89
  77.6 3.9 %scatter.4 = bf16[128,32,256]{2,1,0:T(8,128)(2,1)} dynamic-update-slice(bf16[128,32,256]{2,1,0:T(8,128)(2,1)} %bitcast.1, bf16[128,1,256]{2,1,0:T(2,128)(2,1)S(1)} %copy.125, s32[]{:T(128)} %constant.407.clone.1, s32[]{:T(128)} %constant.411.clone.1, s32[]{:T(128)} %constant.407.clone.1) | dynamic-update-slice | bytes 131076 | tf_op jit(solution)/shard_map/scatter | solution.py:105
  81.6 11.4 %all-to-all-start = ((bf16[128,32,256]{2,1,0:T(8,128)(2,1)}), bf16[128,32,256]{2,1,0:T(8,128)(2,1)S(1)}, u32[]{:S(2)}, u32[]{:S(2)}) async-start(bf16[128,32,256]{2,1,0:T(8,128)(2,1)} %scatter.4), calls=%async_computation | async-start | bytes 4194304 | tf_op jit(solution)/shard_map/all_to_all | solution.py:106
  93.6 6.3 %convert_reduce_fusion = f32[64,32]{1,0:T(8,128)S(1)} fusion(bf16[64,32,2560]{2,1,0:T(8,128)(2,1)} %param.15, pred[2560]{0:T(1024)(128)(4,1)S(1)} %iota_compare_fusion.13), kind=kLoop, calls=%fused_computation.2 | loop fusion | flops 15726592 | bytes 10496512 | tf_op jit(solution)/shard_map/reduce_sum | solution.py:123
  100.0 22.2 %all-to-all-done = bf16[128,32,256]{2,1,0:T(8,128)(2,1)S(1)} async-done(((bf16[128,32,256]{2,1,0:T(8,128)(2,1)}), bf16[128,32,256]{2,1,0:T(8,128)(2,1)S(1)}, u32[]{:S(2)}, u32[]{:S(2)}) %all-to-all-start) | async-done | bytes 2097184 | tf_op jit(solution)/shard_map/all_to_all | solution.py:106
  122.2 1.4 reshape.201
  124.1 17.4 %fusion.13 = bf16[2048,256]{0,1:T(8,128)(2,1)S(1)} fusion(bf16[2048,2560]{1,0:T(8,128)(2,1)} %bitcast.133, bf16[3584,256]{1,0:T(8,128)(2,1)} %reshape.201, s32[3584]{0:T(1024)S(1)} %sub.149, pred[2560]{0:T(1024)(128)(4,1)S(1)} %iota_compare_fusion.13, f32[2048]{0:T(1024)S(1)} %sqrt.11), kind=kOutput, calls=%fused_computation.14 | convolution fusion | flops 7393509376 | bytes 13394432 | tf_op jit(solution)/shard_map/dot_general | solution.py:121
  143.5 1.6 collective-permute-start.2
  145.2 6.3 %collective-permute-done = bf16[3,3,256]{2,1,0:T(4,128)(2,1)S(1)} collective-permute-done((bf16[3,3,256]{2,1,0:T(4,128)(2,1)S(1)}, bf16[3,3,256]{2,1,0:T(4,128)(2,1)S(1)}, u32[]{:S(2)}, u32[]{:S(2)}) %collective-permute-start) | collective-permute-done | bytes 4640 | tf_op jit(solution)/shard_map/ppermute | solution.py:18
  152.3 2.0 slice.311
  154.3 1.7 slice.309
  156.1 10.5 %slice.307 = bf16[33,17,256]{2,1,0:T(8,128)(2,1)} slice(bf16[67,35,256]{2,1,0:T(8,128)(2,1)S(1)} %maximum_maximum_fusion), slice={[2:67:2], [0:33:2], [0:256:1]} | slice | bytes 574464 | tf_op jit(solution)/shard_map/slice | solution.py:27
  166.6 10.5 %slice.305 = bf16[33,17,256]{2,1,0:T(8,128)(2,1)} slice(bf16[67,35,256]{2,1,0:T(8,128)(2,1)S(1)} %maximum_maximum_fusion), slice={[1:66:2], [2:35:2], [0:256:1]} | slice | bytes 574464 | tf_op jit(solution)/shard_map/slice | solution.py:27
  179.2 10.6 %slice.299 = bf16[33,17,256]{2,1,0:T(8,128)(2,1)} slice(bf16[67,35,256]{2,1,0:T(8,128)(2,1)S(1)} %maximum_maximum_fusion), slice={[0:65:2], [2:35:2], [0:256:1]} | slice | bytes 574464 | tf_op jit(solution)/shard_map/slice | solution.py:27
  189.7 10.5 %slice.297 = bf16[33,17,256]{2,1,0:T(8,128)(2,1)} slice(bf16[67,35,256]{2,1,0:T(8,128)(2,1)S(1)} %maximum_maximum_fusion), slice={[0:65:2], [1:34:2], [0:256:1]} | slice | bytes 574464 | tf_op jit(solution)/shard_map/slice | solution.py:27
  200.2 10.5 %slice.295 = bf16[33,17,256]{2,1,0:T(8,128)(2,1)} slice(bf16[67,35,256]{2,1,0:T(8,128)(2,1)S(1)} %maximum_maximum_fusion), slice={[0:65:2], [0:33:2], [0:256:1]} | slice | bytes 574464 | tf_op jit(solution)/shard_map/slice | solution.py:27
  222.3 1.8 reshape.206
  224.2 2.1 fusion.57
  226.2 1.8 reshape.205
  228.0 2.0 fusion.59
  230.1 1.8 reshape.204
  231.9 2.7 %fusion.20 = f32[561,256]{1,0:T(8,128)} fusion(f32[561,256]{1,0:T(8,128)S(1)} %fusion.45, f32[561,256]{1,0:T(8,128)S(1)} %fusion.47, f32[561,256]{1,0:T(8,128)S(1)} %fusion.49, f32[561,256]{1,0:T(8,128)S(1)} %fusion.51, f32[561,256]{1,0:T(8,128)S(1)} %fusion.53, f32[561,256]{1,0:T(8,128)S(1)} %fusion.55, f32[561,256]{1,0:T(8,128)} %fusion.57, ...), kind=kOutput, calls=%fused_computation.24 | convolution fusion | flops 74680320 | bytes 5606400 | tf_op jit(solution)/shard_map/dot_general | solution.py:33
  (131 shorter events, 70.8 us)
Async XLA Ops:
  31.4 12.7 %copy-start.3 = (s32[1024]{0:T(1024)S(1)}, s32[1024]{0:T(1024)}, u32[]{:S(2)}) copy-start(s32[1024]{0:T(1024)} %param.12) | copy-start | bytes 12292
  81.6 40.6 %all-to-all-start = ((bf16[128,32,256]{2,1,0:T(8,128)(2,1)}), bf16[128,32,256]{2,1,0:T(8,128)(2,1)S(1)}, u32[]{:S(2)}, u32[]{:S(2)}) async-start(bf16[128,32,256]{2,1,0:T(8,128)(2,1)} %scatter.4), calls=%async_computation | async-start | bytes 4194304 | tf_op jit(solution)/shard_map/all_to_all | solution.py:106
  141.6 9.8 %collective-permute-start.1 = (bf16[3,32,256]{2,1,0:T(8,128)(2,1)S(1)}, bf16[3,32,256]{2,1,0:T(8,128)(2,1)S(1)}, u32[]{:S(2)}, u32[]{:S(2)}) collective-permute-start(bf16[3,32,256]{2,1,0:T(8,128)(2,1)S(1)} %bitcast.139), channel_id=1, source_target_pairs={{0,16},{16,32},{32,48},{48,64},{64,80},{80,96},{96,112},{112,0},{1... | collective-permute-start | bytes 147464 | tf_op jit(solution)/shard_map/ppermute | solution.py:18
  142.9 8.6 %collective-permute-start = (bf16[3,3,256]{2,1,0:T(4,128)(2,1)S(1)}, bf16[3,3,256]{2,1,0:T(4,128)(2,1)S(1)}, u32[]{:S(2)}, u32[]{:S(2)}) collective-permute-start(bf16[3,3,256]{2,1,0:T(4,128)(2,1)S(1)} %slice.335), channel_id=1, source_target_pairs={{0,17},{1,18},{2,19},{3,20},{4,21},{5,22},{6,23},{7,24},{8,25},{9,... | collective-permute-start | bytes 13832 | tf_op jit(solution)/shard_map/ppermute | solution.py:18
  143.5 8.1 %collective-permute-start.2 = (bf16[64,3,256]{2,1,0:T(4,128)(2,1)S(1)}, bf16[64,3,256]{2,1,0:T(4,128)(2,1)S(1)}, u32[]{:S(2)}, u32[]{:S(2)}) collective-permute-start(bf16[64,3,256]{2,1,0:T(4,128)(2,1)S(1)} %slice.337), channel_id=1, source_target_pairs={{0,1},{1,2},{2,3},{3,4},{4,5},{5,6},{6,7},{7,8},{8,9},{9,10},{10,1... | collective-permute-start | bytes 294920 | tf_op jit(solution)/shard_map/ppermute | solution.py:18
  210.7 3.4 %copy-start.1 = (bf16[33,17,256]{2,1,0:T(8,128)(2,1)S(1)}, bf16[33,17,256]{2,1,0:T(8,128)(2,1)}, u32[]{:S(2)}) copy-start(bf16[33,17,256]{2,1,0:T(8,128)(2,1)} %slice.307) | copy-start | bytes 861700
  211.7 4.5 %copy-start = (bf16[33,17,256]{2,1,0:T(8,128)(2,1)S(1)}, bf16[33,17,256]{2,1,0:T(8,128)(2,1)}, u32[]{:S(2)}) copy-start(bf16[33,17,256]{2,1,0:T(8,128)(2,1)} %slice.305) | copy-start | bytes 861700
  234.6 5.9 %copy-start.2 = (bf16[3,3,256,256]{3,2,1,0:T(8,128)(2,1)S(1)}, bf16[3,3,256,256]{3,2,1,0:T(8,128)(2,1)}, u32[]{:S(2)}) copy-start(bf16[3,3,256,256]{3,2,1,0:T(8,128)(2,1)} %param.17) | copy-start | bytes 3538948

commit v3 on v2

--- a/solution.py
+++ b/solution.py
@@ -21,21 +21,27 @@
 def strided_valid(field, kernel):
     height, breadth, depth = field.shape
     out_rows, out_cols = ((height - 3) // 2 + 1, (breadth - 3) // 2 + 1)
-    summed = jnp.zeros((out_rows * out_cols, kernel.shape[3]), jnp.float32)
+    even_h, even_w = (height + height % 2, breadth + breadth % 2)
+    padded = jnp.pad(field, ((0, even_h - height), (0, even_w - breadth), (0, 0)))
+    pairs = padded.reshape(even_h // 2, 2, even_w // 2, 2 * depth)
+    zero_block = jnp.zeros((depth, depth), kernel.dtype)
+    near = jnp.zeros((out_rows * (even_w // 2), depth), jnp.float32)
+    far = jnp.zeros((out_rows * (even_w // 2), depth), jnp.float32)
     for row_tap in range(3):
-        for col_tap in range(3):
-            window = lax.slice(
-                field,
-                (row_tap, col_tap, 0),
-                (row_tap + 2 * out_rows - 1, col_tap + 2 * out_cols - 1, depth),
-                (2, 2, 1),
-            )
-            summed = summed + jnp.dot(
-                window.reshape(-1, depth),
-                kernel[row_tap, col_tap],
-                preferred_element_type=jnp.float32,
-            )
-    return summed.reshape(out_rows, out_cols, kernel.shape[3])
+        rows = pairs[row_tap // 2 : row_tap // 2 + out_rows, row_tap % 2]
+        stacked = jnp.concatenate(
+            [
+                jnp.concatenate([kernel[row_tap, 0], kernel[row_tap, 2]], axis=1),
+                jnp.concatenate([kernel[row_tap, 1], zero_block], axis=1),
+            ],
+            axis=0,
+        )
+        both = jnp.dot(rows.reshape(-1, 2 * depth), stacked, preferred_element_type=jnp.float32)
+        near = near + both[:, :depth]
+        far = far + both[:, depth:]
+    near = near.reshape(out_rows, even_w // 2, depth)
+    far = far.reshape(out_rows, even_w // 2, depth)
+    return near[:, :out_cols] + far[:, 1 : out_cols + 1]
 
 
 def encode_tile(grid, conv1_weight, conv2_weight):
@@ -88,21 +94,19 @@
     )
     packed = jnp.dot(selector, payload, preferred_element_type=jnp.float32).astype(jnp.bfloat16)
     packed = packed.reshape(peer_count, chunk_rows, channel_count)
-    key = jnp.concatenate([slot_offsets + 1, jnp.zeros((capacity,), jnp.int32)])
-    hi_cols = jnp.stack([key[c : c + obs_count] // digit for c in range(capacity)], axis=1)
-    lo_cols = jnp.stack([key[c : c + obs_count] % digit for c in range(capacity)], axis=1)
-    windows = jnp.concatenate(
-        [hi_cols, lo_cols, jnp.zeros((obs_count, channel_count - 2 * capacity), jnp.int32)],
+    key = slot_offsets + 1
+    digits = jnp.stack([key // digit, key % digit], axis=1).astype(jnp.bfloat16)
+    packed_digits = jnp.dot(selector, digits, preferred_element_type=jnp.float32)
+    packed_digits = packed_digits.reshape(peer_count, chunk_rows, 2)[:, :capacity]
+    digit_row = jnp.concatenate(
+        [
+            packed_digits[:, :, 0],
+            packed_digits[:, :, 1],
+            jnp.zeros((peer_count, channel_count - 2 * capacity), jnp.float32),
+        ],
         axis=1,
     ).astype(jnp.bfloat16)
-    run_head = (run_starts[:, None] == row_index[None, :]).astype(jnp.bfloat16)
-    digit_row = jnp.dot(run_head, windows, preferred_element_type=jnp.float32)
-    column = jnp.arange(channel_count, dtype=jnp.int32)
-    digit_live = (column[None, :] % capacity < run_counts[:, None]) & (
-        column[None, :] < 2 * capacity
-    )
-    digit_row = jnp.where(digit_live, digit_row, 0.0).astype(jnp.bfloat16)
-    outgoing = packed.at[:, capacity, :].set(digit_row)
+    outgoing = lax.dynamic_update_slice(packed, digit_row[:, None, :], (0, capacity, 0))
     arrived = lax.all_to_all(outgoing, ("lat", "lon"), split_axis=0, concat_axis=0, tiled=True)
     arrived_rows = arrived[:, :capacity].reshape(-1, channel_count)
     arrived_digits = arrived[:, capacity].astype(jnp.int32)

time: 244 us -> 111 us (0.45)
  local copies, waits for them, and re-layouts: 137 us -> 14.1 us
  matrix products: 52.8 us -> 42.5 us
    slice x18 -> x2, local copies, waits for them, and re-layouts: 62.7 us -> 1.2 us  [strided_valid(): rows = pairs[row_tap // 2:row_tap // 2 + out_rows, row_tap % 2]]
    another operation x57 -> x9, local copies, waits for them, and re-layouts: 43 us -> 2.79 us  [the longest x6 2.67 us: strided_valid(): rows.reshape(-1, 2 * depth)]
    concatenate x1 -> x4, local copies, waits for them, and re-layouts: 13.6 us -> 0.19 us  [body(): jnp.concatenate([packed_digits[:, :, 0], packed_digits[:, :, 1], jnp.zero...]
    dot_general x19 -> x7, matrix products: 17.5 us -> 7.25 us  [the longest x1 3.88 us: body(): jnp.dot(selector, digits, preferred_element_type=jnp.float32)]
    reshape x10 -> x6, local copies, waits for them, and re-layouts: 10.9 us -> 0.85 us  [the longest x2 0.64 us: strided_valid(): pairs = padded.reshape(even_h // 2, 2, even_w // 2, 2 * depth)]
    scatter x1 -> x0, local copies, waits for them, and re-layouts: 3.92 us -> none  [body(): outgoing = packed.at[:, capacity, :].set(digit_row)]
    dynamic_update_slice x0 -> x1, local copies, waits for them, and re-layouts: none -> 3.92 us  [body(): lax.dynamic_update_slice(packed, digit_row[:, None, :], (0, capacity, 0))]
  transfers between devices with their start and end apart: 4 -> 4, of which waited for: 3 -> 3; matrix products, arithmetic and copies ran while one was open for 3% -> 8% of each run, Pallas kernels for 0% -> 0%
where the time goes in v3:
time: 111 us
  matrix products  42.5 us (38%)
  waiting for transfers between devices  28.6 us (26%)
  local copies, waits for them, and re-layouts  14.1 us (13%)
  starting transfers between devices  13.6 us (12%)
  other arithmetic  10.8 us (10%)
  between operations  1.17 us (1%)
    all_to_all x1, waiting for transfers between devices, body(): lax.all_to_all(outgoing, ('lat', 'lon'), split_axis=0, concat_axis=0, til...  21.1 us
    dot_general x1, matrix products, body(): jnp.dot(weights_flat, obs_masked, preferred_element_type=jnp.float32)  17.4 us
    dot_general x1, matrix products, body(): jnp.dot(radiances, project_weight, preferred_element_type=jnp.float32)  12 us
    all_to_all x1, starting transfers between devices, body(): lax.all_to_all(outgoing, ('lat', 'lon'), split_axis=0, concat_axis=0, til...  11.3 us
    ppermute x3, waiting for transfers between devices, cyclic(): return lax.ppermute(value, axes if len(axes) > 1 else axes[0], pairs)  7.58 us
    reduce_sum x1, other arithmetic, body(): density = jnp.sum(masked, axis=1, dtype=jnp.float32)  6.38 us
    dot_general x1, matrix products, body(): jnp.dot(selector, payload, preferred_element_type=jnp.float32)  5.93 us
    dynamic_update_slice x1, local copies, waits for them, and re-layouts, body(): lax.dynamic_update_slice(packed, digit_row[:, None, :], (0, capacity, 0))  3.92 us
  transfers between devices with their start and end apart: 4, of which 3 were waited for; matrix products, arithmetic and copies ran while one was open for 8% of the time, Pallas kernels for 0%

profile of v3, /device:TPU:0, one launch (start us, length us, event | category | flops | bytes accessed | tf_op | source)
XLA Modules:
  0.0 110.8 jit_solution(17250471256152158031)
XLA Ops:
  0.0 0.9 convert_reduce_fusion.1
  1.3 0.7 fusion.102
  2.0 3.9 %fusion.14 = bf16[4096,2]{0,1:T(2,128)(2,1)S(1)} fusion(s32[4096]{0:T(1024)S(1)} %add.102, pred[4096]{0:T(1024)(128)(4,1)S(1)} %and.36, bf16[1024,1]{0,1:T(2,128)(2,1)S(1)} %stack.13, bf16[1024,1]{0,1:T(2,128)(2,1)S(1)} %stack.12), kind=kOutput, calls=%fused_computation.13 | convolution fusion | flops 25182208 | bytes 40960 | tf_op jit(solution)/shard_map/dot_general | solution.py:99
  6.1 12.0 %fusion.164 = bf16[1024,256]{1,0:T(8,128)(2,1)S(1)} fusion(bf16[8461,256]{1,0:T(8,128)(2,1)} %param.9, bf16[1024,8461]{0,1:T(8,128)(2,1)} %param.8), kind=kOutput, calls=%bitcast_fusion.7.clone.2 | convolution fusion | flops 4436262912 | bytes 22184448 | tf_op jit(solution)/shard_map/dot_general | solution.py:92
  18.1 5.9 %fusion.11 = bf16[4096,256]{1,0:T(8,128)(2,1)} fusion(s32[4096]{0:T(1024)S(1)} %add.102, pred[4096]{0:T(1024)(128)(4,1)S(1)} %and.36, bf16[1024,256]{1,0:T(8,128)(2,1)S(1)} %fusion.164), kind=kOutput, calls=%fused_computation.12 | convolution fusion | flops 2156920832 | bytes 2641920 | tf_op jit(solution)/shard_map/dot_general | solution.py:95
  24.4 3.9 %dynamic_update_slice.3 = bf16[128,32,256]{2,1,0:T(8,128)(2,1)} dynamic-update-slice(bf16[128,32,256]{2,1,0:T(8,128)(2,1)} %bitcast.1, bf16[128,1,256]{2,1,0:T(2,128)(2,1)S(1)} %maximum_maximum_fusion, s32[]{:T(128)} %constant.25.clone.1, s32[]{:T(128)} %constant.51.clone.1, s32[]{:T(128)} %constant.25.clone.1) | dynamic-update-slice | bytes 131076 | tf_op jit(solution)/shard_map/dynamic_update_slice | solution.py:109
  28.3 11.3 %all-to-all-start = ((bf16[128,32,256]{2,1,0:T(8,128)(2,1)}), bf16[128,32,256]{2,1,0:T(8,128)(2,1)S(1)}, u32[]{:S(2)}, u32[]{:S(2)}) async-start(bf16[128,32,256]{2,1,0:T(8,128)(2,1)} %dynamic_update_slice.3), calls=%async_computation | async-start | bytes 4194304 | tf_op jit(solution)/shard_map/all_to_all | solution.py:110
  40.4 6.4 %convert_reduce_fusion = f32[64,32]{1,0:T(8,128)S(1)} fusion(bf16[64,32,2560]{2,1,0:T(8,128)(2,1)} %param.13, pred[2560]{0:T(1024)(128)(4,1)S(1)} %iota_compare_fusion.14), kind=kLoop, calls=%fused_computation.2 | loop fusion | flops 15726592 | bytes 10496512 | tf_op jit(solution)/shard_map/reduce_sum | solution.py:127
  46.8 1.1 slice_bitcast_fusion.17
  47.9 21.1 %all-to-all-done = bf16[128,32,256]{2,1,0:T(8,128)(2,1)S(1)} async-done(((bf16[128,32,256]{2,1,0:T(8,128)(2,1)}), bf16[128,32,256]{2,1,0:T(8,128)(2,1)S(1)}, u32[]{:S(2)}, u32[]{:S(2)}) %all-to-all-start) | async-done | bytes 2097184 | tf_op jit(solution)/shard_map/all_to_all | solution.py:110
  69.0 1.4 %reshape.151 = bf16[3584,256]{1,0:T(8,128)(2,1)} reshape(bf16[128,28,256]{2,1,0:T(8,128)(2,1)S(1)} %bitcast.87) | data formatting | bytes 3670016 | tf_op jit(solution)/shard_map/reshape | solution.py:111
  70.8 17.4 %fusion.24 = bf16[2048,256]{0,1:T(8,128)(2,1)S(1)} fusion(bf16[2048,2560]{1,0:T(8,128)(2,1)} %bitcast.86, bf16[3584,256]{1,0:T(8,128)(2,1)} %reshape.151, s32[3584]{0:T(1024)S(1)} %sub.14, pred[2560]{0:T(1024)(128)(4,1)S(1)} %iota_compare_fusion.14, f32[2048]{0:T(1024)S(1)} %sqrt.11), kind=kOutput, calls=%fused_computation.24 | convolution fusion | flops 7393509376 | bytes 13394432 | tf_op jit(solution)/shard_map/dot_general | solution.py:125
  88.2 0.5 copy.18
  89.3 1.3 %collective-permute-start.1 = (bf16[3,32,256]{2,1,0:T(8,128)(2,1)S(1)}, bf16[3,32,256]{2,1,0:T(8,128)(2,1)S(1)}, u32[]{:S(2)}, u32[]{:S(2)}) collective-permute-start(bf16[3,32,256]{2,1,0:T(8,128)(2,1)S(1)} %bitcast.92), channel_id=1, source_target_pairs={{0,16},{16,32},{32,48},{48,64},{64,80},{80,96},{96,112},{112,0},{1... | collective-permute-start | bytes 147464 | tf_op jit(solution)/shard_map/ppermute | solution.py:18
  90.5 0.9 slice_bitcast_fusion.8
  91.6 0.7 collective-permute-start.2
  92.2 5.2 %collective-permute-done = bf16[3,3,256]{2,1,0:T(4,128)(2,1)S(1)} collective-permute-done((bf16[3,3,256]{2,1,0:T(4,128)(2,1)S(1)}, bf16[3,3,256]{2,1,0:T(4,128)(2,1)S(1)}, u32[]{:S(2)}, u32[]{:S(2)}) %collective-permute-start) | collective-permute-done | bytes 4640 | tf_op jit(solution)/shard_map/ppermute | solution.py:18
  97.4 2.4 %collective-permute-done.2 = bf16[64,3,256]{2,1,0:T(4,128)(2,1)S(1)} collective-permute-done((bf16[64,3,256]{2,1,0:T(4,128)(2,1)S(1)}, bf16[64,3,256]{2,1,0:T(4,128)(2,1)S(1)}, u32[]{:S(2)}, u32[]{:S(2)}) %collective-permute-start.2) | collective-permute-done | bytes 98336 | tf_op jit(solution)/shard_map/ppermute | solution.py:18
  99.9 0.7 fusion.28
  100.5 0.5 reshape.154
  101.0 1.1 %fusion.129 = (bf16[33,1,18,512]{3,2,1,0:T(8,128)(2,1)}, bf16[33,1,18,512]{3,2,1,0:T(8,128)(2,1)S(1)}, bf16[33,1,18,512]{3,2,1,0:T(8,128)(2,1)S(1)}) fusion(bf16[34,2,18,512]{3,2,1,0:T(8,128)(2,1)S(1)} %reshape.154), kind=kLoop, calls=%fused_computation.176 | loop fusion | bytes 3649536 | tf_op jit(solution)/shard_map/slice | solution.py:31
  102.2 2.1 %reshape_squeeze.18 = bf16[594,512]{1,0:T(8,128)(2,1)} reshape(bf16[33,1,18,512]{3,2,1,0:T(8,128)(2,1)} %get-tuple-element.9) | data formatting | bytes 1216512 | tf_op jit(solution)/shard_map/reshape;squeeze | solution.py:39
  104.7 1.7 %fusion.46 = f32[594,512]{1,0:T(8,128)S(1)} fusion(bf16[594,512]{1,0:T(8,128)(2,1)} %reshape_squeeze.18, bf16[256,256]{1,0:T(8,128)(2,1)} %get-tuple-element.26, bf16[256,256]{1,0:T(8,128)(2,1)} %get-tuple-element.27, bf16[256,256]{1,0:T(8,128)(2,1)} %get-tuple-element.21), kind=kOutput, calls=%fused_computation.54 | convolution fusion | flops 313524224 | bytes 2217984 | tf_op jit(solution)/shard_map/dot_general | solution.py:39
  110.2 0.7 fusion.99
  (78 shorter events, 6.0 us)
Async XLA Ops:
  28.3 40.6 %all-to-all-start = ((bf16[128,32,256]{2,1,0:T(8,128)(2,1)}), bf16[128,32,256]{2,1,0:T(8,128)(2,1)S(1)}, u32[]{:S(2)}, u32[]{:S(2)}) async-start(bf16[128,32,256]{2,1,0:T(8,128)(2,1)} %dynamic_update_slice.3), calls=%async_computation | async-start | bytes 4194304 | tf_op jit(solution)/shard_map/all_to_all | solution.py:110
  40.4 6.5 %copy-start = (bf16[3,3,256,256]{3,2,1,0:T(8,128)(2,1)S(1)}, bf16[3,3,256,256]{3,2,1,0:T(8,128)(2,1)}, u32[]{:S(2)}) copy-start(bf16[3,3,256,256]{3,2,1,0:T(8,128)(2,1)} %param.14) | copy-start | bytes 3538948
  88.2 2.3 %copy-start.1 = (bf16[3,3,256,256]{3,2,1,0:T(8,128)(2,1)S(1)}, bf16[3,3,256,256]{3,2,1,0:T(8,128)(2,1)}, u32[]{:S(2)}) copy-start(bf16[3,3,256,256]{3,2,1,0:T(8,128)(2,1)} %param.15) | copy-start | bytes 3538948
  88.9 8.6 %collective-permute-start = (bf16[3,3,256]{2,1,0:T(4,128)(2,1)S(1)}, bf16[3,3,256]{2,1,0:T(4,128)(2,1)S(1)}, u32[]{:S(2)}, u32[]{:S(2)}) collective-permute-start(bf16[3,3,256]{2,1,0:T(4,128)(2,1)S(1)} %slice.211), channel_id=1, source_target_pairs={{0,17},{1,18},{2,19},{3,20},{4,21},{5,22},{6,23},{7,24},{8,25},{9,... | collective-permute-start | bytes 13832 | tf_op jit(solution)/shard_map/ppermute | solution.py:18
  89.3 8.1 %collective-permute-start.1 = (bf16[3,32,256]{2,1,0:T(8,128)(2,1)S(1)}, bf16[3,32,256]{2,1,0:T(8,128)(2,1)S(1)}, u32[]{:S(2)}, u32[]{:S(2)}) collective-permute-start(bf16[3,32,256]{2,1,0:T(8,128)(2,1)S(1)} %bitcast.92), channel_id=1, source_target_pairs={{0,16},{16,32},{32,48},{48,64},{64,80},{80,96},{96,112},{112,0},{1... | collective-permute-start | bytes 147464 | tf_op jit(solution)/shard_map/ppermute | solution.py:18
  91.6 8.3 %collective-permute-start.2 = (bf16[64,3,256]{2,1,0:T(4,128)(2,1)S(1)}, bf16[64,3,256]{2,1,0:T(4,128)(2,1)S(1)}, u32[]{:S(2)}, u32[]{:S(2)}) collective-permute-start(bf16[64,3,256]{2,1,0:T(4,128)(2,1)S(1)} %slice.213), channel_id=1, source_target_pairs={{0,1},{1,2},{2,3},{3,4},{4,5},{5,6},{6,7},{7,8},{8,9},{9,10},{10,1... | collective-permute-start | bytes 294920 | tf_op jit(solution)/shard_map/ppermute | solution.py:18
  104.4 2.0 %copy-start.12 = (bf16[256,256]{1,0:T(8,128)(2,1)S(1)}, bf16[256,256]{1,0:T(8,128)(2,1)}, u32[]{:S(2)}) copy-start(bf16[256,256]{1,0:T(8,128)(2,1)} %get-tuple-element.23) | copy-start | bytes 393220
  104.4 2.0 %copy-start.13 = (bf16[256,256]{1,0:T(8,128)(2,1)S(1)}, bf16[256,256]{1,0:T(8,128)(2,1)}, u32[]{:S(2)}) copy-start(bf16[256,256]{1,0:T(8,128)(2,1)} %get-tuple-element.24) | copy-start | bytes 393220
  104.4 2.0 %copy-start.14 = (bf16[256,256]{1,0:T(8,128)(2,1)S(1)}, bf16[256,256]{1,0:T(8,128)(2,1)}, u32[]{:S(2)}) copy-start(bf16[256,256]{1,0:T(8,128)(2,1)} %get-tuple-element.25) | copy-start | bytes 393220
  104.6 2.2 %copy-start.6 = (bf16[256,256]{1,0:T(8,128)(2,1)S(1)}, bf16[256,256]{1,0:T(8,128)(2,1)}, u32[]{:S(2)}) copy-start(bf16[256,256]{1,0:T(8,128)(2,1)} %get-tuple-element.22) | copy-start | bytes 393220
  104.7 2.2 %copy-start.7 = (bf16[256,256]{1,0:T(8,128)(2,1)S(1)}, bf16[256,256]{1,0:T(8,128)(2,1)}, u32[]{:S(2)}) copy-start(bf16[256,256]{1,0:T(8,128)(2,1)} %get-tuple-element.28) | copy-start | bytes 393220
  104.7 2.2 %copy-start.8 = (bf16[256,256]{1,0:T(8,128)(2,1)S(1)}, bf16[256,256]{1,0:T(8,128)(2,1)}, u32[]{:S(2)}) copy-start(bf16[256,256]{1,0:T(8,128)(2,1)} %get-tuple-element.29) | copy-start | bytes 393220
  108.2 0.9 copy-start.9
  108.2 1.0 copy-start.10
  108.2 1.0 copy-start.11
  108.4 1.1 copy-start.3
  108.4 1.1 copy-start.4
  108.5 1.1 copy-start.5
  108.6 1.1 %copy-start.2 = (bf16[256,256]{1,0:T(8,128)(2,1)S(1)}, bf16[256,256]{1,0:T(8,128)(2,1)}, u32[]{:S(2)}) copy-start(bf16[256,256]{1,0:T(8,128)(2,1)} %get-tuple-element.20) | copy-start | bytes 393220

commit v4 on v3

--- a/solution.py
+++ b/solution.py
@@ -44,11 +44,7 @@
     return near[:, :out_cols] + far[:, 1 : out_cols + 1]
 
 
-def encode_tile(grid, conv1_weight, conv2_weight):
-    rim = 3
-    north = cyclic(grid[-rim:], ("lat",), (1,))
-    west = cyclic(grid[:, -rim:], ("lon",), (1,))
-    north_west = cyclic(grid[-rim:, -rim:], ("lat", "lon"), (1, 1))
+def encode_tile(grid, north, west, north_west, conv1_weight, conv2_weight):
     top = jnp.concatenate([north_west, north], axis=1)
     top = jnp.where(lax.axis_index("lat") == 0, jnp.zeros((), top.dtype), top)
     body_rows = jnp.concatenate([west, grid], axis=1)
@@ -92,8 +88,6 @@
     payload = jnp.dot(radiances, project_weight, preferred_element_type=jnp.float32).astype(
         jnp.bfloat16
     )
-    packed = jnp.dot(selector, payload, preferred_element_type=jnp.float32).astype(jnp.bfloat16)
-    packed = packed.reshape(peer_count, chunk_rows, channel_count)
     key = slot_offsets + 1
     digits = jnp.stack([key // digit, key % digit], axis=1).astype(jnp.bfloat16)
     packed_digits = jnp.dot(selector, digits, preferred_element_type=jnp.float32)
@@ -106,7 +100,15 @@
         ],
         axis=1,
     ).astype(jnp.bfloat16)
-    outgoing = lax.dynamic_update_slice(packed, digit_row[:, None, :], (0, capacity, 0))
+    chunk_of = jnp.repeat(targets, chunk_rows)
+    row_of = jnp.tile(within, peer_count)
+    digit_pick = (row_of[:, None] == capacity) & (chunk_of[:, None] == targets[None, :])
+    selector_all = jnp.concatenate([selector, digit_pick.astype(jnp.bfloat16)], axis=1)
+    sources = jnp.concatenate([payload, digit_row], axis=0)
+    outgoing = jnp.dot(selector_all, sources, preferred_element_type=jnp.float32).astype(
+        jnp.bfloat16
+    )
+    outgoing = outgoing.reshape(peer_count, chunk_rows, channel_count)
     arrived = lax.all_to_all(outgoing, ("lat", "lon"), split_axis=0, concat_axis=0, tiled=True)
     arrived_rows = arrived[:, :capacity].reshape(-1, channel_count)
     arrived_digits = arrived[:, capacity].astype(jnp.int32)
@@ -122,15 +124,33 @@
     weights_flat = setconv_weights.reshape(-1, slot_count)
     live_mask = jnp.arange(slot_count, dtype=jnp.int32) < tile_counts.reshape(-1)[0]
     obs_masked = jnp.where(live_mask[:, None], obs_block, jnp.zeros((), jnp.bfloat16))
-    numerator = jnp.dot(weights_flat, obs_masked, preferred_element_type=jnp.float32)
     masked = jnp.where(live_mask[None, :], weights_flat, jnp.zeros((), jnp.bfloat16))
     density = jnp.sum(masked, axis=1, dtype=jnp.float32)
-    grid = (
-        (numerator / jnp.sqrt(density)[:, None])
-        .astype(jnp.bfloat16)
-        .reshape(tile_rows, tile_cols, channel_count)
+    root = jnp.sqrt(density).reshape(tile_rows, tile_cols, 1)
+    weights_cells = setconv_weights
+
+    def cells(weights, roots):
+        shape = weights.shape[:-1]
+        numer = jnp.dot(weights.reshape(-1, slot_count), obs_masked, preferred_element_type=jnp.float32)
+        return (numer.reshape(shape + (channel_count,)) / roots).astype(jnp.bfloat16)
+
+    rim = 3
+    rim_weights = jnp.concatenate(
+        [
+            weights_cells[-rim:].reshape(-1, slot_count),
+            weights_cells[:, -rim:].reshape(-1, slot_count),
+        ],
+        axis=0,
     )
-    return encode_tile(grid, conv1_weight, conv2_weight)
+    rim_roots = jnp.concatenate([root[-rim:].reshape(-1, 1), root[:, -rim:].reshape(-1, 1)], axis=0)
+    rim_cells = cells(rim_weights, rim_roots)
+    north_rows = rim_cells[: rim * tile_cols].reshape(rim, tile_cols, channel_count)
+    west_cols = rim_cells[rim * tile_cols :].reshape(tile_rows, rim, channel_count)
+    north = cyclic(north_rows, ("lat",), (1,))
+    west = cyclic(west_cols, ("lon",), (1,))
+    north_west = cyclic(north_rows[:, -rim:], ("lat", "lon"), (1, 1))
+    grid = cells(weights_cells, root)
+    return encode_tile(grid, north, west, north_west, conv1_weight, conv2_weight)
 
 
 def solution(mesh):

time: 111 us -> 107 us (0.964); the launches traced: 111 us -> 105 us
  waiting for transfers between devices: 28.6 us -> 14.4 us
  local copies, waits for them, and re-layouts: 14.1 us -> 20.2 us
  other arithmetic: 10.8 us -> 15.4 us
  matrix products: 42.5 us -> 39.6 us
    ppermute x3, waiting for transfers between devices: 7.58 us -> 0.01 us  [cyclic(): return lax.ppermute(value, axes if len(axes) > 1 else axes[0], pairs)]
    all_to_all x1, waiting for transfers between devices: 21.1 us -> 14.4 us  [body(): lax.all_to_all(outgoing, ('lat', 'lon'), split_axis=0, concat_axis=0, til...]
    and x0 -> x2, other arithmetic: none -> 4.54 us  [the longest x1 3.15 us: body(): (source_rows[:, None] == row_index[None, :]) & valid_slot[:, None]]
    dynamic_update_slice x1 -> x0, local copies, waits for them, and re-layouts: 3.92 us -> none  [body(): lax.dynamic_update_slice(packed, digit_row[:, None, :], (0, capacity, 0))]
    unnamed x31 -> x43, local copies, waits for them, and re-layouts: 0.5 us -> 3.5 us
    slice x4 -> x8, local copies, waits for them, and re-layouts: 0.27 us -> 2.53 us  [the longest x1 2.42 us: body(): weights_cells[:, -rim:].reshape(-1, slot_count)]
    dot_general x0 -> x1, local copies, waits for them, and re-layouts: none -> 1.92 us  [cells(): jnp.dot(weights.reshape(-1, slot_count), obs_masked, preferred_element_ty...]
    reshape x0 -> x4, local copies, waits for them, and re-layouts: none -> 1.9 us  [the longest x1 1.63 us: body(): weights_cells[:, -rim:].reshape(-1, slot_count)]
  transfers between devices with their start and end apart: 4 -> 4, of which waited for: 3 -> 1; matrix products, arithmetic and copies ran while one was open for 8% -> 24% of each run, Pallas kernels for 0% -> 0%
where the time goes in v4:
time: 107 us; the launch traced here: 105 us
  matrix products  39.6 us (37%)
  local copies, waits for them, and re-layouts  20.2 us (19%)
  other arithmetic  15.4 us (14%)
  starting transfers between devices  14.5 us (14%)
  waiting for transfers between devices  14.4 us (13%)
  between operations  1.26 us (1%)
    all_to_all x1, waiting for transfers between devices, body(): lax.all_to_all(outgoing, ('lat', 'lon'), split_axis=0, concat_axis=0, til...  14.4 us
    dot_general x1, matrix products, body(): jnp.dot(radiances, project_weight, preferred_element_type=jnp.float32)  12.1 us
    all_to_all x1, starting transfers between devices, body(): lax.all_to_all(outgoing, ('lat', 'lon'), split_axis=0, concat_axis=0, til...  11.3 us
    dot_general x2, matrix products, cells(): jnp.dot(weights.reshape(-1, slot_count), obs_masked, preferred_element_ty...  8.79 us
    dot_general x1, matrix products, body(): jnp.dot(slot_table, arrived_rows, preferred_element_type=jnp.float32)  8.75 us
    reduce_sum x1, other arithmetic, body(): density = jnp.sum(masked, axis=1, dtype=jnp.float32)  6.28 us
    dot_general x1, matrix products, body(): jnp.dot(selector_all, sources, preferred_element_type=jnp.float32)  4.47 us
    unnamed x43, local copies, waits for them, and re-layouts  3.5 us
  transfers between devices with their start and end apart: 4, of which 1 were waited for; matrix products, arithmetic and copies ran while one was open for 24% of the time, Pallas kernels for 0%

profile of v4, /device:TPU:0, one launch (start us, length us, event | category | flops | bytes accessed | tf_op | source)
XLA Modules:
  0.0 105.4 jit_solution(8938430271724648415)
XLA Ops:
  0.0 0.9 convert_reduce_fusion.1
  1.3 0.7 fusion.110
  2.0 3.2 %fusion.6 = pred[4096,1024]{1,0:T(32,128)(4,1)S(1)} fusion(s32[4096]{0:T(1024)S(1)} %add.104, pred[4096]{0:T(1024)(128)(4,1)S(1)} %and.44), kind=kLoop, calls=%fused_computation.9 | loop fusion | flops 8388608 | bytes 4214784 | tf_op jit(solution)/shard_map/and | solution.py:86
  5.2 1.9 %copy-done = pred[4096,1024]{1,0:T(32,128)(4,1)} copy-done((pred[4096,1024]{1,0:T(32,128)(4,1)}, pred[4096,1024]{1,0:T(32,128)(4,1)S(1)}, u32[]{:S(2)}) %copy-start) | copy-done | bytes 4194328
  7.1 2.3 %convolution_convert_fusion = bf16[4096,2]{0,1:T(2,128)(2,1)S(1)} fusion(pred[4096,1024]{1,0:T(32,128)(4,1)S(1)} %fusion.6, bf16[1024,1]{0,1:T(2,128)(2,1)S(1)} %stack.13, bf16[1024,1]{0,1:T(2,128)(2,1)S(1)} %stack.12), kind=kOutput, calls=%fused_computation.11 | convolution fusion | flops 16793600 | bytes 4214784 | tf_op jit(solution)/shard_map/dot_general | solution.py:93
  9.7 1.4 %fusion.16 = pred[4096,128]{1,0:T(32,128)(4,1)S(1)} fusion(s32[4096]{0:T(1024)S(1)} %eq.84, pred[4096]{0:T(1024)(128)(4,1)S(1)} %eq.83), kind=kLoop, calls=%fused_computation.23 | loop fusion | flops 1048576 | bytes 544768 | tf_op jit(solution)/shard_map/and | solution.py:105
  11.1 12.1 %convolution_convert_fusion.1 = bf16[1024,256]{1,0:T(8,128)(2,1)S(1)} fusion(bf16[1024,8461]{0,1:T(8,128)(2,1)} %param.8, bf16[8461,256]{1,0:T(8,128)(2,1)} %param.9), kind=kOutput, calls=%fused_computation.33 | convolution fusion | flops 4436262912 | bytes 22184448 | tf_op jit(solution)/shard_map/dot_general | solution.py:88
  23.3 4.5 %fusion.7 = bf16[4096,256]{1,0:T(8,128)(2,1)} fusion(pred[4096,128]{1,0:T(32,128)(4,1)S(1)} %fusion.16, pred[4096,1024]{1,0:T(32,128)(4,1)S(1)} %copy-done.1, bf16[128,200]{1,0:T(8,128)(2,1)S(1)} %broadcast_in_dim.65, bf16[128,28]{1,0:T(8,128)(2,1)S(1)} %get-tuple-element.36, bf16[128,28]{1,0:T(8,128)(2,1)S(1)} %get-tuple-element.35, ...), kind=kOutput, calls=%fused_computation.10 | convolution fusion | flops 2424045568 | bytes 7405568 | tf_op jit(solution)/shard_map/dot_general | solution.py:108
  27.8 11.3 %all-to-all-start = ((bf16[128,32,256]{2,1,0:T(8,128)(2,1)}), bf16[128,32,256]{2,1,0:T(8,128)(2,1)S(1)}, u32[]{:S(2)}, u32[]{:S(2)}) async-start(bf16[128,32,256]{2,1,0:T(8,128)(2,1)} %bitcast.76), calls=%async_computation | async-start | bytes 4194304 | tf_op jit(solution)/shard_map/all_to_all | solution.py:112
  39.1 2.4 %slice.167 = bf16[64,3,2560]{2,1,0:T(4,128)(2,1)S(1)} slice(bf16[64,32,2560]{2,1,0:T(8,128)(2,1)} %param.13), slice={[0:64], [29:32], [0:2560]} | slice | bytes 1966080 | tf_op jit(solution)/shard_map/slice | solution.py:141
  42.2 6.3 %convert_reduce_fusion = f32[64,32]{1,0:T(8,128)S(1)} fusion(bf16[64,32,2560]{2,1,0:T(8,128)(2,1)} %param.13, pred[2560]{0:T(1024)(128)(4,1)S(1)} %iota_compare_fusion.14), kind=kLoop, calls=%fused_computation.2 | loop fusion | flops 15726592 | bytes 10496512 | tf_op jit(solution)/shard_map/reduce_sum | solution.py:128
  48.8 1.6 %reshape.146 = bf16[192,2560]{1,0:T(8,128)(2,1)} reshape(bf16[64,3,2560]{2,1,0:T(4,128)(2,1)S(1)} %slice.167) | data formatting | bytes 1966080 | tf_op jit(solution)/shard_map/reshape | solution.py:141
  50.5 2.4 %slice_bitcast_fusion.17 = (bf16[256,256]{1,0:T(8,128)(2,1)}, bf16[256,256]{1,0:T(8,128)(2,1)}, bf16[256,256]{1,0:T(8,128)(2,1)}, bf16[256,256]{1,0:T(8,128)(2,1...) fusion(bf16[3,3,256,256]{3,2,1,0:T(8,128)(2,1)} %param.14), kind=kLoop, calls=%fused_computation.140 | loop fusion | bytes 2359296 | tf_op jit(solution)/shard_map/squeeze | solution.py:34
  53.0 1.0 slice_bitcast_fusion.8
  54.0 14.4 %all-to-all-done = bf16[128,32,256]{2,1,0:T(8,128)(2,1)S(1)} async-done(((bf16[128,32,256]{2,1,0:T(8,128)(2,1)}), bf16[128,32,256]{2,1,0:T(8,128)(2,1)S(1)}, u32[]{:S(2)}, u32[]{:S(2)}) %all-to-all-start) | async-done | bytes 2097184 | tf_op jit(solution)/shard_map/all_to_all | solution.py:112
  68.4 1.4 %reshape.149 = bf16[3584,256]{1,0:T(8,128)(2,1)} reshape(bf16[128,28,256]{2,1,0:T(8,128)(2,1)S(1)} %bitcast.74) | data formatting | bytes 3670016 | tf_op jit(solution)/shard_map/reshape | solution.py:113
  70.3 8.7 %fusion.11 = bf16[2560,256]{1,0:T(8,128)(2,1)S(1)} fusion(bf16[3584,256]{1,0:T(8,128)(2,1)} %reshape.149, s32[3584]{0:T(1024)S(1)} %sub.14, pred[2560]{0:T(1024)(128)(4,1)S(1)} %iota_compare_fusion.14), kind=kOutput, calls=%fused_computation.13 | convolution fusion | flops 4708106240 | bytes 3162624 | tf_op jit(solution)/shard_map/dot_general | solution.py:120
  79.6 0.8 collective-permute-start.1
  81.0 1.9 %collective-permute-start.2 = (bf16[64,3,256]{2,1,0:T(4,128)(2,1)S(1)}, bf16[64,3,256]{2,1,0:T(4,128)(2,1)S(1)}, u32[]{:S(2)}, u32[]{:S(2)}) collective-permute-start(bf16[64,3,256]{2,1,0:T(4,128)(2,1)S(1)} %reshape.153), channel_id=1, source_target_pairs={{0,1},{1,2},{2,3},{3,4},{4,5},{5,6},{6,7},{7,8},{8,9},{9,10},{10,1... | collective-permute-start | bytes 294920 | tf_op jit(solution)/shard_map/ppermute | solution.py:18
  82.8 8.2 %convolution_bitcast_fusion = f32[2048,256]{0,1:T(8,128)} fusion(bf16[2560,256]{1,0:T(8,128)(2,1)S(1)} %fusion.11, bf16[2048,2560]{1,0:T(8,128)(2,1)} %bitcast.72), kind=kOutput, calls=%fused_computation.20 | convolution fusion | flops 2684354560 | bytes 13893632 | tf_op jit(solution)/shard_map/dot_general | solution.py:134
  91.1 1.9 %copy.12 = f32[2048,256]{1,0:T(8,128)S(1)} copy(f32[2048,256]{0,1:T(8,128)} %convolution_bitcast_fusion) | data formatting | bytes 4194304 | tf_op jit(solution)/shard_map/dot_general | solution.py:134
  94.6 1.1 %fusion.139 = (bf16[33,1,18,512]{3,2,1,0:T(8,128)(2,1)}, bf16[33,1,18,512]{3,2,1,0:T(8,128)(2,1)S(1)}, bf16[33,1,18,512]{3,2,1,0:T(8,128)(2,1)S(1)}) fusion(bf16[34,2,18,512]{3,2,1,0:T(8,128)(2,1)S(1)} %reshape.156), kind=kLoop, calls=%fused_computation.191 | loop fusion | bytes 3649536 | tf_op jit(solution)/shard_map/slice | solution.py:31
  95.8 2.2 %reshape_squeeze.18 = bf16[594,512]{1,0:T(8,128)(2,1)} reshape(bf16[33,1,18,512]{3,2,1,0:T(8,128)(2,1)} %get-tuple-element.9) | data formatting | bytes 1216512 | tf_op jit(solution)/shard_map/reshape;squeeze | solution.py:39
  98.3 1.6 %fusion.54 = f32[594,512]{1,0:T(8,128)S(1)} fusion(bf16[594,512]{1,0:T(8,128)(2,1)} %reshape_squeeze.18, bf16[256,256]{1,0:T(8,128)(2,1)S(1)} %copy-done.20, bf16[256,256]{1,0:T(8,128)(2,1)} %get-tuple-element.27, bf16[256,256]{1,0:T(8,128)(2,1)S(1)} %copy-done.19), kind=kOutput, calls=%fused_computation.65 | convolution fusion | flops 313524224 | bytes 2217984 | tf_op jit(solution)/shard_map/dot_general | solution.py:39
  (102 shorter events, 9.9 us)
Async XLA Ops:
  5.2 1.9 %copy-start = (pred[4096,1024]{1,0:T(32,128)(4,1)}, pred[4096,1024]{1,0:T(32,128)(4,1)S(1)}, u32[]{:S(2)}) copy-start(pred[4096,1024]{1,0:T(32,128)(4,1)S(1)} %fusion.6) | copy-start | bytes 12582916
  11.1 12.2 %copy-start.1 = (pred[4096,1024]{1,0:T(32,128)(4,1)S(1)}, pred[4096,1024]{1,0:T(32,128)(4,1)}, u32[]{:S(2)}) copy-start(pred[4096,1024]{1,0:T(32,128)(4,1)} %copy-done) | copy-start | bytes 12582916
  27.8 40.6 %all-to-all-start = ((bf16[128,32,256]{2,1,0:T(8,128)(2,1)}), bf16[128,32,256]{2,1,0:T(8,128)(2,1)S(1)}, u32[]{:S(2)}, u32[]{:S(2)}) async-start(bf16[128,32,256]{2,1,0:T(8,128)(2,1)} %bitcast.76), calls=%async_computation | async-start | bytes 4194304 | tf_op jit(solution)/shard_map/all_to_all | solution.py:112
  50.4 2.5 %copy-start.2 = (bf16[3,3,256,256]{3,2,1,0:T(8,128)(2,1)S(1)}, bf16[3,3,256,256]{3,2,1,0:T(8,128)(2,1)}, u32[]{:S(2)}) copy-start(bf16[3,3,256,256]{3,2,1,0:T(8,128)(2,1)} %param.15) | copy-start | bytes 3538948
  70.3 8.8 %slice-start = ((bf16[64,32,2560]{2,1,0:T(8,128)(2,1)}), bf16[3,32,2560]{2,1,0:T(8,128)(2,1)S(1)}, s32[]{:S(2)}) async-start(bf16[64,32,2560]{2,1,0:T(8,128)(2,1)} %param.13), calls=%async_computation.1 | async-start | bytes 983040 | tf_op jit(solution)/shard_map/slice | solution.py:140
  70.3 8.8 %copy-start.3 = (bf16[192,2560]{1,0:T(8,128)(2,1)S(1)}, bf16[192,2560]{1,0:T(8,128)(2,1)}, u32[]{:S(2)}) copy-start(bf16[192,2560]{1,0:T(8,128)(2,1)} %reshape.146) | copy-start | bytes 2949124
  79.6 13.8 %collective-permute-start.1 = (bf16[3,32,256]{2,1,0:T(8,128)(2,1)S(1)}, bf16[3,32,256]{2,1,0:T(8,128)(2,1)S(1)}, u32[]{:S(2)}, u32[]{:S(2)}) collective-permute-start(bf16[3,32,256]{2,1,0:T(8,128)(2,1)S(1)} %bitcast.78), channel_id=1, source_target_pairs={{0,16},{16,32},{32,48},{48,64},{64,80},{80,96},{96,112},{112,0},{1... | collective-permute-start | bytes 147464 | tf_op jit(solution)/shard_map/ppermute | solution.py:18
  80.4 13.0 %collective-permute-start = (bf16[3,3,256]{2,1,0:T(4,128)(2,1)S(1)}, bf16[3,3,256]{2,1,0:T(4,128)(2,1)S(1)}, u32[]{:S(2)}, u32[]{:S(2)}) collective-permute-start(bf16[3,3,256]{2,1,0:T(4,128)(2,1)S(1)} %slice.228), channel_id=1, source_target_pairs={{0,17},{1,18},{2,19},{3,20},{4,21},{5,22},{6,23},{7,24},{8,25},{9,... | collective-permute-start | bytes 13832 | tf_op jit(solution)/shard_map/ppermute | solution.py:18
  81.0 12.4 %collective-permute-start.2 = (bf16[64,3,256]{2,1,0:T(4,128)(2,1)S(1)}, bf16[64,3,256]{2,1,0:T(4,128)(2,1)S(1)}, u32[]{:S(2)}, u32[]{:S(2)}) collective-permute-start(bf16[64,3,256]{2,1,0:T(4,128)(2,1)S(1)} %reshape.153), channel_id=1, source_target_pairs={{0,1},{1,2},{2,3},{3,4},{4,5},{5,6},{6,7},{7,8},{8,9},{9,10},{10,1... | collective-permute-start | bytes 294920 | tf_op jit(solution)/shard_map/ppermute | solution.py:18
  95.8 2.6 %copy-start.19 = (bf16[256,256]{1,0:T(8,128)(2,1)S(1)}, bf16[256,256]{1,0:T(8,128)(2,1)}, u32[]{:S(2)}) copy-start(bf16[256,256]{1,0:T(8,128)(2,1)} %get-tuple-element.21) | copy-start | bytes 393220
  95.8 2.6 %copy-start.20 = (bf16[256,256]{1,0:T(8,128)(2,1)S(1)}, bf16[256,256]{1,0:T(8,128)(2,1)}, u32[]{:S(2)}) copy-start(bf16[256,256]{1,0:T(8,128)(2,1)} %get-tuple-element.26) | copy-start | bytes 393220
  98.1 1.8 %copy-start.16 = (bf16[256,256]{1,0:T(8,128)(2,1)S(1)}, bf16[256,256]{1,0:T(8,128)(2,1)}, u32[]{:S(2)}) copy-start(bf16[256,256]{1,0:T(8,128)(2,1)} %get-tuple-element.23) | copy-start | bytes 393220
  98.1 1.8 %copy-start.17 = (bf16[256,256]{1,0:T(8,128)(2,1)S(1)}, bf16[256,256]{1,0:T(8,128)(2,1)}, u32[]{:S(2)}) copy-start(bf16[256,256]{1,0:T(8,128)(2,1)} %get-tuple-element.24) | copy-start | bytes 393220
  98.1 1.8 %copy-start.18 = (bf16[256,256]{1,0:T(8,128)(2,1)S(1)}, bf16[256,256]{1,0:T(8,128)(2,1)}, u32[]{:S(2)}) copy-start(bf16[256,256]{1,0:T(8,128)(2,1)} %get-tuple-element.25) | copy-start | bytes 393220
  99.9 1.0 copy-start.14
  99.9 1.0 copy-start.15
  102.3 1.0 copy-start.11
  102.3 1.0 copy-start.12
  102.6 1.0 copy-start.7
  102.6 1.0 copy-start.8
  102.6 1.0 copy-start.9
  103.3 0.9 copy-start.4
  103.3 1.0 copy-start.5
  103.3 1.0 copy-start.6
  (2 other events, 1.8 us)

commit v5 on v4

--- a/solution.py
+++ b/solution.py
@@ -89,17 +89,25 @@
         jnp.bfloat16
     )
     key = slot_offsets + 1
-    digits = jnp.stack([key // digit, key % digit], axis=1).astype(jnp.bfloat16)
-    packed_digits = jnp.dot(selector, digits, preferred_element_type=jnp.float32)
-    packed_digits = packed_digits.reshape(peer_count, chunk_rows, 2)[:, :capacity]
-    digit_row = jnp.concatenate(
+    period = obs_count + 2 * capacity
+    key_ext = jnp.concatenate([key, jnp.zeros((period - obs_count,), jnp.int32)])
+    tiled_keys = jnp.tile(key_ext, capacity + 1)[: capacity * (period + 1)]
+    hankel = tiled_keys.reshape(capacity, period + 1)[:, :obs_count].T
+    windows = jnp.concatenate(
         [
-            packed_digits[:, :, 0],
-            packed_digits[:, :, 1],
-            jnp.zeros((peer_count, channel_count - 2 * capacity), jnp.float32),
+            hankel // digit,
+            hankel % digit,
+            jnp.zeros((obs_count, channel_count - 2 * capacity), jnp.int32),
         ],
         axis=1,
     ).astype(jnp.bfloat16)
+    run_head = (run_starts[:, None] == row_index[None, :]).astype(jnp.bfloat16)
+    digit_row = jnp.dot(run_head, windows, preferred_element_type=jnp.float32)
+    column = jnp.arange(channel_count, dtype=jnp.int32)
+    digit_live = (column[None, :] % capacity < run_counts[:, None]) & (
+        column[None, :] < 2 * capacity
+    )
+    digit_row = jnp.where(digit_live, digit_row, 0.0).astype(jnp.bfloat16)
     chunk_of = jnp.repeat(targets, chunk_rows)
     row_of = jnp.tile(within, peer_count)
     digit_pick = (row_of[:, None] == capacity) & (chunk_of[:, None] == targets[None, :])
@@ -130,9 +138,8 @@
     weights_cells = setconv_weights
 
     def cells(weights, roots):
-        shape = weights.shape[:-1]
-        numer = jnp.dot(weights.reshape(-1, slot_count), obs_masked, preferred_element_type=jnp.float32)
-        return (numer.reshape(shape + (channel_count,)) / roots).astype(jnp.bfloat16)
+        numer = jnp.dot(weights, obs_masked, preferred_element_type=jnp.float32)
+        return (numer / roots).astype(jnp.bfloat16)
 
     rim = 3
     rim_weights = jnp.concatenate(
@@ -149,7 +156,7 @@
     north = cyclic(north_rows, ("lat",), (1,))
     west = cyclic(west_cols, ("lon",), (1,))
     north_west = cyclic(north_rows[:, -rim:], ("lat", "lon"), (1, 1))
-    grid = cells(weights_cells, root)
+    grid = cells(weights_flat, root.reshape(-1, 1)).reshape(tile_rows, tile_cols, channel_count)
     return encode_tile(grid, north, west, north_west, conv1_weight, conv2_weight)
 
 

time: 107 us -> 97.1 us (0.907)
  matrix products: 39.6 us -> 33.1 us
  local copies, waits for them, and re-layouts: 20.2 us -> 18.5 us
    dot_general x1, matrix products: 12.1 us -> 8.82 us  [body(): jnp.dot(radiances, project_weight, preferred_element_type=jnp.float32)]
    dot_general x3, matrix products: 11.1 us -> 8.3 us  [the longest x2 7.87 us: cells(): numer = jnp.dot(weights, obs_masked, preferred_element_type=jnp.float32)]
    dot_general x1 -> x0, local copies, waits for them, and re-layouts: 1.92 us -> none  [cells(): jnp.dot(weights.reshape(-1, slot_count), obs_masked, preferred_element_ty...]
    unnamed x43 -> x49, local copies, waits for them, and re-layouts: 3.5 us -> 1.98 us
where the time goes in v5:
time: 97.1 us; the launch traced here: 95.7 us
  matrix products  33.1 us (34%)
  local copies, waits for them, and re-layouts  18.5 us (19%)
  other arithmetic  14.5 us (15%)
  starting transfers between devices  14.2 us (15%)
  waiting for transfers between devices  13.9 us (14%)
  between operations  1.33 us (1%)
    all_to_all x1, waiting for transfers between devices, body(): lax.all_to_all(outgoing, ('lat', 'lon'), split_axis=0, concat_axis=0, til...  13.9 us
    all_to_all x1, starting transfers between devices, body(): lax.all_to_all(outgoing, ('lat', 'lon'), split_axis=0, concat_axis=0, til...  11.2 us
    dot_general x1, matrix products, body(): jnp.dot(radiances, project_weight, preferred_element_type=jnp.float32)  8.82 us
    dot_general x1, matrix products, body(): jnp.dot(slot_table, arrived_rows, preferred_element_type=jnp.float32)  8.75 us
    dot_general x2, matrix products, cells(): numer = jnp.dot(weights, obs_masked, preferred_element_type=jnp.float32)  7.87 us
    reduce_sum x1, other arithmetic, body(): density = jnp.sum(masked, axis=1, dtype=jnp.float32)  6.28 us
    dot_general x1, matrix products, body(): jnp.dot(selector_all, sources, preferred_element_type=jnp.float32)  4.04 us
    squeeze x2, local copies, waits for them, and re-layouts, strided_valid(): kernel[row_tap, 0]  3.42 us
  transfers between devices with their start and end apart: 4, of which 1 were waited for; matrix products, arithmetic and copies ran while one was open for 24% of the time, Pallas kernels for 0%

profile of v5, /device:TPU:0, one launch (start us, length us, event | category | flops | bytes accessed | tf_op | source)
XLA Modules:
  0.0 95.7 jit_solution(5771389941037984623)
XLA Ops:
  0.1 0.7 broadcast_add_fusion
  2.5 3.1 %fusion.6 = pred[4096,1024]{1,0:T(32,128)(4,1)S(1)} fusion(s32[4096]{0:T(1024)S(1)} %add.117, pred[4096]{0:T(1024)(128)(4,1)S(1)} %and.61), kind=kLoop, calls=%fused_computation.9 | loop fusion | flops 8388608 | bytes 4214784 | tf_op jit(solution)/shard_map/and | solution.py:86
  5.6 1.4 %fusion.18 = pred[4096,128]{1,0:T(32,128)(4,1)S(1)} fusion(s32[4096]{0:T(1024)S(1)} %eq.99, pred[4096]{0:T(1024)(128)(4,1)S(1)} %eq.98), kind=kLoop, calls=%fused_computation.23 | loop fusion | flops 1048576 | bytes 544768 | tf_op jit(solution)/shard_map/and | solution.py:113
  7.0 8.8 %convolution_convert_fusion = bf16[1024,256]{1,0:T(8,128)(2,1)S(1)} fusion(bf16[1024,8461]{0,1:T(8,128)(2,1)} %param.8, bf16[8461,256]{1,0:T(8,128)(2,1)S(1)} %copy-done.22), kind=kOutput, calls=%fused_computation.33 | convolution fusion | flops 4436262912 | bytes 22184448 | tf_op jit(solution)/shard_map/dot_general | solution.py:88
  16.3 4.0 %fusion.7 = bf16[4096,256]{1,0:T(8,128)(2,1)} fusion(pred[4096,128]{1,0:T(32,128)(4,1)S(1)} %fusion.18, pred[4096,1024]{1,0:T(32,128)(4,1)S(1)} %fusion.6, bf16[128,256]{1,0:T(8,128)(2,1)S(1)} %fusion.34, bf16[1024,256]{1,0:T(8,128)(2,1)S(1)} %convolution_convert_fusion), kind=kOutput, calls=%fused_computation.10 | convolution fusion | flops 2422865920 | bytes 7405568 | tf_op jit(solution)/shard_map/dot_general | solution.py:116
  20.3 11.2 %all-to-all-start = ((bf16[128,32,256]{2,1,0:T(8,128)(2,1)}), bf16[128,32,256]{2,1,0:T(8,128)(2,1)S(1)}, u32[]{:S(2)}, u32[]{:S(2)}) async-start(bf16[128,32,256]{2,1,0:T(8,128)(2,1)} %bitcast.90), calls=%async_computation | async-start | bytes 4194304 | tf_op jit(solution)/shard_map/all_to_all | solution.py:120
  31.5 2.4 %slice.162 = bf16[64,3,2560]{2,1,0:T(4,128)(2,1)S(1)} slice(bf16[64,32,2560]{2,1,0:T(8,128)(2,1)} %param.13), slice={[0:64], [29:32], [0:2560]} | slice | bytes 1966080 | tf_op jit(solution)/shard_map/slice | solution.py:148
  34.6 6.3 %convert_reduce_fusion = f32[64,32]{1,0:T(8,128)S(1)} fusion(bf16[64,32,2560]{2,1,0:T(8,128)(2,1)} %param.13, pred[2560]{0:T(1024)(128)(4,1)S(1)} %iota_compare_fusion.16), kind=kLoop, calls=%fused_computation.2 | loop fusion | flops 15726592 | bytes 10496512 | tf_op jit(solution)/shard_map/reduce_sum | solution.py:136
  40.9 0.7 sqrt.22
  41.9 1.6 %reshape.172 = bf16[192,2560]{1,0:T(8,128)(2,1)} reshape(bf16[64,3,2560]{2,1,0:T(4,128)(2,1)S(1)} %slice.162) | data formatting | bytes 1966080 | tf_op jit(solution)/shard_map/reshape | solution.py:148
  43.6 2.5 %slice_bitcast_fusion.18 = (bf16[256,256]{1,0:T(8,128)(2,1)}, bf16[256,256]{1,0:T(8,128)(2,1)}, bf16[256,256]{1,0:T(8,128)(2,1)}, bf16[256,256]{1,0:T(8,128)(2,1...) fusion(bf16[3,3,256,256]{3,2,1,0:T(8,128)(2,1)} %param.14), kind=kLoop, calls=%fused_computation.153 | loop fusion | bytes 2359296 | tf_op jit(solution)/shard_map/squeeze | solution.py:34
  46.1 1.0 %slice_bitcast_fusion.9 = (bf16[256,256]{1,0:T(8,128)(2,1)}, bf16[256,256]{1,0:T(8,128)(2,1)S(1)}, bf16[256,256]{1,0:T(8,128)(2,1)}, bf16[256,256]{1,0:T(8,128)(...) fusion(bf16[3,3,256,256]{3,2,1,0:T(8,128)(2,1)S(1)} %copy-done), kind=kLoop, calls=%fused_computation.144 | loop fusion | bytes 2359296 | tf_op jit(solution)/shard_map/squeeze | solution.py:34
  47.1 13.9 %all-to-all-done = bf16[128,32,256]{2,1,0:T(8,128)(2,1)S(1)} async-done(((bf16[128,32,256]{2,1,0:T(8,128)(2,1)}), bf16[128,32,256]{2,1,0:T(8,128)(2,1)S(1)}, u32[]{:S(2)}, u32[]{:S(2)}) %all-to-all-start) | async-done | bytes 2097184 | tf_op jit(solution)/shard_map/all_to_all | solution.py:120
  61.0 1.4 %reshape.175 = bf16[3584,256]{1,0:T(8,128)(2,1)} reshape(bf16[128,28,256]{2,1,0:T(8,128)(2,1)S(1)} %bitcast.88) | data formatting | bytes 3670016 | tf_op jit(solution)/shard_map/reshape | solution.py:121
  62.9 8.7 %fusion.11 = bf16[2560,256]{1,0:T(8,128)(2,1)S(1)} fusion(bf16[3584,256]{1,0:T(8,128)(2,1)} %reshape.175, s32[3584]{0:T(1024)S(1)} %sub.14, pred[2560]{0:T(1024)(128)(4,1)S(1)} %copy-done.19), kind=kOutput, calls=%fused_computation.12 | convolution fusion | flops 4708106240 | bytes 3162624 | tf_op jit(solution)/shard_map/dot_general | solution.py:128
  71.7 0.5 fusion.31
  72.7 0.7 collective-permute-start.1
  74.0 1.9 %collective-permute-start.2 = (bf16[64,3,256]{2,1,0:T(4,128)(2,1)S(1)}, bf16[64,3,256]{2,1,0:T(4,128)(2,1)S(1)}, u32[]{:S(2)}, u32[]{:S(2)}) collective-permute-start(bf16[64,3,256]{2,1,0:T(4,128)(2,1)S(1)} %reshape.179), channel_id=1, source_target_pairs={{0,1},{1,2},{2,3},{3,4},{4,5},{5,6},{6,7},{7,8},{8,9},{9,10},{10,1... | collective-permute-start | bytes 294920 | tf_op jit(solution)/shard_map/ppermute | solution.py:18
  75.9 7.3 %fusion.17 = bf16[2048,256]{0,1:T(8,128)(2,1)S(1)} fusion(bf16[2560,256]{1,0:T(8,128)(2,1)} %copy-done.23, bf16[2048,2560]{1,0:T(8,128)(2,1)} %bitcast.86, f32[2048]{0:T(1024)S(1)} %copy-done.20), kind=kOutput, calls=%fused_computation.21 | convolution fusion | flops 2685403136 | bytes 12853248 | tf_op jit(solution)/shard_map/dot_general | solution.py:141
  83.8 0.7 fusion.26
  85.0 1.1 %fusion.143 = (bf16[33,1,18,512]{3,2,1,0:T(8,128)(2,1)}, bf16[33,1,18,512]{3,2,1,0:T(8,128)(2,1)S(1)}, bf16[33,1,18,512]{3,2,1,0:T(8,128)(2,1)S(1)}) fusion(bf16[34,2,18,512]{3,2,1,0:T(8,128)(2,1)S(1)} %reshape.182), kind=kLoop, calls=%fused_computation.195 | loop fusion | bytes 3649536 | tf_op jit(solution)/shard_map/slice | solution.py:31
  86.1 2.2 %reshape_squeeze.18 = bf16[594,512]{1,0:T(8,128)(2,1)} reshape(bf16[33,1,18,512]{3,2,1,0:T(8,128)(2,1)} %get-tuple-element.11) | data formatting | bytes 1216512 | tf_op jit(solution)/shard_map/reshape;squeeze | solution.py:39
  88.7 1.6 %fusion.53 = f32[594,512]{1,0:T(8,128)S(1)} fusion(bf16[594,512]{1,0:T(8,128)(2,1)} %reshape_squeeze.18, bf16[256,256]{1,0:T(8,128)(2,1)S(1)} %copy-done.16, bf16[256,256]{1,0:T(8,128)(2,1)S(1)} %copy-done.17, bf16[256,256]{1,0:T(8,128)(2,1)S(1)} %copy-done.15), kind=kOutput, calls=%fused_computation.63 | convolution fusion | flops 313524224 | bytes 2217984 | tf_op jit(solution)/shard_map/dot_general | solution.py:39
  95.0 0.7 fusion.114
  (116 shorter events, 10.0 us)
Async XLA Ops:
  0.0 1.6 %copy-start.21 = (s32[1024]{0:T(1024)S(1)}, s32[1024]{0:T(1024)}, u32[]{:S(2)}) copy-start(s32[1024]{0:T(1024)} %param.10) | copy-start | bytes 12292
  2.5 4.5 %copy-start.22 = (bf16[8461,256]{1,0:T(8,128)(2,1)S(1)}, bf16[8461,256]{1,0:T(8,128)(2,1)}, u32[]{:S(2)}) copy-start(bf16[8461,256]{1,0:T(8,128)(2,1)} %param.9) | copy-start | bytes 12996100
  20.3 40.6 %all-to-all-start = ((bf16[128,32,256]{2,1,0:T(8,128)(2,1)}), bf16[128,32,256]{2,1,0:T(8,128)(2,1)S(1)}, u32[]{:S(2)}, u32[]{:S(2)}) async-start(bf16[128,32,256]{2,1,0:T(8,128)(2,1)} %bitcast.90), calls=%async_computation | async-start | bytes 4194304 | tf_op jit(solution)/shard_map/all_to_all | solution.py:120
  34.6 6.3 %copy-start.18 = (pred[2560]{0:T(1024)(128)(4,1)}, pred[2560]{0:T(1024)(128)(4,1)S(1)}, u32[]{:S(2)}) copy-start(pred[2560]{0:T(1024)(128)(4,1)S(1)} %iota_compare_fusion.16) | copy-start | bytes 7684
  43.5 2.5 %copy-start = (bf16[3,3,256,256]{3,2,1,0:T(8,128)(2,1)S(1)}, bf16[3,3,256,256]{3,2,1,0:T(8,128)(2,1)}, u32[]{:S(2)}) copy-start(bf16[3,3,256,256]{3,2,1,0:T(8,128)(2,1)} %param.15) | copy-start | bytes 3538948
  61.0 1.9 %copy-start.19 = (pred[2560]{0:T(1024)(128)(4,1)S(1)}, pred[2560]{0:T(1024)(128)(4,1)}, u32[]{:S(2)}) copy-start(pred[2560]{0:T(1024)(128)(4,1)} %copy-done.18) | copy-start | bytes 7684
  62.9 8.8 %slice-start = ((bf16[64,32,2560]{2,1,0:T(8,128)(2,1)}), bf16[3,32,2560]{2,1,0:T(8,128)(2,1)S(1)}, s32[]{:S(2)}) async-start(bf16[64,32,2560]{2,1,0:T(8,128)(2,1)} %param.13), calls=%async_computation.1 | async-start | bytes 983040 | tf_op jit(solution)/shard_map/slice | solution.py:147
  62.9 8.8 %copy-start.1 = (bf16[192,2560]{1,0:T(8,128)(2,1)S(1)}, bf16[192,2560]{1,0:T(8,128)(2,1)}, u32[]{:S(2)}) copy-start(bf16[192,2560]{1,0:T(8,128)(2,1)} %reshape.172) | copy-start | bytes 2949124
  71.6 1.1 %copy-start.23 = (bf16[2560,256]{1,0:T(8,128)(2,1)}, bf16[2560,256]{1,0:T(8,128)(2,1)S(1)}, u32[]{:S(2)}) copy-start(bf16[2560,256]{1,0:T(8,128)(2,1)S(1)} %fusion.11) | copy-start | bytes 3932164
  71.7 4.2 %copy-start.20 = (f32[2048]{0:T(1024)S(1)}, f32[2048]{0:T(1024)}, u32[]{:S(2)}) copy-start(f32[2048]{0:T(1024)} %sqrt.22) | copy-start | bytes 24580
  72.7 11.0 %collective-permute-start.1 = (bf16[3,32,256]{2,1,0:T(8,128)(2,1)S(1)}, bf16[3,32,256]{2,1,0:T(8,128)(2,1)S(1)}, u32[]{:S(2)}, u32[]{:S(2)}) collective-permute-start(bf16[3,32,256]{2,1,0:T(8,128)(2,1)S(1)} %bitcast.92), channel_id=1, source_target_pairs={{0,16},{16,32},{32,48},{48,64},{64,80},{80,96},{96,112},{112,0},{1... | collective-permute-start | bytes 147464 | tf_op jit(solution)/shard_map/ppermute | solution.py:18
  73.4 10.3 %collective-permute-start = (bf16[3,3,256]{2,1,0:T(4,128)(2,1)S(1)}, bf16[3,3,256]{2,1,0:T(4,128)(2,1)S(1)}, u32[]{:S(2)}, u32[]{:S(2)}) collective-permute-start(bf16[3,3,256]{2,1,0:T(4,128)(2,1)S(1)} %slice.223), channel_id=1, source_target_pairs={{0,17},{1,18},{2,19},{3,20},{4,21},{5,22},{6,23},{7,24},{8,25},{9,... | collective-permute-start | bytes 13832 | tf_op jit(solution)/shard_map/ppermute | solution.py:18
  74.0 9.8 %collective-permute-start.2 = (bf16[64,3,256]{2,1,0:T(4,128)(2,1)S(1)}, bf16[64,3,256]{2,1,0:T(4,128)(2,1)S(1)}, u32[]{:S(2)}, u32[]{:S(2)}) collective-permute-start(bf16[64,3,256]{2,1,0:T(4,128)(2,1)S(1)} %reshape.179), channel_id=1, source_target_pairs={{0,1},{1,2},{2,3},{3,4},{4,5},{5,6},{6,7},{7,8},{8,9},{9,10},{10,1... | collective-permute-start | bytes 294920 | tf_op jit(solution)/shard_map/ppermute | solution.py:18
  86.1 2.6 %copy-start.15 = (bf16[256,256]{1,0:T(8,128)(2,1)S(1)}, bf16[256,256]{1,0:T(8,128)(2,1)}, u32[]{:S(2)}) copy-start(bf16[256,256]{1,0:T(8,128)(2,1)} %get-tuple-element.23) | copy-start | bytes 393220
  86.1 2.6 %copy-start.16 = (bf16[256,256]{1,0:T(8,128)(2,1)S(1)}, bf16[256,256]{1,0:T(8,128)(2,1)}, u32[]{:S(2)}) copy-start(bf16[256,256]{1,0:T(8,128)(2,1)} %get-tuple-element.28) | copy-start | bytes 393220
  86.1 2.6 %copy-start.17 = (bf16[256,256]{1,0:T(8,128)(2,1)S(1)}, bf16[256,256]{1,0:T(8,128)(2,1)}, u32[]{:S(2)}) copy-start(bf16[256,256]{1,0:T(8,128)(2,1)} %get-tuple-element.29) | copy-start | bytes 393220
  88.5 1.8 %copy-start.12 = (bf16[256,256]{1,0:T(8,128)(2,1)S(1)}, bf16[256,256]{1,0:T(8,128)(2,1)}, u32[]{:S(2)}) copy-start(bf16[256,256]{1,0:T(8,128)(2,1)} %get-tuple-element.25) | copy-start | bytes 393220
  88.5 1.8 %copy-start.13 = (bf16[256,256]{1,0:T(8,128)(2,1)S(1)}, bf16[256,256]{1,0:T(8,128)(2,1)}, u32[]{:S(2)}) copy-start(bf16[256,256]{1,0:T(8,128)(2,1)} %get-tuple-element.26) | copy-start | bytes 393220
  88.5 1.8 %copy-start.14 = (bf16[256,256]{1,0:T(8,128)(2,1)S(1)}, bf16[256,256]{1,0:T(8,128)(2,1)}, u32[]{:S(2)}) copy-start(bf16[256,256]{1,0:T(8,128)(2,1)} %get-tuple-element.27) | copy-start | bytes 393220
  90.3 1.0 %copy-start.11 = (bf16[256,256]{1,0:T(8,128)(2,1)S(1)}, bf16[256,256]{1,0:T(8,128)(2,1)}, u32[]{:S(2)}) copy-start(bf16[256,256]{1,0:T(8,128)(2,1)} %get-tuple-element.31) | copy-start | bytes 393220
  92.7 1.0 %copy-start.8 = (bf16[256,256]{1,0:T(8,128)(2,1)S(1)}, bf16[256,256]{1,0:T(8,128)(2,1)}, u32[]{:S(2)}) copy-start(bf16[256,256]{1,0:T(8,128)(2,1)} %get-tuple-element.20) | copy-start | bytes 393220
  92.9 1.0 %copy-start.3 = (bf16[256,256]{1,0:T(8,128)(2,1)S(1)}, bf16[256,256]{1,0:T(8,128)(2,1)}, u32[]{:S(2)}) copy-start(bf16[256,256]{1,0:T(8,128)(2,1)} %get-tuple-element.16) | copy-start | bytes 393220
  93.0 1.0 %copy-start.4 = (bf16[256,256]{1,0:T(8,128)(2,1)S(1)}, bf16[256,256]{1,0:T(8,128)(2,1)}, u32[]{:S(2)}) copy-start(bf16[256,256]{1,0:T(8,128)(2,1)} %get-tuple-element.17) | copy-start | bytes 393220
  93.0 1.0 %copy-start.5 = (bf16[256,256]{1,0:T(8,128)(2,1)S(1)}, bf16[256,256]{1,0:T(8,128)(2,1)}, u32[]{:S(2)}) copy-start(bf16[256,256]{1,0:T(8,128)(2,1)} %get-tuple-element.18) | copy-start | bytes 393220
  (5 other events, 4.7 us)

commit v6 on v5

--- a/solution.py
+++ b/solution.py
@@ -108,15 +108,11 @@
         column[None, :] < 2 * capacity
     )
     digit_row = jnp.where(digit_live, digit_row, 0.0).astype(jnp.bfloat16)
-    chunk_of = jnp.repeat(targets, chunk_rows)
-    row_of = jnp.tile(within, peer_count)
-    digit_pick = (row_of[:, None] == capacity) & (chunk_of[:, None] == targets[None, :])
-    selector_all = jnp.concatenate([selector, digit_pick.astype(jnp.bfloat16)], axis=1)
-    sources = jnp.concatenate([payload, digit_row], axis=0)
-    outgoing = jnp.dot(selector_all, sources, preferred_element_type=jnp.float32).astype(
-        jnp.bfloat16
+    packed = jnp.dot(selector, payload, preferred_element_type=jnp.float32).astype(jnp.bfloat16)
+    packed = packed.reshape(peer_count, chunk_rows, channel_count)
+    outgoing = jnp.where(
+        (within == capacity)[None, :, None], digit_row[:, None, :], packed
     )
-    outgoing = outgoing.reshape(peer_count, chunk_rows, channel_count)
     arrived = lax.all_to_all(outgoing, ("lat", "lon"), split_axis=0, concat_axis=0, tiled=True)
     arrived_rows = arrived[:, :capacity].reshape(-1, channel_count)
     arrived_digits = arrived[:, capacity].astype(jnp.int32)

time: 97.1 us -> 98.8 us (1.018)
  matrix products: 33.1 us -> 37.2 us
  other arithmetic: 14.5 us -> 12.2 us
    and x2 -> x0, other arithmetic: 4.52 us -> none  [the longest x1 3.13 us: body(): (source_rows[:, None] == row_index[None, :]) & valid_slot[:, None]]
    dot_general x1, matrix products: 8.82 us -> 12 us  [body(): jnp.dot(radiances, project_weight, preferred_element_type=jnp.float32)]
    select_n x0 -> x1, other arithmetic: none -> 1.55 us  [body(): jnp.where((within == capacity)[None, :, None], digit_row[:, None, :], pac...]
    unnamed x49 -> x45, local copies, waits for them, and re-layouts: 1.98 us -> 1.97 us
  transfers between devices with their start and end apart: 4 -> 4, of which waited for: 1 -> 1; matrix products, arithmetic and copies ran while one was open for 24% -> 23% of each run, Pallas kernels for 0% -> 0%
where the time goes in v6:
time: 98.8 us; the launch traced here: 97.3 us
  matrix products  37.2 us (38%)
  local copies, waits for them, and re-layouts  18.3 us (19%)
  starting transfers between devices  14.5 us (15%)
  waiting for transfers between devices  13.8 us (14%)
  other arithmetic  12.2 us (12%)
  between operations  1.28 us (1%)
    all_to_all x1, waiting for transfers between devices, body(): lax.all_to_all(outgoing, ('lat', 'lon'), split_axis=0, concat_axis=0, til...  13.7 us
    dot_general x1, matrix products, body(): jnp.dot(radiances, project_weight, preferred_element_type=jnp.float32)  12 us
    all_to_all x1, starting transfers between devices, body(): lax.all_to_all(outgoing, ('lat', 'lon'), split_axis=0, concat_axis=0, til...  11.4 us
    dot_general x1, matrix products, body(): jnp.dot(slot_table, arrived_rows, preferred_element_type=jnp.float32)  8.74 us
    dot_general x2, matrix products, cells(): numer = jnp.dot(weights, obs_masked, preferred_element_type=jnp.float32)  7.87 us
    reduce_sum x1, other arithmetic, body(): density = jnp.sum(masked, axis=1, dtype=jnp.float32)  6.28 us
    dot_general x1, matrix products, body(): jnp.dot(selector, payload, preferred_element_type=jnp.float32)  5 us
    squeeze x2, local copies, waits for them, and re-layouts, strided_valid(): kernel[row_tap, 0]  3.43 us
  transfers between devices with their start and end apart: 4, of which 1 were waited for; matrix products, arithmetic and copies ran while one was open for 23% of the time, Pallas kernels for 0%

profile of v6, /device:TPU:0, one launch (start us, length us, event | category | flops | bytes accessed | tf_op | source)
XLA Modules:
  0.0 97.3 jit_solution(10418039402653593553)
XLA Ops:
  0.0 0.7 broadcast_add_fusion
  1.6 0.9 convert_reduce_fusion.1
  3.0 12.0 %fusion.175 = bf16[1024,256]{1,0:T(8,128)(2,1)S(1)} fusion(bf16[8461,256]{1,0:T(8,128)(2,1)} %param.9, bf16[1024,8461]{0,1:T(8,128)(2,1)} %param.8), kind=kOutput, calls=%bitcast_fusion.8.clone.2 | convolution fusion | flops 4436262912 | bytes 22184448 | tf_op jit(solution)/shard_map/dot_general | solution.py:88
  14.9 5.0 %fusion.7 = bf16[4096,256]{1,0:T(8,128)(2,1)S(1)} fusion(s32[4096]{0:T(1024)S(1)} %add.119, pred[4096]{0:T(1024)(128)(4,1)S(1)} %and.58, bf16[1024,256]{1,0:T(8,128)(2,1)S(1)} %fusion.175), kind=kOutput, calls=%fused_computation.9 | convolution fusion | flops 2156920832 | bytes 2641920 | tf_op jit(solution)/shard_map/dot_general | solution.py:111
  20.4 1.6 %broadcast_select_fusion = bf16[128,32,256]{2,1,0:T(8,128)(2,1)} fusion(bf16[128,32,256]{2,1,0:T(8,128)(2,1)S(1)} %bitcast.112, pred[32]{0:T(512)(128)(4,1)S(1)} %iota_compare_fusion.17, bf16[128,256]{1,0:T(8,128)(2,1)S(1)} %fusion.33), kind=kLoop, calls=%fused_computation.21 | loop fusion | flops 1048576 | bytes 4259872 | tf_op jit(solution)/shard_map/jit(_where)/select_n | solution.py:113
  21.9 11.4 %all-to-all-start = ((bf16[128,32,256]{2,1,0:T(8,128)(2,1)}), bf16[128,32,256]{2,1,0:T(8,128)(2,1)S(1)}, u32[]{:S(2)}, u32[]{:S(2)}) async-start(bf16[128,32,256]{2,1,0:T(8,128)(2,1)} %broadcast_select_fusion), calls=%async_computation | async-start | bytes 4194304 | tf_op jit(solution)/shard_map/all_to_all | solution.py:116
  33.3 2.4 %slice.162 = bf16[64,3,2560]{2,1,0:T(4,128)(2,1)S(1)} slice(bf16[64,32,2560]{2,1,0:T(8,128)(2,1)} %param.13), slice={[0:64], [29:32], [0:2560]} | slice | bytes 1966080 | tf_op jit(solution)/shard_map/slice | solution.py:144
  36.4 6.3 %convert_reduce_fusion = f32[64,32]{1,0:T(8,128)S(1)} fusion(bf16[64,32,2560]{2,1,0:T(8,128)(2,1)} %param.13, pred[2560]{0:T(1024)(128)(4,1)S(1)} %iota_compare_fusion.14), kind=kLoop, calls=%fused_computation.2 | loop fusion | flops 15726592 | bytes 10496512 | tf_op jit(solution)/shard_map/reduce_sum | solution.py:132
  42.7 0.7 sqrt.22
  43.7 1.6 %reshape.167 = bf16[192,2560]{1,0:T(8,128)(2,1)} reshape(bf16[64,3,2560]{2,1,0:T(4,128)(2,1)S(1)} %slice.162) | data formatting | bytes 1966080 | tf_op jit(solution)/shard_map/reshape | solution.py:144
  45.4 2.5 %slice_bitcast_fusion.18 = (bf16[256,256]{1,0:T(8,128)(2,1)}, bf16[256,256]{1,0:T(8,128)(2,1)}, bf16[256,256]{1,0:T(8,128)(2,1)}, bf16[256,256]{1,0:T(8,128)(2,1...) fusion(bf16[3,3,256,256]{3,2,1,0:T(8,128)(2,1)} %param.14), kind=kLoop, calls=%fused_computation.148 | loop fusion | bytes 2359296 | tf_op jit(solution)/shard_map/squeeze | solution.py:34
  47.9 1.0 slice_bitcast_fusion.9
  48.8 13.7 %all-to-all-done = bf16[128,32,256]{2,1,0:T(8,128)(2,1)S(1)} async-done(((bf16[128,32,256]{2,1,0:T(8,128)(2,1)}), bf16[128,32,256]{2,1,0:T(8,128)(2,1)S(1)}, u32[]{:S(2)}, u32[]{:S(2)}) %all-to-all-start) | async-done | bytes 2097184 | tf_op jit(solution)/shard_map/all_to_all | solution.py:116
  62.6 1.4 %reshape.170 = bf16[3584,256]{1,0:T(8,128)(2,1)} reshape(bf16[128,28,256]{2,1,0:T(8,128)(2,1)S(1)} %bitcast.110) | data formatting | bytes 3670016 | tf_op jit(solution)/shard_map/reshape | solution.py:117
  64.5 8.7 %fusion.11 = bf16[2560,256]{1,0:T(8,128)(2,1)S(1)} fusion(bf16[3584,256]{1,0:T(8,128)(2,1)} %reshape.170, s32[3584]{0:T(1024)S(1)} %sub.14, pred[2560]{0:T(1024)(128)(4,1)S(1)} %copy-done.19), kind=kOutput, calls=%fused_computation.11 | convolution fusion | flops 4708106240 | bytes 3162624 | tf_op jit(solution)/shard_map/dot_general | solution.py:124
  74.3 0.7 collective-permute-start.1
  75.0 0.5 collective-permute-start
  75.6 1.9 %collective-permute-start.2 = (bf16[64,3,256]{2,1,0:T(4,128)(2,1)S(1)}, bf16[64,3,256]{2,1,0:T(4,128)(2,1)S(1)}, u32[]{:S(2)}, u32[]{:S(2)}) collective-permute-start(bf16[64,3,256]{2,1,0:T(4,128)(2,1)S(1)} %reshape.174), channel_id=1, source_target_pairs={{0,1},{1,2},{2,3},{3,4},{4,5},{5,6},{6,7},{7,8},{8,9},{9,10},{10,1... | collective-permute-start | bytes 294920 | tf_op jit(solution)/shard_map/ppermute | solution.py:18
  77.5 7.3 %fusion.17 = bf16[2048,256]{0,1:T(8,128)(2,1)S(1)} fusion(bf16[2560,256]{1,0:T(8,128)(2,1)} %copy-done.21, bf16[2048,2560]{1,0:T(8,128)(2,1)} %bitcast.108, f32[2048]{0:T(1024)S(1)} %copy-done.20), kind=kOutput, calls=%fused_computation.20 | convolution fusion | flops 2685403136 | bytes 12853248 | tf_op jit(solution)/shard_map/dot_general | solution.py:137
  85.4 0.7 fusion.25
  86.6 1.1 %fusion.137 = (bf16[33,1,18,512]{3,2,1,0:T(8,128)(2,1)}, bf16[33,1,18,512]{3,2,1,0:T(8,128)(2,1)S(1)}, bf16[33,1,18,512]{3,2,1,0:T(8,128)(2,1)S(1)}) fusion(bf16[34,2,18,512]{3,2,1,0:T(8,128)(2,1)S(1)} %reshape.177), kind=kLoop, calls=%fused_computation.188 | loop fusion | bytes 3649536 | tf_op jit(solution)/shard_map/slice | solution.py:31
  87.7 2.2 %reshape_squeeze.18 = bf16[594,512]{1,0:T(8,128)(2,1)} reshape(bf16[33,1,18,512]{3,2,1,0:T(8,128)(2,1)} %get-tuple-element.11) | data formatting | bytes 1216512 | tf_op jit(solution)/shard_map/reshape;squeeze | solution.py:39
  90.3 1.6 %fusion.49 = f32[594,512]{1,0:T(8,128)S(1)} fusion(bf16[594,512]{1,0:T(8,128)(2,1)} %reshape_squeeze.18, bf16[256,256]{1,0:T(8,128)(2,1)S(1)} %copy-done.16, bf16[256,256]{1,0:T(8,128)(2,1)S(1)} %copy-done.17, bf16[256,256]{1,0:T(8,128)(2,1)S(1)} %copy-done.15), kind=kOutput, calls=%fused_computation.58 | convolution fusion | flops 313524224 | bytes 2217984 | tf_op jit(solution)/shard_map/dot_general | solution.py:39
  96.6 0.7 fusion.110
  (108 shorter events, 9.6 us)
Async XLA Ops:
  21.9 40.7 %all-to-all-start = ((bf16[128,32,256]{2,1,0:T(8,128)(2,1)}), bf16[128,32,256]{2,1,0:T(8,128)(2,1)S(1)}, u32[]{:S(2)}, u32[]{:S(2)}) async-start(bf16[128,32,256]{2,1,0:T(8,128)(2,1)} %broadcast_select_fusion), calls=%async_computation | async-start | bytes 4194304 | tf_op jit(solution)/shard_map/all_to_all | solution.py:116
  36.4 6.3 %copy-start.18 = (pred[2560]{0:T(1024)(128)(4,1)}, pred[2560]{0:T(1024)(128)(4,1)S(1)}, u32[]{:S(2)}) copy-start(pred[2560]{0:T(1024)(128)(4,1)S(1)} %iota_compare_fusion.14) | copy-start | bytes 7684
  45.3 2.6 %copy-start = (bf16[3,3,256,256]{3,2,1,0:T(8,128)(2,1)S(1)}, bf16[3,3,256,256]{3,2,1,0:T(8,128)(2,1)}, u32[]{:S(2)}) copy-start(bf16[3,3,256,256]{3,2,1,0:T(8,128)(2,1)} %param.15) | copy-start | bytes 3538948
  62.6 1.9 %copy-start.19 = (pred[2560]{0:T(1024)(128)(4,1)S(1)}, pred[2560]{0:T(1024)(128)(4,1)}, u32[]{:S(2)}) copy-start(pred[2560]{0:T(1024)(128)(4,1)} %copy-done.18) | copy-start | bytes 7684
  64.5 8.8 %slice-start = ((bf16[64,32,2560]{2,1,0:T(8,128)(2,1)}), bf16[3,32,2560]{2,1,0:T(8,128)(2,1)S(1)}, s32[]{:S(2)}) async-start(bf16[64,32,2560]{2,1,0:T(8,128)(2,1)} %param.13), calls=%async_computation.1 | async-start | bytes 983040 | tf_op jit(solution)/shard_map/slice | solution.py:143
  64.5 8.8 %copy-start.1 = (bf16[192,2560]{1,0:T(8,128)(2,1)S(1)}, bf16[192,2560]{1,0:T(8,128)(2,1)}, u32[]{:S(2)}) copy-start(bf16[192,2560]{1,0:T(8,128)(2,1)} %reshape.167) | copy-start | bytes 2949124
  73.2 1.1 %copy-start.21 = (bf16[2560,256]{1,0:T(8,128)(2,1)}, bf16[2560,256]{1,0:T(8,128)(2,1)S(1)}, u32[]{:S(2)}) copy-start(bf16[2560,256]{1,0:T(8,128)(2,1)S(1)} %fusion.11) | copy-start | bytes 3932164
  73.3 4.2 %copy-start.20 = (f32[2048]{0:T(1024)S(1)}, f32[2048]{0:T(1024)}, u32[]{:S(2)}) copy-start(f32[2048]{0:T(1024)} %sqrt.22) | copy-start | bytes 24580
  74.3 11.0 %collective-permute-start.1 = (bf16[3,32,256]{2,1,0:T(8,128)(2,1)S(1)}, bf16[3,32,256]{2,1,0:T(8,128)(2,1)S(1)}, u32[]{:S(2)}, u32[]{:S(2)}) collective-permute-start(bf16[3,32,256]{2,1,0:T(8,128)(2,1)S(1)} %bitcast.114), channel_id=1, source_target_pairs={{0,16},{16,32},{32,48},{48,64},{64,80},{80,96},{96,112},{112,0},{1... | collective-permute-start | bytes 147464 | tf_op jit(solution)/shard_map/ppermute | solution.py:18
  75.0 10.3 %collective-permute-start = (bf16[3,3,256]{2,1,0:T(4,128)(2,1)S(1)}, bf16[3,3,256]{2,1,0:T(4,128)(2,1)S(1)}, u32[]{:S(2)}, u32[]{:S(2)}) collective-permute-start(bf16[3,3,256]{2,1,0:T(4,128)(2,1)S(1)} %slice.223), channel_id=1, source_target_pairs={{0,17},{1,18},{2,19},{3,20},{4,21},{5,22},{6,23},{7,24},{8,25},{9,... | collective-permute-start | bytes 13832 | tf_op jit(solution)/shard_map/ppermute | solution.py:18
  75.6 9.8 %collective-permute-start.2 = (bf16[64,3,256]{2,1,0:T(4,128)(2,1)S(1)}, bf16[64,3,256]{2,1,0:T(4,128)(2,1)S(1)}, u32[]{:S(2)}, u32[]{:S(2)}) collective-permute-start(bf16[64,3,256]{2,1,0:T(4,128)(2,1)S(1)} %reshape.174), channel_id=1, source_target_pairs={{0,1},{1,2},{2,3},{3,4},{4,5},{5,6},{6,7},{7,8},{8,9},{9,10},{10,1... | collective-permute-start | bytes 294920 | tf_op jit(solution)/shard_map/ppermute | solution.py:18
  87.7 2.6 %copy-start.15 = (bf16[256,256]{1,0:T(8,128)(2,1)S(1)}, bf16[256,256]{1,0:T(8,128)(2,1)}, u32[]{:S(2)}) copy-start(bf16[256,256]{1,0:T(8,128)(2,1)} %get-tuple-element.23) | copy-start | bytes 393220
  87.7 2.6 %copy-start.16 = (bf16[256,256]{1,0:T(8,128)(2,1)S(1)}, bf16[256,256]{1,0:T(8,128)(2,1)}, u32[]{:S(2)}) copy-start(bf16[256,256]{1,0:T(8,128)(2,1)} %get-tuple-element.28) | copy-start | bytes 393220
  87.7 2.6 %copy-start.17 = (bf16[256,256]{1,0:T(8,128)(2,1)S(1)}, bf16[256,256]{1,0:T(8,128)(2,1)}, u32[]{:S(2)}) copy-start(bf16[256,256]{1,0:T(8,128)(2,1)} %get-tuple-element.29) | copy-start | bytes 393220
  90.1 1.8 %copy-start.12 = (bf16[256,256]{1,0:T(8,128)(2,1)S(1)}, bf16[256,256]{1,0:T(8,128)(2,1)}, u32[]{:S(2)}) copy-start(bf16[256,256]{1,0:T(8,128)(2,1)} %get-tuple-element.25) | copy-start | bytes 393220
  90.1 1.8 %copy-start.13 = (bf16[256,256]{1,0:T(8,128)(2,1)S(1)}, bf16[256,256]{1,0:T(8,128)(2,1)}, u32[]{:S(2)}) copy-start(bf16[256,256]{1,0:T(8,128)(2,1)} %get-tuple-element.26) | copy-start | bytes 393220
  90.1 1.8 %copy-start.14 = (bf16[256,256]{1,0:T(8,128)(2,1)S(1)}, bf16[256,256]{1,0:T(8,128)(2,1)}, u32[]{:S(2)}) copy-start(bf16[256,256]{1,0:T(8,128)(2,1)} %get-tuple-element.27) | copy-start | bytes 393220
  91.9 1.0 copy-start.10
  91.9 1.0 %copy-start.11 = (bf16[256,256]{1,0:T(8,128)(2,1)S(1)}, bf16[256,256]{1,0:T(8,128)(2,1)}, u32[]{:S(2)}) copy-start(bf16[256,256]{1,0:T(8,128)(2,1)} %get-tuple-element.31) | copy-start | bytes 393220
  94.3 1.0 copy-start.7
  94.3 1.0 %copy-start.8 = (bf16[256,256]{1,0:T(8,128)(2,1)S(1)}, bf16[256,256]{1,0:T(8,128)(2,1)}, u32[]{:S(2)}) copy-start(bf16[256,256]{1,0:T(8,128)(2,1)} %get-tuple-element.20) | copy-start | bytes 393220
  94.5 1.0 %copy-start.3 = (bf16[256,256]{1,0:T(8,128)(2,1)S(1)}, bf16[256,256]{1,0:T(8,128)(2,1)}, u32[]{:S(2)}) copy-start(bf16[256,256]{1,0:T(8,128)(2,1)} %get-tuple-element.16) | copy-start | bytes 393220
  94.5 1.0 %copy-start.4 = (bf16[256,256]{1,0:T(8,128)(2,1)S(1)}, bf16[256,256]{1,0:T(8,128)(2,1)}, u32[]{:S(2)}) copy-start(bf16[256,256]{1,0:T(8,128)(2,1)} %get-tuple-element.17) | copy-start | bytes 393220
  94.6 1.0 %copy-start.5 = (bf16[256,256]{1,0:T(8,128)(2,1)S(1)}, bf16[256,256]{1,0:T(8,128)(2,1)}, u32[]{:S(2)}) copy-start(bf16[256,256]{1,0:T(8,128)(2,1)} %get-tuple-element.18) | copy-start | bytes 393220
  (3 other events, 2.7 us)

commit v7 on v5

--- a/solution.py
+++ b/solution.py
@@ -21,7 +21,7 @@
 def strided_valid(field, kernel):
     height, breadth, depth = field.shape
     out_rows, out_cols = ((height - 3) // 2 + 1, (breadth - 3) // 2 + 1)
-    even_h, even_w = (height + height % 2, breadth + breadth % 2)
+    even_h, even_w = (height + height % 2, -(-breadth // 32) * 32)
     padded = jnp.pad(field, ((0, even_h - height), (0, even_w - breadth), (0, 0)))
     pairs = padded.reshape(even_h // 2, 2, even_w // 2, 2 * depth)
     zero_block = jnp.zeros((depth, depth), kernel.dtype)

time: 97.1 us -> 99 us (1.020)
  other arithmetic: 14.5 us -> 16.6 us
    reshape x2, local copies, waits for them, and re-layouts: 0.64 us -> 3.62 us  [strided_valid(): pairs = padded.reshape(even_h // 2, 2, even_w // 2, 2 * depth)]
    another operation x8 -> x2, local copies, waits for them, and re-layouts: 3.14 us -> 0.38 us  [the longest x6 2.76 us: strided_valid(): rows.reshape(-1, 2 * depth)]
    concatenate x1, other arithmetic: 0.68 us -> 1.88 us  [encode_tile(): extended = jnp.concatenate([top, body_rows], axis=0)]
    unnamed x49 -> x41, local copies, waits for them, and re-layouts: 1.98 us -> 2.67 us
  transfers between devices with their start and end apart: 4 -> 4, of which waited for: 1 -> 1; matrix products, arithmetic and copies ran while one was open for 24% -> 23% of each run, Pallas kernels for 0% -> 0%
where the time goes in v7:
time: 99 us; the launch traced here: 97.5 us
  matrix products  33 us (33%)
  local copies, waits for them, and re-layouts  17.9 us (18%)
  other arithmetic  16.6 us (17%)
  waiting for transfers between devices  14.6 us (15%)
  starting transfers between devices  14.3 us (14%)
  between operations  1.17 us (1%)
    all_to_all x1, waiting for transfers between devices, body(): lax.all_to_all(outgoing, ('lat', 'lon'), split_axis=0, concat_axis=0, til...  14.6 us
    all_to_all x1, starting transfers between devices, body(): lax.all_to_all(outgoing, ('lat', 'lon'), split_axis=0, concat_axis=0, til...  11.2 us
    dot_general x1, matrix products, body(): jnp.dot(radiances, project_weight, preferred_element_type=jnp.float32)  8.82 us
    dot_general x1, matrix products, body(): jnp.dot(slot_table, arrived_rows, preferred_element_type=jnp.float32)  8.74 us
    dot_general x2, matrix products, cells(): numer = jnp.dot(weights, obs_masked, preferred_element_type=jnp.float32)  7.87 us
    reduce_sum x1, other arithmetic, body(): density = jnp.sum(masked, axis=1, dtype=jnp.float32)  6.28 us
    dot_general x1, matrix products, body(): jnp.dot(selector_all, sources, preferred_element_type=jnp.float32)  4.06 us
    reshape x2, local copies, waits for them, and re-layouts, strided_valid(): pairs = padded.reshape(even_h // 2, 2, even_w // 2, 2 * depth)  3.62 us
  transfers between devices with their start and end apart: 4, of which 1 were waited for; matrix products, arithmetic and copies ran while one was open for 23% of the time, Pallas kernels for 0%

profile of v7, /device:TPU:0, one launch (start us, length us, event | category | flops | bytes accessed | tf_op | source)
XLA Modules:
  0.0 97.5 jit_solution(17946127174635197151)
XLA Ops:
  0.0 0.7 broadcast_add_fusion
  1.6 0.9 convert_reduce_fusion.1
  3.2 3.1 %fusion.6 = pred[4096,1024]{1,0:T(32,128)(4,1)S(1)} fusion(s32[4096]{0:T(1024)S(1)} %add.117, pred[4096]{0:T(1024)(128)(4,1)S(1)} %and.61), kind=kLoop, calls=%fused_computation.9 | loop fusion | flops 8388608 | bytes 4214784 | tf_op jit(solution)/shard_map/and | solution.py:86
  6.3 1.4 %fusion.23 = pred[4096,128]{1,0:T(32,128)(4,1)S(1)} fusion(s32[4096]{0:T(1024)S(1)} %eq.99, pred[4096]{0:T(1024)(128)(4,1)S(1)} %eq.98), kind=kLoop, calls=%fused_computation.28 | loop fusion | flops 1048576 | bytes 544768 | tf_op jit(solution)/shard_map/and | solution.py:113
  7.7 8.8 %convolution_convert_fusion = bf16[1024,256]{1,0:T(8,128)(2,1)S(1)} fusion(bf16[1024,8461]{0,1:T(8,128)(2,1)} %param.8, bf16[8461,256]{1,0:T(8,128)(2,1)S(1)} %copy-done.18), kind=kOutput, calls=%fused_computation.33 | convolution fusion | flops 4436262912 | bytes 22184448 | tf_op jit(solution)/shard_map/dot_general | solution.py:88
  17.0 4.1 %fusion.7 = bf16[4096,256]{1,0:T(8,128)(2,1)} fusion(pred[4096,128]{1,0:T(32,128)(4,1)S(1)} %fusion.23, pred[4096,1024]{1,0:T(32,128)(4,1)S(1)} %fusion.6, bf16[128,256]{1,0:T(8,128)(2,1)S(1)} %fusion.34, bf16[1024,256]{1,0:T(8,128)(2,1)S(1)} %convolution_convert_fusion), kind=kOutput, calls=%fused_computation.10 | convolution fusion | flops 2422865920 | bytes 7405568 | tf_op jit(solution)/shard_map/dot_general | solution.py:116
  21.0 11.2 %all-to-all-start = ((bf16[128,32,256]{2,1,0:T(8,128)(2,1)}), bf16[128,32,256]{2,1,0:T(8,128)(2,1)S(1)}, u32[]{:S(2)}, u32[]{:S(2)}) async-start(bf16[128,32,256]{2,1,0:T(8,128)(2,1)} %bitcast.102), calls=%async_computation | async-start | bytes 4194304 | tf_op jit(solution)/shard_map/all_to_all | solution.py:120
  32.2 2.4 %slice.162 = bf16[64,3,2560]{2,1,0:T(4,128)(2,1)S(1)} slice(bf16[64,32,2560]{2,1,0:T(8,128)(2,1)} %param.13), slice={[0:64], [29:32], [0:2560]} | slice | bytes 1966080 | tf_op jit(solution)/shard_map/slice | solution.py:148
  35.3 6.3 %convert_reduce_fusion = f32[64,32]{1,0:T(8,128)S(1)} fusion(bf16[64,32,2560]{2,1,0:T(8,128)(2,1)} %param.13, pred[2560]{0:T(1024)(128)(4,1)S(1)} %iota_compare_fusion.16), kind=kLoop, calls=%fused_computation.2 | loop fusion | flops 15726592 | bytes 10496512 | tf_op jit(solution)/shard_map/reduce_sum | solution.py:136
  42.0 1.6 %reshape.172 = bf16[192,2560]{1,0:T(8,128)(2,1)} reshape(bf16[64,3,2560]{2,1,0:T(4,128)(2,1)S(1)} %slice.162) | data formatting | bytes 1966080 | tf_op jit(solution)/shard_map/reshape | solution.py:148
  43.7 2.5 %slice_bitcast_fusion.18 = (bf16[256,256]{1,0:T(8,128)(2,1)}, bf16[256,256]{1,0:T(8,128)(2,1)}, bf16[256,256]{1,0:T(8,128)(2,1)}, bf16[256,256]{1,0:T(8,128)(2,1...) fusion(bf16[3,3,256,256]{3,2,1,0:T(8,128)(2,1)} %param.14), kind=kLoop, calls=%fused_computation.153 | loop fusion | bytes 2359296 | tf_op jit(solution)/shard_map/squeeze | solution.py:34
  46.2 0.9 slice_bitcast_fusion.9
  47.1 14.6 %all-to-all-done = bf16[128,32,256]{2,1,0:T(8,128)(2,1)S(1)} async-done(((bf16[128,32,256]{2,1,0:T(8,128)(2,1)}), bf16[128,32,256]{2,1,0:T(8,128)(2,1)S(1)}, u32[]{:S(2)}, u32[]{:S(2)}) %all-to-all-start) | async-done | bytes 2097184 | tf_op jit(solution)/shard_map/all_to_all | solution.py:120
  61.7 1.4 %reshape.175 = bf16[3584,256]{1,0:T(8,128)(2,1)} reshape(bf16[128,28,256]{2,1,0:T(8,128)(2,1)S(1)} %bitcast.98) | data formatting | bytes 3670016 | tf_op jit(solution)/shard_map/reshape | solution.py:121
  63.6 8.7 %fusion.15 = bf16[2560,256]{1,0:T(8,128)(2,1)S(1)} fusion(bf16[3584,256]{1,0:T(8,128)(2,1)} %reshape.175, s32[3584]{0:T(1024)S(1)} %sub.14, pred[2560]{0:T(1024)(128)(4,1)S(1)} %iota_compare_fusion.16), kind=kOutput, calls=%fused_computation.18 | convolution fusion | flops 4708106240 | bytes 3162624 | tf_op jit(solution)/shard_map/dot_general | solution.py:128
  73.4 0.7 collective-permute-start.1
  74.7 1.9 %collective-permute-start.2 = (bf16[64,3,256]{2,1,0:T(4,128)(2,1)S(1)}, bf16[64,3,256]{2,1,0:T(4,128)(2,1)S(1)}, u32[]{:S(2)}, u32[]{:S(2)}) collective-permute-start(bf16[64,3,256]{2,1,0:T(4,128)(2,1)S(1)} %reshape.179), channel_id=1, source_target_pairs={{0,1},{1,2},{2,3},{3,4},{4,5},{5,6},{6,7},{7,8},{8,9},{9,10},{10,1... | collective-permute-start | bytes 294920 | tf_op jit(solution)/shard_map/ppermute | solution.py:18
  76.6 7.3 %fusion.20 = bf16[2048,256]{0,1:T(8,128)(2,1)S(1)} fusion(bf16[2560,256]{1,0:T(8,128)(2,1)} %copy-done.19, bf16[2048,2560]{1,0:T(8,128)(2,1)} %bitcast.96, f32[2048]{0:T(1024)S(1)} %sqrt.22), kind=kOutput, calls=%fused_computation.24 | convolution fusion | flops 2685403136 | bytes 12853248 | tf_op jit(solution)/shard_map/dot_general | solution.py:141
  84.5 1.9 %fusion.21 = bf16[68,64,256]{2,1,0:T(8,128)(2,1)} fusion(bf16[3,35,256]{2,1,0:T(8,128)(2,1)S(1)} %maximum_select_fusion, bf16[64,32,256]{2,1,0:T(8,128)(2,1)S(1)} %bitcast.99, bf16[64,3,256]{2,1,0:T(4,128)(2,1)S(1)} %collective-permute-done.2), kind=kLoop, calls=%fused_computation.25 | loop fusion | flops 16711680 | bytes 3428864 | tf_op jit(solution)/shard_map/concatenate | solution.py:51
  86.4 3.4 %reshape.182 = bf16[34,2,32,512]{3,2,1,0:T(8,128)(2,1)S(1)} reshape(bf16[68,64,256]{2,1,0:T(8,128)(2,1)} %fusion.21) | data formatting | bytes 4456448 | tf_op jit(solution)/shard_map/reshape | solution.py:26
  90.9 0.7 fusion.53
  91.9 0.7 fusion.56
  92.9 0.7 fusion.59
  96.8 0.7 fusion.114
  (98 shorter events, 9.6 us)
Async XLA Ops:
  3.2 4.5 %copy-start.18 = (bf16[8461,256]{1,0:T(8,128)(2,1)S(1)}, bf16[8461,256]{1,0:T(8,128)(2,1)}, u32[]{:S(2)}) copy-start(bf16[8461,256]{1,0:T(8,128)(2,1)} %param.9) | copy-start | bytes 12996100
  21.0 40.7 %all-to-all-start = ((bf16[128,32,256]{2,1,0:T(8,128)(2,1)}), bf16[128,32,256]{2,1,0:T(8,128)(2,1)S(1)}, u32[]{:S(2)}, u32[]{:S(2)}) async-start(bf16[128,32,256]{2,1,0:T(8,128)(2,1)} %bitcast.102), calls=%async_computation | async-start | bytes 4194304 | tf_op jit(solution)/shard_map/all_to_all | solution.py:120
  43.6 2.6 %copy-start = (bf16[3,3,256,256]{3,2,1,0:T(8,128)(2,1)S(1)}, bf16[3,3,256,256]{3,2,1,0:T(8,128)(2,1)}, u32[]{:S(2)}) copy-start(bf16[3,3,256,256]{3,2,1,0:T(8,128)(2,1)} %param.15) | copy-start | bytes 3538948
  63.6 8.8 %slice-start = ((bf16[64,32,2560]{2,1,0:T(8,128)(2,1)}), bf16[3,32,2560]{2,1,0:T(8,128)(2,1)S(1)}, s32[]{:S(2)}) async-start(bf16[64,32,2560]{2,1,0:T(8,128)(2,1)} %param.13), calls=%async_computation.1 | async-start | bytes 983040 | tf_op jit(solution)/shard_map/slice | solution.py:147
  63.6 8.8 %copy-start.1 = (bf16[192,2560]{1,0:T(8,128)(2,1)S(1)}, bf16[192,2560]{1,0:T(8,128)(2,1)}, u32[]{:S(2)}) copy-start(bf16[192,2560]{1,0:T(8,128)(2,1)} %reshape.172) | copy-start | bytes 2949124
  72.3 1.1 %copy-start.19 = (bf16[2560,256]{1,0:T(8,128)(2,1)}, bf16[2560,256]{1,0:T(8,128)(2,1)S(1)}, u32[]{:S(2)}) copy-start(bf16[2560,256]{1,0:T(8,128)(2,1)S(1)} %fusion.15) | copy-start | bytes 3932164
  73.4 11.0 %collective-permute-start.1 = (bf16[3,32,256]{2,1,0:T(8,128)(2,1)S(1)}, bf16[3,32,256]{2,1,0:T(8,128)(2,1)S(1)}, u32[]{:S(2)}, u32[]{:S(2)}) collective-permute-start(bf16[3,32,256]{2,1,0:T(8,128)(2,1)S(1)} %bitcast.112), channel_id=1, source_target_pairs={{0,16},{16,32},{32,48},{48,64},{64,80},{80,96},{96,112},{112,0},{1... | collective-permute-start | bytes 147464 | tf_op jit(solution)/shard_map/ppermute | solution.py:18
  74.1 10.3 %collective-permute-start = (bf16[3,3,256]{2,1,0:T(4,128)(2,1)S(1)}, bf16[3,3,256]{2,1,0:T(4,128)(2,1)S(1)}, u32[]{:S(2)}, u32[]{:S(2)}) collective-permute-start(bf16[3,3,256]{2,1,0:T(4,128)(2,1)S(1)} %slice.223), channel_id=1, source_target_pairs={{0,17},{1,18},{2,19},{3,20},{4,21},{5,22},{6,23},{7,24},{8,25},{9,... | collective-permute-start | bytes 13832 | tf_op jit(solution)/shard_map/ppermute | solution.py:18
  74.7 9.8 %collective-permute-start.2 = (bf16[64,3,256]{2,1,0:T(4,128)(2,1)S(1)}, bf16[64,3,256]{2,1,0:T(4,128)(2,1)S(1)}, u32[]{:S(2)}, u32[]{:S(2)}) collective-permute-start(bf16[64,3,256]{2,1,0:T(4,128)(2,1)S(1)} %reshape.179), channel_id=1, source_target_pairs={{0,1},{1,2},{2,3},{3,4},{4,5},{5,6},{6,7},{7,8},{8,9},{9,10},{10,1... | collective-permute-start | bytes 294920 | tf_op jit(solution)/shard_map/ppermute | solution.py:18
  89.8 0.9 copy-start.15
  89.8 1.0 copy-start.16
  89.8 1.0 %copy-start.17 = (bf16[256,256]{1,0:T(8,128)(2,1)S(1)}, bf16[256,256]{1,0:T(8,128)(2,1)}, u32[]{:S(2)}) copy-start(bf16[256,256]{1,0:T(8,128)(2,1)} %get-tuple-element.31) | copy-start | bytes 393220
  90.9 0.9 copy-start.12
  90.9 1.0 copy-start.13
  90.9 1.0 %copy-start.14 = (bf16[256,256]{1,0:T(8,128)(2,1)S(1)}, bf16[256,256]{1,0:T(8,128)(2,1)}, u32[]{:S(2)}) copy-start(bf16[256,256]{1,0:T(8,128)(2,1)} %get-tuple-element.29) | copy-start | bytes 393220
  91.9 1.0 copy-start.10
  91.9 1.0 %copy-start.11 = (bf16[256,256]{1,0:T(8,128)(2,1)S(1)}, bf16[256,256]{1,0:T(8,128)(2,1)}, u32[]{:S(2)}) copy-start(bf16[256,256]{1,0:T(8,128)(2,1)} %get-tuple-element.33) | copy-start | bytes 393220
  94.4 0.9 copy-start.6
  94.4 1.0 copy-start.7
  94.4 1.0 %copy-start.8 = (bf16[256,256]{1,0:T(8,128)(2,1)S(1)}, bf16[256,256]{1,0:T(8,128)(2,1)}, u32[]{:S(2)}) copy-start(bf16[256,256]{1,0:T(8,128)(2,1)} %get-tuple-element.22) | copy-start | bytes 393220
  94.7 1.1 %copy-start.3 = (bf16[256,256]{1,0:T(8,128)(2,1)S(1)}, bf16[256,256]{1,0:T(8,128)(2,1)}, u32[]{:S(2)}) copy-start(bf16[256,256]{1,0:T(8,128)(2,1)} %get-tuple-element.18) | copy-start | bytes 393220
  94.7 1.1 %copy-start.4 = (bf16[256,256]{1,0:T(8,128)(2,1)S(1)}, bf16[256,256]{1,0:T(8,128)(2,1)}, u32[]{:S(2)}) copy-start(bf16[256,256]{1,0:T(8,128)(2,1)} %get-tuple-element.19) | copy-start | bytes 393220
  94.7 1.1 %copy-start.5 = (bf16[256,256]{1,0:T(8,128)(2,1)S(1)}, bf16[256,256]{1,0:T(8,128)(2,1)}, u32[]{:S(2)}) copy-start(bf16[256,256]{1,0:T(8,128)(2,1)} %get-tuple-element.20) | copy-start | bytes 393220
  95.5 0.9 copy-start.2
  (1 other events, 0.9 us)

commit v8 on v5

--- a/solution.py
+++ b/solution.py
@@ -47,7 +47,7 @@
 def encode_tile(grid, north, west, north_west, conv1_weight, conv2_weight):
     top = jnp.concatenate([north_west, north], axis=1)
     top = jnp.where(lax.axis_index("lat") == 0, jnp.zeros((), top.dtype), top)
-    body_rows = jnp.concatenate([west, grid], axis=1)
+    body_rows = jnp.concatenate([jnp.swapaxes(west, 0, 1), grid], axis=1)
     extended = jnp.concatenate([top, body_rows], axis=0)
     hidden = jax.nn.gelu(strided_valid(extended, conv1_weight)).astype(jnp.bfloat16)
     return strided_valid(hidden, conv2_weight).astype(jnp.bfloat16)
@@ -145,14 +145,16 @@
     rim_weights = jnp.concatenate(
         [
             weights_cells[-rim:].reshape(-1, slot_count),
-            weights_cells[:, -rim:].reshape(-1, slot_count),
+            jnp.swapaxes(weights_cells[:, -rim:], 0, 1).reshape(-1, slot_count),
         ],
         axis=0,
     )
-    rim_roots = jnp.concatenate([root[-rim:].reshape(-1, 1), root[:, -rim:].reshape(-1, 1)], axis=0)
+    rim_roots = jnp.concatenate(
+        [root[-rim:].reshape(-1, 1), jnp.swapaxes(root[:, -rim:], 0, 1).reshape(-1, 1)], axis=0
+    )
     rim_cells = cells(rim_weights, rim_roots)
     north_rows = rim_cells[: rim * tile_cols].reshape(rim, tile_cols, channel_count)
-    west_cols = rim_cells[rim * tile_cols :].reshape(tile_rows, rim, channel_count)
+    west_cols = rim_cells[rim * tile_cols :].reshape(rim, tile_rows, channel_count)
     north = cyclic(north_rows, ("lat",), (1,))
     west = cyclic(west_cols, ("lon",), (1,))
     north_west = cyclic(north_rows[:, -rim:], ("lat", "lon"), (1, 1))

time: 97.1 us -> 104 us (1.071); the launches traced: 95.7 us -> 104 us
  local copies, waits for them, and re-layouts: 18.5 us -> 24 us
  waiting for transfers between devices: 13.9 us -> 16.8 us
  other arithmetic: 14.5 us -> 16.4 us
  matrix products: 33.1 us -> 31.3 us
    dot_general x2, matrix products: 7.87 us -> 4.9 us  [cells(): numer = jnp.dot(weights, obs_masked, preferred_element_type=jnp.float32)]
    reshape x1, local copies, waits for them, and re-layouts: 1.43 us -> 3.89 us  [body(): arrived_rows = arrived[:, :capacity].reshape(-1, channel_count)]
    ppermute x3, waiting for transfers between devices: 0.01 us -> 2.41 us  [cyclic(): return lax.ppermute(value, axes if len(axes) > 1 else axes[0], pairs)]
    unnamed x49 -> x58, local copies, waits for them, and re-layouts: 1.98 us -> 4.03 us
    slice x1, local copies, waits for them, and re-layouts: 0.01 us -> 1.34 us  [body(): north_west = cyclic(north_rows[:, -rim:], ('lat', 'lon'), (1, 1))]
    dot_general x1, matrix products: 8.75 us -> 9.87 us  [body(): jnp.dot(slot_table, arrived_rows, preferred_element_type=jnp.float32)]
    slice x3 -> x2, local copies, waits for them, and re-layouts: 2.5 us -> 2.43 us  [the longest x1 2.42 us: body(): weights_cells[:, -rim:]]
  transfers between devices with their start and end apart: 4 -> 4, of which waited for: 1 -> 2; matrix products, arithmetic and copies ran while one was open for 24% -> 20% of each run, Pallas kernels for 0% -> 0%
where the time goes in v8:
time: 104 us
  matrix products  31.3 us (30%)
  local copies, waits for them, and re-layouts  24 us (23%)
  waiting for transfers between devices  16.8 us (16%)
  other arithmetic  16.4 us (16%)
  starting transfers between devices  14 us (13%)
  between operations  1.31 us (1%)
    all_to_all x1, waiting for transfers between devices, body(): lax.all_to_all(outgoing, ('lat', 'lon'), split_axis=0, concat_axis=0, til...  14.4 us
    all_to_all x1, starting transfers between devices, body(): lax.all_to_all(outgoing, ('lat', 'lon'), split_axis=0, concat_axis=0, til...  11.2 us
    dot_general x1, matrix products, body(): jnp.dot(slot_table, arrived_rows, preferred_element_type=jnp.float32)  9.87 us
    dot_general x1, matrix products, body(): jnp.dot(radiances, project_weight, preferred_element_type=jnp.float32)  8.82 us
    reduce_sum x1, other arithmetic, body(): density = jnp.sum(masked, axis=1, dtype=jnp.float32)  6.28 us
    dot_general x2, matrix products, cells(): numer = jnp.dot(weights, obs_masked, preferred_element_type=jnp.float32)  4.9 us
    dot_general x1, matrix products, body(): jnp.dot(selector_all, sources, preferred_element_type=jnp.float32)  4.05 us
    unnamed x58, local copies, waits for them, and re-layouts  4.03 us
  transfers between devices with their start and end apart: 4, of which 2 were waited for; matrix products, arithmetic and copies ran while one was open for 20% of the time, Pallas kernels for 0%

profile of v8, /device:TPU:0, one launch (start us, length us, event | category | flops | bytes accessed | tf_op | source)
XLA Modules:
  0.0 103.7 jit_solution(8501673751792454579)
XLA Ops:
  2.5 3.1 %fusion.6 = pred[4096,1024]{1,0:T(32,128)(4,1)S(1)} fusion(s32[4096]{0:T(1024)S(1)} %add.117, pred[4096]{0:T(1024)(128)(4,1)S(1)} %and.61), kind=kLoop, calls=%fused_computation.9 | loop fusion | flops 8388608 | bytes 4214784 | tf_op jit(solution)/shard_map/and | solution.py:86
  5.6 1.4 %fusion.18 = pred[4096,128]{1,0:T(32,128)(4,1)S(1)} fusion(s32[4096]{0:T(1024)S(1)} %eq.99, pred[4096]{0:T(1024)(128)(4,1)S(1)} %eq.98), kind=kLoop, calls=%fused_computation.23 | loop fusion | flops 1048576 | bytes 544768 | tf_op jit(solution)/shard_map/and | solution.py:113
  7.0 8.8 %convolution_convert_fusion = bf16[1024,256]{1,0:T(8,128)(2,1)S(1)} fusion(bf16[1024,8461]{0,1:T(8,128)(2,1)} %param.8, bf16[8461,256]{1,0:T(8,128)(2,1)S(1)} %copy-done.23), kind=kOutput, calls=%fused_computation.33 | convolution fusion | flops 4436262912 | bytes 22184448 | tf_op jit(solution)/shard_map/dot_general | solution.py:88
  16.3 4.0 %fusion.7 = bf16[4096,256]{1,0:T(8,128)(2,1)} fusion(pred[4096,128]{1,0:T(32,128)(4,1)S(1)} %fusion.18, pred[4096,1024]{1,0:T(32,128)(4,1)S(1)} %fusion.6, bf16[128,256]{1,0:T(8,128)(2,1)S(1)} %fusion.34, bf16[1024,256]{1,0:T(8,128)(2,1)S(1)} %convolution_convert_fusion), kind=kOutput, calls=%fused_computation.10 | convolution fusion | flops 2422865920 | bytes 7405568 | tf_op jit(solution)/shard_map/dot_general | solution.py:116
  20.4 11.2 %all-to-all-start = ((bf16[128,32,256]{2,1,0:T(8,128)(2,1)}), bf16[128,32,256]{2,1,0:T(8,128)(2,1)S(1)}, u32[]{:S(2)}, u32[]{:S(2)}) async-start(bf16[128,32,256]{2,1,0:T(8,128)(2,1)} %bitcast.99), calls=%async_computation | async-start | bytes 4194304 | tf_op jit(solution)/shard_map/all_to_all | solution.py:120
  31.5 2.4 %slice.162 = bf16[64,3,2560]{2,1,0:T(4,128)(2,1)S(1)} slice(bf16[64,32,2560]{2,1,0:T(8,128)(2,1)} %param.13), slice={[0:64], [29:32], [0:2560]} | slice | bytes 1966080 | tf_op jit(solution)/shard_map/slice | solution.py:148
  34.6 6.3 %convert_reduce_fusion = f32[64,32]{1,0:T(8,128)S(1)} fusion(bf16[64,32,2560]{2,1,0:T(8,128)(2,1)} %param.13, pred[2560]{0:T(1024)(128)(4,1)S(1)} %iota_compare_fusion.16), kind=kLoop, calls=%fused_computation.2 | loop fusion | flops 15726592 | bytes 10496512 | tf_op jit(solution)/shard_map/reduce_sum | solution.py:136
  41.9 1.2 %copy.27 = bf16[64,3,2560]{2,0,1:T(8,128)(2,1)} copy(bf16[64,3,2560]{2,1,0:T(4,128)(2,1)S(1)} %slice.162) | data formatting | bytes 1966080
  43.2 2.5 %slice_bitcast_fusion.18 = (bf16[256,256]{1,0:T(8,128)(2,1)}, bf16[256,256]{1,0:T(8,128)(2,1)}, bf16[256,256]{1,0:T(8,128)(2,1)}, bf16[256,256]{1,0:T(8,128)(2,1...) fusion(bf16[3,3,256,256]{3,2,1,0:T(8,128)(2,1)} %param.14), kind=kLoop, calls=%fused_computation.153 | loop fusion | bytes 2359296 | tf_op jit(solution)/shard_map/squeeze | solution.py:34
  45.7 1.0 slice_bitcast_fusion.9
  46.6 14.4 %all-to-all-done = bf16[128,32,256]{2,1,0:T(8,128)(2,1)S(1)} async-done(((bf16[128,32,256]{2,1,0:T(8,128)(2,1)}), bf16[128,32,256]{2,1,0:T(8,128)(2,1)S(1)}, u32[]{:S(2)}, u32[]{:S(2)}) %all-to-all-start) | async-done | bytes 2097184 | tf_op jit(solution)/shard_map/all_to_all | solution.py:120
  61.0 1.3 %copy-done = bf16[128,32,256]{2,1,0:T(8,128)(2,1)} copy-done((bf16[128,32,256]{2,1,0:T(8,128)(2,1)}, bf16[128,32,256]{2,1,0:T(8,128)(2,1)S(1)}, u32[]{:S(2)}) %copy-start) | copy-done | bytes 2097176
  62.3 3.9 %reshape.175 = bf16[3584,256]{1,0:T(8,128)(2,1)} reshape(bf16[128,28,256]{2,1,0:T(8,128)(2,1)} %bitcast.97) | data formatting | bytes 3670016 | tf_op jit(solution)/shard_map/reshape | solution.py:121
  66.2 1.3 %slice_convert_fusion = s32[128,1,256]{2,1,0:T(1,128)S(1)} fusion(bf16[128,32,256]{2,1,0:T(8,128)(2,1)} %copy-done), kind=kLoop, calls=%fused_computation.133 | loop fusion | flops 32768 | bytes 196608 | tf_op jit(solution)/shard_map/convert_element_type | solution.py:122
  67.8 9.9 %fusion.11 = bf16[2560,256]{1,0:T(8,128)(2,1)} fusion(bf16[3584,256]{1,0:T(8,128)(2,1)} %reshape.175, s32[3584]{0:T(1024)S(1)} %sub.14, pred[2560]{0:T(1024)(128)(4,1)S(1)} %copy-done.20), kind=kOutput, calls=%fused_computation.12 | convolution fusion | flops 4708106240 | bytes 3162624 | tf_op jit(solution)/shard_map/dot_general | solution.py:128
  77.6 2.0 %fusion.31 = bf16[288,256]{1,0:T(8,128)(2,1)S(1)} fusion(bf16[2560,256]{1,0:T(8,128)(2,1)} %fusion.11, bf16[192,2560]{1,0:T(8,128)(2,1)S(1)} %bitcast.100, bf16[96,2560]{1,0:T(8,128)(2,1)S(1)} %bitcast.96, f32[288]{0:T(512)S(1)} %maximum_reduce_fusion), kind=kOutput, calls=%fused_computation.36 | convolution fusion | flops 380583936 | bytes 2933888 | tf_op jit(solution)/shard_map/dot_general | solution.py:141
  80.9 1.3 %slice.223 = bf16[3,3,256]{2,1,0:T(4,128)(2,1)} slice(bf16[3,32,256]{2,1,0:T(8,128)(2,1)} %bitcast.8), slice={[0:3], [29:32], [0:256]} | slice | bytes 9216 | tf_op jit(solution)/shard_map/slice | solution.py:160
  83.5 1.6 %collective-permute-start.2 = (bf16[3,64,256]{2,0,1:T(4,128)(2,1)}, bf16[3,64,256]{2,0,1:T(4,128)(2,1)S(1)}, u32[]{:S(2)}, u32[]{:S(2)}) collective-permute-start(bf16[3,64,256]{2,0,1:T(4,128)(2,1)} %copy.24), channel_id=1, source_target_pairs={{0,1},{1,2},{2,3},{3,4},{4,5},{5,6},{6,7},{7,8},{8,9},{9,10},{10,1... | collective-permute-start | bytes 294920 | tf_op jit(solution)/shard_map/ppermute | solution.py:18
  85.2 2.9 %fusion.17 = bf16[2048,256]{0,1:T(8,128)(2,1)S(1)} fusion(bf16[2560,256]{1,0:T(8,128)(2,1)S(1)} %copy-done.24, bf16[2048,2560]{1,0:T(8,128)(2,1)S(1)} %bitcast.95, f32[2048]{0:T(1024)S(1)} %copy-done.21), kind=kOutput, calls=%fused_computation.21 | convolution fusion | flops 2685403136 | bytes 12853248 | tf_op jit(solution)/shard_map/dot_general | solution.py:141
  88.6 2.4 %collective-permute-done = bf16[3,3,256]{2,1,0:T(4,128)(2,1)S(1)} collective-permute-done((bf16[3,3,256]{2,1,0:T(4,128)(2,1)}, bf16[3,3,256]{2,1,0:T(4,128)(2,1)S(1)}, u32[]{:S(2)}, u32[]{:S(2)}) %collective-permute-start) | collective-permute-done | bytes 4640 | tf_op jit(solution)/shard_map/ppermute | solution.py:18
  91.0 0.8 maximum_select_fusion
  93.1 1.1 %fusion.143 = (bf16[33,1,18,512]{3,2,1,0:T(8,128)(2,1)}, bf16[33,1,18,512]{3,2,1,0:T(8,128)(2,1)S(1)}, bf16[33,1,18,512]{3,2,1,0:T(8,128)(2,1)S(1)}) fusion(bf16[34,2,18,512]{3,2,1,0:T(8,128)(2,1)S(1)} %reshape.182), kind=kLoop, calls=%fused_computation.196 | loop fusion | bytes 3649536 | tf_op jit(solution)/shard_map/slice | solution.py:31
  94.2 2.2 %reshape_squeeze.18 = bf16[594,512]{1,0:T(8,128)(2,1)} reshape(bf16[33,1,18,512]{3,2,1,0:T(8,128)(2,1)} %get-tuple-element.11) | data formatting | bytes 1216512 | tf_op jit(solution)/shard_map/reshape;squeeze | solution.py:39
  96.8 1.6 %fusion.53 = f32[594,512]{1,0:T(8,128)S(1)} fusion(bf16[594,512]{1,0:T(8,128)(2,1)} %reshape_squeeze.18, bf16[256,256]{1,0:T(8,128)(2,1)S(1)} %copy-done.17, bf16[256,256]{1,0:T(8,128)(2,1)S(1)} %copy-done.18, bf16[256,256]{1,0:T(8,128)(2,1)S(1)} %copy-done.16), kind=kOutput, calls=%fused_computation.63 | convolution fusion | flops 313524224 | bytes 2217984 | tf_op jit(solution)/shard_map/dot_general | solution.py:39
  (126 shorter events, 13.9 us)
Async XLA Ops:
  0.0 1.6 %copy-start.22 = (s32[1024]{0:T(1024)S(1)}, s32[1024]{0:T(1024)}, u32[]{:S(2)}) copy-start(s32[1024]{0:T(1024)} %param.10) | copy-start | bytes 12292
  2.5 4.5 %copy-start.23 = (bf16[8461,256]{1,0:T(8,128)(2,1)S(1)}, bf16[8461,256]{1,0:T(8,128)(2,1)}, u32[]{:S(2)}) copy-start(bf16[8461,256]{1,0:T(8,128)(2,1)} %param.9) | copy-start | bytes 12996100
  20.4 40.6 %all-to-all-start = ((bf16[128,32,256]{2,1,0:T(8,128)(2,1)}), bf16[128,32,256]{2,1,0:T(8,128)(2,1)S(1)}, u32[]{:S(2)}, u32[]{:S(2)}) async-start(bf16[128,32,256]{2,1,0:T(8,128)(2,1)} %bitcast.99), calls=%async_computation | async-start | bytes 4194304 | tf_op jit(solution)/shard_map/all_to_all | solution.py:120
  34.6 6.3 %copy-start.19 = (pred[2560]{0:T(1024)(128)(4,1)}, pred[2560]{0:T(1024)(128)(4,1)S(1)}, u32[]{:S(2)}) copy-start(pred[2560]{0:T(1024)(128)(4,1)S(1)} %iota_compare_fusion.16) | copy-start | bytes 7684
  43.1 2.6 %copy-start.1 = (bf16[3,3,256,256]{3,2,1,0:T(8,128)(2,1)S(1)}, bf16[3,3,256,256]{3,2,1,0:T(8,128)(2,1)}, u32[]{:S(2)}) copy-start(bf16[3,3,256,256]{3,2,1,0:T(8,128)(2,1)} %param.15) | copy-start | bytes 3538948
  61.0 1.3 %copy-start = (bf16[128,32,256]{2,1,0:T(8,128)(2,1)}, bf16[128,32,256]{2,1,0:T(8,128)(2,1)S(1)}, u32[]{:S(2)}) copy-start(bf16[128,32,256]{2,1,0:T(8,128)(2,1)S(1)} %all-to-all-done) | copy-start | bytes 6291460
  62.3 5.4 %copy-start.20 = (pred[2560]{0:T(1024)(128)(4,1)S(1)}, pred[2560]{0:T(1024)(128)(4,1)}, u32[]{:S(2)}) copy-start(pred[2560]{0:T(1024)(128)(4,1)} %copy-done.19) | copy-start | bytes 7684
  62.3 22.8 %slice-start = ((s8[10485760]{0:T(1024)(128)(4,1)}), s8[2097152]{0:T(1024)(128)(4,1)S(1)}, s32[]{:S(2)}) async-start(s8[10485760]{0:T(1024)(128)(4,1)} %bitcast.93), calls=%async_computation.1 | async-start | bytes 4194304
  67.7 9.9 %slice-start.3 = ((bf16[64,32,2560]{2,1,0:T(8,128)(2,1)}), bf16[3,32,2560]{2,1,0:T(8,128)(2,1)S(1)}, s32[]{:S(2)}) async-start(bf16[64,32,2560]{2,1,0:T(8,128)(2,1)} %param.13), calls=%async_computation.4 | async-start | bytes 983040 | tf_op jit(solution)/shard_map/slice | solution.py:147
  67.7 9.9 %copy-start.2 = (bf16[64,3,2560]{2,0,1:T(8,128)(2,1)S(1)}, bf16[64,3,2560]{2,0,1:T(8,128)(2,1)}, u32[]{:S(2)}) copy-start(bf16[64,3,2560]{2,0,1:T(8,128)(2,1)} %copy.27) | copy-start | bytes 2949124
  67.7 17.4 %slice-start.1 = ((s8[10485760]{0:T(1024)(128)(4,1)}), s8[4194304]{0:T(1024)(128)(4,1)S(1)}, s32[]{:S(2)}) async-start(s8[10485760]{0:T(1024)(128)(4,1)} %bitcast.93), calls=%async_computation.2 | async-start | bytes 8388608
  67.8 17.4 %slice-start.2 = ((s8[10485760]{0:T(1024)(128)(4,1)}), s8[4194304]{0:T(1024)(128)(4,1)S(1)}, s32[]{:S(2)}) async-start(s8[10485760]{0:T(1024)(128)(4,1)} %bitcast.93), calls=%async_computation.3 | async-start | bytes 8388608
  77.6 7.5 %copy-start.21 = (f32[2048]{0:T(1024)S(1)}, f32[2048]{0:T(1024)}, u32[]{:S(2)}) copy-start(f32[2048]{0:T(1024)} %sqrt.22) | copy-start | bytes 24580
  77.6 7.5 %copy-start.24 = (bf16[2560,256]{1,0:T(8,128)(2,1)S(1)}, bf16[2560,256]{1,0:T(8,128)(2,1)}, u32[]{:S(2)}) copy-start(bf16[2560,256]{1,0:T(8,128)(2,1)} %fusion.11) | copy-start | bytes 3932164
  80.2 10.8 %collective-permute-start.1 = (bf16[3,32,256]{2,1,0:T(8,128)(2,1)}, bf16[3,32,256]{2,1,0:T(8,128)(2,1)}, u32[]{:S(2)}, u32[]{:S(2)}) collective-permute-start(bf16[3,32,256]{2,1,0:T(8,128)(2,1)} %bitcast.8), channel_id=1, source_target_pairs={{0,16},{16,32},{32,48},{48,64},{64,80},{80,96},{96,112},{112,0},{1... | collective-permute-start | bytes 147464 | tf_op jit(solution)/shard_map/ppermute | solution.py:18
  82.3 8.8 %collective-permute-start = (bf16[3,3,256]{2,1,0:T(4,128)(2,1)}, bf16[3,3,256]{2,1,0:T(4,128)(2,1)S(1)}, u32[]{:S(2)}, u32[]{:S(2)}) collective-permute-start(bf16[3,3,256]{2,1,0:T(4,128)(2,1)} %slice.223), channel_id=1, source_target_pairs={{0,17},{1,18},{2,19},{3,20},{4,21},{5,22},{6,23},{7,24},{8,25},{9,... | collective-permute-start | bytes 13832 | tf_op jit(solution)/shard_map/ppermute | solution.py:18
  83.5 8.3 %collective-permute-start.2 = (bf16[3,64,256]{2,0,1:T(4,128)(2,1)}, bf16[3,64,256]{2,0,1:T(4,128)(2,1)S(1)}, u32[]{:S(2)}, u32[]{:S(2)}) collective-permute-start(bf16[3,64,256]{2,0,1:T(4,128)(2,1)} %copy.24), channel_id=1, source_target_pairs={{0,1},{1,2},{2,3},{3,4},{4,5},{5,6},{6,7},{7,8},{8,9},{9,10},{10,1... | collective-permute-start | bytes 294920 | tf_op jit(solution)/shard_map/ppermute | solution.py:18
  94.2 2.6 %copy-start.16 = (bf16[256,256]{1,0:T(8,128)(2,1)S(1)}, bf16[256,256]{1,0:T(8,128)(2,1)}, u32[]{:S(2)}) copy-start(bf16[256,256]{1,0:T(8,128)(2,1)} %get-tuple-element.23) | copy-start | bytes 393220
  94.2 2.6 %copy-start.17 = (bf16[256,256]{1,0:T(8,128)(2,1)S(1)}, bf16[256,256]{1,0:T(8,128)(2,1)}, u32[]{:S(2)}) copy-start(bf16[256,256]{1,0:T(8,128)(2,1)} %get-tuple-element.28) | copy-start | bytes 393220
  94.2 2.6 %copy-start.18 = (bf16[256,256]{1,0:T(8,128)(2,1)S(1)}, bf16[256,256]{1,0:T(8,128)(2,1)}, u32[]{:S(2)}) copy-start(bf16[256,256]{1,0:T(8,128)(2,1)} %get-tuple-element.29) | copy-start | bytes 393220
  96.5 1.8 %copy-start.13 = (bf16[256,256]{1,0:T(8,128)(2,1)S(1)}, bf16[256,256]{1,0:T(8,128)(2,1)}, u32[]{:S(2)}) copy-start(bf16[256,256]{1,0:T(8,128)(2,1)} %get-tuple-element.25) | copy-start | bytes 393220
  96.6 1.8 %copy-start.14 = (bf16[256,256]{1,0:T(8,128)(2,1)S(1)}, bf16[256,256]{1,0:T(8,128)(2,1)}, u32[]{:S(2)}) copy-start(bf16[256,256]{1,0:T(8,128)(2,1)} %get-tuple-element.26) | copy-start | bytes 393220
  96.6 1.8 %copy-start.15 = (bf16[256,256]{1,0:T(8,128)(2,1)S(1)}, bf16[256,256]{1,0:T(8,128)(2,1)}, u32[]{:S(2)}) copy-start(bf16[256,256]{1,0:T(8,128)(2,1)} %get-tuple-element.27) | copy-start | bytes 393220
  101.0 1.0 %copy-start.6 = (bf16[256,256]{1,0:T(8,128)(2,1)S(1)}, bf16[256,256]{1,0:T(8,128)(2,1)}, u32[]{:S(2)}) copy-start(bf16[256,256]{1,0:T(8,128)(2,1)} %get-tuple-element.18) | copy-start | bytes 393220
  (9 other events, 8.7 us)

commit v9 on v5

--- a/solution.py
+++ b/solution.py
@@ -118,9 +118,12 @@
     )
     outgoing = outgoing.reshape(peer_count, chunk_rows, channel_count)
     arrived = lax.all_to_all(outgoing, ("lat", "lon"), split_axis=0, concat_axis=0, tiled=True)
-    arrived_rows = arrived[:, :capacity].reshape(-1, channel_count)
+    arrived_rows = arrived.reshape(-1, channel_count)
     arrived_digits = arrived[:, capacity].astype(jnp.int32)
     arrived_key = arrived_digits[:, :capacity] * digit + arrived_digits[:, capacity : 2 * capacity]
+    arrived_key = jnp.concatenate(
+        [arrived_key, jnp.zeros((peer_count, chunk_rows - capacity), jnp.int32)], axis=1
+    )
     arrived_offsets = arrived_key.reshape(-1) - 1
     slot_table = (
         jnp.arange(slot_count, dtype=jnp.int32)[:, None] == arrived_offsets[None, :]

time: 97.1 us -> 95.1 us (0.979)
  local copies, waits for them, and re-layouts: 18.5 us -> 16.5 us
    reshape x1 -> x0, local copies, waits for them, and re-layouts: 1.43 us -> none  [body(): arrived_rows = arrived[:, :capacity].reshape(-1, channel_count)]
    unnamed x49 -> x45, local copies, waits for them, and re-layouts: 1.98 us -> 2.03 us
where the time goes in v9:
time: 95.1 us; the launch traced here: 93.6 us
  matrix products  32.5 us (34%)
  local copies, waits for them, and re-layouts  16.5 us (17%)
  other arithmetic  14.5 us (15%)
  waiting for transfers between devices  14.5 us (15%)
  starting transfers between devices  14.2 us (15%)
  between operations  1.31 us (1%)
    all_to_all x1, waiting for transfers between devices, body(): lax.all_to_all(outgoing, ('lat', 'lon'), split_axis=0, concat_axis=0, til...  14.5 us
    all_to_all x1, starting transfers between devices, body(): lax.all_to_all(outgoing, ('lat', 'lon'), split_axis=0, concat_axis=0, til...  11.2 us
    dot_general x1, matrix products, body(): jnp.dot(radiances, project_weight, preferred_element_type=jnp.float32)  8.82 us
    dot_general x1, matrix products, body(): jnp.dot(slot_table, arrived_rows, preferred_element_type=jnp.float32)  8.1 us
    dot_general x2, matrix products, cells(): numer = jnp.dot(weights, obs_masked, preferred_element_type=jnp.float32)  7.87 us
    reduce_sum x1, other arithmetic, body(): density = jnp.sum(masked, axis=1, dtype=jnp.float32)  6.28 us
    dot_general x1, matrix products, body(): jnp.dot(selector_all, sources, preferred_element_type=jnp.float32)  4.05 us
    squeeze x2, local copies, waits for them, and re-layouts, strided_valid(): kernel[row_tap, 0]  3.47 us
  transfers between devices with their start and end apart: 4, of which 1 were waited for; matrix products, arithmetic and copies ran while one was open for 24% of the time, Pallas kernels for 0%

profile of v9, /device:TPU:0, one launch (start us, length us, event | category | flops | bytes accessed | tf_op | source)
XLA Modules:
  0.0 93.6 jit_solution(16876992946318253374)
XLA Ops:
  0.1 0.7 broadcast_add_fusion
  2.5 3.1 %fusion.6 = pred[4096,1024]{1,0:T(32,128)(4,1)S(1)} fusion(s32[4096]{0:T(1024)S(1)} %add.119, pred[4096]{0:T(1024)(128)(4,1)S(1)} %and.61), kind=kLoop, calls=%fused_computation.9 | loop fusion | flops 8388608 | bytes 4214784 | tf_op jit(solution)/shard_map/and | solution.py:86
  5.6 1.4 %fusion.18 = pred[4096,128]{1,0:T(32,128)(4,1)S(1)} fusion(s32[4096]{0:T(1024)S(1)} %eq.99, pred[4096]{0:T(1024)(128)(4,1)S(1)} %eq.98), kind=kLoop, calls=%fused_computation.23 | loop fusion | flops 1048576 | bytes 544768 | tf_op jit(solution)/shard_map/and | solution.py:113
  7.0 8.8 %convolution_convert_fusion = bf16[1024,256]{1,0:T(8,128)(2,1)S(1)} fusion(bf16[1024,8461]{0,1:T(8,128)(2,1)} %param.8, bf16[8461,256]{1,0:T(8,128)(2,1)S(1)} %copy-done.20), kind=kOutput, calls=%fused_computation.33 | convolution fusion | flops 4436262912 | bytes 22184448 | tf_op jit(solution)/shard_map/dot_general | solution.py:88
  16.3 4.0 %fusion.7 = bf16[4096,256]{1,0:T(8,128)(2,1)} fusion(pred[4096,128]{1,0:T(32,128)(4,1)S(1)} %fusion.18, pred[4096,1024]{1,0:T(32,128)(4,1)S(1)} %fusion.6, bf16[128,256]{1,0:T(8,128)(2,1)S(1)} %fusion.34, bf16[1024,256]{1,0:T(8,128)(2,1)S(1)} %convolution_convert_fusion), kind=kOutput, calls=%fused_computation.10 | convolution fusion | flops 2422865920 | bytes 7405568 | tf_op jit(solution)/shard_map/dot_general | solution.py:116
  20.4 11.2 %all-to-all-start = ((bf16[128,32,256]{2,1,0:T(8,128)(2,1)}), bf16[128,32,256]{2,1,0:T(8,128)(2,1)S(1)}, u32[]{:S(2)}, u32[]{:S(2)}) async-start(bf16[128,32,256]{2,1,0:T(8,128)(2,1)} %bitcast.90), calls=%async_computation | async-start | bytes 4194304 | tf_op jit(solution)/shard_map/all_to_all | solution.py:120
  31.5 2.4 %slice.159 = bf16[64,3,2560]{2,1,0:T(4,128)(2,1)S(1)} slice(bf16[64,32,2560]{2,1,0:T(8,128)(2,1)} %param.13), slice={[0:64], [29:32], [0:2560]} | slice | bytes 1966080 | tf_op jit(solution)/shard_map/slice | solution.py:151
  34.6 6.3 %convert_reduce_fusion = f32[64,32]{1,0:T(8,128)S(1)} fusion(bf16[64,32,2560]{2,1,0:T(8,128)(2,1)} %param.13, pred[2560]{0:T(1024)(128)(4,1)S(1)} %iota_compare_fusion.16), kind=kLoop, calls=%fused_computation.2 | loop fusion | flops 15726592 | bytes 10496512 | tf_op jit(solution)/shard_map/reduce_sum | solution.py:139
  41.3 1.6 %reshape.172 = bf16[192,2560]{1,0:T(8,128)(2,1)} reshape(bf16[64,3,2560]{2,1,0:T(4,128)(2,1)S(1)} %slice.159) | data formatting | bytes 1966080 | tf_op jit(solution)/shard_map/reshape | solution.py:151
  43.0 2.5 %slice_bitcast_fusion.18 = (bf16[256,256]{1,0:T(8,128)(2,1)}, bf16[256,256]{1,0:T(8,128)(2,1)}, bf16[256,256]{1,0:T(8,128)(2,1)}, bf16[256,256]{1,0:T(8,128)(2,1...) fusion(bf16[3,3,256,256]{3,2,1,0:T(8,128)(2,1)} %param.14), kind=kLoop, calls=%fused_computation.153 | loop fusion | bytes 2359296 | tf_op jit(solution)/shard_map/squeeze | solution.py:34
  45.5 1.0 %slice_bitcast_fusion.9 = (bf16[256,256]{1,0:T(8,128)(2,1)}, bf16[256,256]{1,0:T(8,128)(2,1)S(1)}, bf16[256,256]{1,0:T(8,128)(2,1)}, bf16[256,256]{1,0:T(8,128)(...) fusion(bf16[3,3,256,256]{3,2,1,0:T(8,128)(2,1)S(1)} %copy-done), kind=kLoop, calls=%fused_computation.144 | loop fusion | bytes 2359296 | tf_op jit(solution)/shard_map/squeeze | solution.py:34
  46.5 14.5 %all-to-all-done = bf16[128,32,256]{2,1,0:T(8,128)(2,1)S(1)} async-done(((bf16[128,32,256]{2,1,0:T(8,128)(2,1)}), bf16[128,32,256]{2,1,0:T(8,128)(2,1)S(1)}, u32[]{:S(2)}, u32[]{:S(2)}) %all-to-all-start) | async-done | bytes 2097184 | tf_op jit(solution)/shard_map/all_to_all | solution.py:120
  61.4 8.1 %fusion.11 = bf16[2560,256]{1,0:T(8,128)(2,1)S(1)} fusion(bf16[4096,256]{1,0:T(8,128)(2,1)S(1)} %bitcast.89, s32[4096]{0:T(1024)S(1)} %sub.14, pred[2560]{0:T(1024)(128)(4,1)S(1)} %iota_compare_fusion.16), kind=kOutput, calls=%fused_computation.12 | convolution fusion | flops 5380505600 | bytes 3426816 | tf_op jit(solution)/shard_map/dot_general | solution.py:131
  69.6 0.5 fusion.31
  70.6 0.7 collective-permute-start.1
  71.3 0.5 collective-permute-start
  71.9 1.9 %collective-permute-start.2 = (bf16[64,3,256]{2,1,0:T(4,128)(2,1)S(1)}, bf16[64,3,256]{2,1,0:T(4,128)(2,1)S(1)}, u32[]{:S(2)}, u32[]{:S(2)}) collective-permute-start(bf16[64,3,256]{2,1,0:T(4,128)(2,1)S(1)} %reshape.179), channel_id=1, source_target_pairs={{0,1},{1,2},{2,3},{3,4},{4,5},{5,6},{6,7},{7,8},{8,9},{9,10},{10,1... | collective-permute-start | bytes 294920 | tf_op jit(solution)/shard_map/ppermute | solution.py:18
  73.8 7.3 %fusion.17 = bf16[2048,256]{0,1:T(8,128)(2,1)S(1)} fusion(bf16[2560,256]{1,0:T(8,128)(2,1)} %copy-done.21, bf16[2048,2560]{1,0:T(8,128)(2,1)} %bitcast.86, f32[2048]{0:T(1024)S(1)} %sqrt.22), kind=kOutput, calls=%fused_computation.21 | convolution fusion | flops 2685403136 | bytes 12853248 | tf_op jit(solution)/shard_map/dot_general | solution.py:144
  81.1 0.5 copy.22
  81.7 0.7 fusion.26
  82.9 1.1 %fusion.142 = (bf16[33,1,18,512]{3,2,1,0:T(8,128)(2,1)}, bf16[33,1,18,512]{3,2,1,0:T(8,128)(2,1)S(1)}, bf16[33,1,18,512]{3,2,1,0:T(8,128)(2,1)S(1)}) fusion(bf16[34,2,18,512]{3,2,1,0:T(8,128)(2,1)S(1)} %reshape.182), kind=kLoop, calls=%fused_computation.195 | loop fusion | bytes 3649536 | tf_op jit(solution)/shard_map/slice | solution.py:31
  84.0 2.2 %reshape_squeeze.18 = bf16[594,512]{1,0:T(8,128)(2,1)} reshape(bf16[33,1,18,512]{3,2,1,0:T(8,128)(2,1)} %get-tuple-element.11) | data formatting | bytes 1216512 | tf_op jit(solution)/shard_map/reshape;squeeze | solution.py:39
  86.6 1.6 %fusion.53 = f32[594,512]{1,0:T(8,128)S(1)} fusion(bf16[594,512]{1,0:T(8,128)(2,1)} %reshape_squeeze.18, bf16[256,256]{1,0:T(8,128)(2,1)S(1)} %copy-done.17, bf16[256,256]{1,0:T(8,128)(2,1)S(1)} %copy-done.18, bf16[256,256]{1,0:T(8,128)(2,1)S(1)} %copy-done.16), kind=kOutput, calls=%fused_computation.63 | convolution fusion | flops 313524224 | bytes 2217984 | tf_op jit(solution)/shard_map/dot_general | solution.py:39
  93.0 0.7 fusion.114
  (112 shorter events, 9.0 us)
Async XLA Ops:
  0.0 1.6 %copy-start.19 = (s32[1024]{0:T(1024)S(1)}, s32[1024]{0:T(1024)}, u32[]{:S(2)}) copy-start(s32[1024]{0:T(1024)} %param.10) | copy-start | bytes 12292
  2.5 4.5 %copy-start.20 = (bf16[8461,256]{1,0:T(8,128)(2,1)S(1)}, bf16[8461,256]{1,0:T(8,128)(2,1)}, u32[]{:S(2)}) copy-start(bf16[8461,256]{1,0:T(8,128)(2,1)} %param.9) | copy-start | bytes 12996100
  20.4 40.6 %all-to-all-start = ((bf16[128,32,256]{2,1,0:T(8,128)(2,1)}), bf16[128,32,256]{2,1,0:T(8,128)(2,1)S(1)}, u32[]{:S(2)}, u32[]{:S(2)}) async-start(bf16[128,32,256]{2,1,0:T(8,128)(2,1)} %bitcast.90), calls=%async_computation | async-start | bytes 4194304 | tf_op jit(solution)/shard_map/all_to_all | solution.py:120
  42.9 2.6 %copy-start = (bf16[3,3,256,256]{3,2,1,0:T(8,128)(2,1)S(1)}, bf16[3,3,256,256]{3,2,1,0:T(8,128)(2,1)}, u32[]{:S(2)}) copy-start(bf16[3,3,256,256]{3,2,1,0:T(8,128)(2,1)} %param.15) | copy-start | bytes 3538948
  61.4 8.1 %slice-start = ((bf16[64,32,2560]{2,1,0:T(8,128)(2,1)}), bf16[3,32,2560]{2,1,0:T(8,128)(2,1)S(1)}, s32[]{:S(2)}) async-start(bf16[64,32,2560]{2,1,0:T(8,128)(2,1)} %param.13), calls=%async_computation.1 | async-start | bytes 983040 | tf_op jit(solution)/shard_map/slice | solution.py:150
  61.4 8.1 %copy-start.1 = (bf16[192,2560]{1,0:T(8,128)(2,1)S(1)}, bf16[192,2560]{1,0:T(8,128)(2,1)}, u32[]{:S(2)}) copy-start(bf16[192,2560]{1,0:T(8,128)(2,1)} %reshape.172) | copy-start | bytes 2949124
  69.5 1.1 %copy-start.21 = (bf16[2560,256]{1,0:T(8,128)(2,1)}, bf16[2560,256]{1,0:T(8,128)(2,1)S(1)}, u32[]{:S(2)}) copy-start(bf16[2560,256]{1,0:T(8,128)(2,1)S(1)} %fusion.11) | copy-start | bytes 3932164
  70.6 11.0 %collective-permute-start.1 = (bf16[3,32,256]{2,1,0:T(8,128)(2,1)S(1)}, bf16[3,32,256]{2,1,0:T(8,128)(2,1)S(1)}, u32[]{:S(2)}, u32[]{:S(2)}) collective-permute-start(bf16[3,32,256]{2,1,0:T(8,128)(2,1)S(1)} %bitcast.92), channel_id=1, source_target_pairs={{0,16},{16,32},{32,48},{48,64},{64,80},{80,96},{96,112},{112,0},{1... | collective-permute-start | bytes 147464 | tf_op jit(solution)/shard_map/ppermute | solution.py:18
  71.3 10.3 %collective-permute-start = (bf16[3,3,256]{2,1,0:T(4,128)(2,1)S(1)}, bf16[3,3,256]{2,1,0:T(4,128)(2,1)S(1)}, u32[]{:S(2)}, u32[]{:S(2)}) collective-permute-start(bf16[3,3,256]{2,1,0:T(4,128)(2,1)S(1)} %slice.218), channel_id=1, source_target_pairs={{0,17},{1,18},{2,19},{3,20},{4,21},{5,22},{6,23},{7,24},{8,25},{9,... | collective-permute-start | bytes 13832 | tf_op jit(solution)/shard_map/ppermute | solution.py:18
  71.9 9.8 %collective-permute-start.2 = (bf16[64,3,256]{2,1,0:T(4,128)(2,1)S(1)}, bf16[64,3,256]{2,1,0:T(4,128)(2,1)S(1)}, u32[]{:S(2)}, u32[]{:S(2)}) collective-permute-start(bf16[64,3,256]{2,1,0:T(4,128)(2,1)S(1)} %reshape.179), channel_id=1, source_target_pairs={{0,1},{1,2},{2,3},{3,4},{4,5},{5,6},{6,7},{7,8},{8,9},{9,10},{10,1... | collective-permute-start | bytes 294920 | tf_op jit(solution)/shard_map/ppermute | solution.py:18
  84.0 2.6 %copy-start.16 = (bf16[256,256]{1,0:T(8,128)(2,1)S(1)}, bf16[256,256]{1,0:T(8,128)(2,1)}, u32[]{:S(2)}) copy-start(bf16[256,256]{1,0:T(8,128)(2,1)} %get-tuple-element.23) | copy-start | bytes 393220
  84.0 2.6 %copy-start.17 = (bf16[256,256]{1,0:T(8,128)(2,1)S(1)}, bf16[256,256]{1,0:T(8,128)(2,1)}, u32[]{:S(2)}) copy-start(bf16[256,256]{1,0:T(8,128)(2,1)} %get-tuple-element.28) | copy-start | bytes 393220
  84.0 2.6 %copy-start.18 = (bf16[256,256]{1,0:T(8,128)(2,1)S(1)}, bf16[256,256]{1,0:T(8,128)(2,1)}, u32[]{:S(2)}) copy-start(bf16[256,256]{1,0:T(8,128)(2,1)} %get-tuple-element.29) | copy-start | bytes 393220
  86.4 1.8 %copy-start.13 = (bf16[256,256]{1,0:T(8,128)(2,1)S(1)}, bf16[256,256]{1,0:T(8,128)(2,1)}, u32[]{:S(2)}) copy-start(bf16[256,256]{1,0:T(8,128)(2,1)} %get-tuple-element.25) | copy-start | bytes 393220
  86.4 1.8 %copy-start.14 = (bf16[256,256]{1,0:T(8,128)(2,1)S(1)}, bf16[256,256]{1,0:T(8,128)(2,1)}, u32[]{:S(2)}) copy-start(bf16[256,256]{1,0:T(8,128)(2,1)} %get-tuple-element.26) | copy-start | bytes 393220
  86.4 1.8 %copy-start.15 = (bf16[256,256]{1,0:T(8,128)(2,1)S(1)}, bf16[256,256]{1,0:T(8,128)(2,1)}, u32[]{:S(2)}) copy-start(bf16[256,256]{1,0:T(8,128)(2,1)} %get-tuple-element.27) | copy-start | bytes 393220
  88.2 1.0 %copy-start.11 = (bf16[256,256]{1,0:T(8,128)(2,1)S(1)}, bf16[256,256]{1,0:T(8,128)(2,1)}, u32[]{:S(2)}) copy-start(bf16[256,256]{1,0:T(8,128)(2,1)} %get-tuple-element.30) | copy-start | bytes 393220
  88.2 1.0 %copy-start.12 = (bf16[256,256]{1,0:T(8,128)(2,1)S(1)}, bf16[256,256]{1,0:T(8,128)(2,1)}, u32[]{:S(2)}) copy-start(bf16[256,256]{1,0:T(8,128)(2,1)} %get-tuple-element.31) | copy-start | bytes 393220
  90.6 1.0 %copy-start.8 = (bf16[256,256]{1,0:T(8,128)(2,1)S(1)}, bf16[256,256]{1,0:T(8,128)(2,1)}, u32[]{:S(2)}) copy-start(bf16[256,256]{1,0:T(8,128)(2,1)} %get-tuple-element.19) | copy-start | bytes 393220
  90.6 1.0 %copy-start.9 = (bf16[256,256]{1,0:T(8,128)(2,1)S(1)}, bf16[256,256]{1,0:T(8,128)(2,1)}, u32[]{:S(2)}) copy-start(bf16[256,256]{1,0:T(8,128)(2,1)} %get-tuple-element.20) | copy-start | bytes 393220
  90.8 1.0 %copy-start.4 = (bf16[256,256]{1,0:T(8,128)(2,1)S(1)}, bf16[256,256]{1,0:T(8,128)(2,1)}, u32[]{:S(2)}) copy-start(bf16[256,256]{1,0:T(8,128)(2,1)} %get-tuple-element.16) | copy-start | bytes 393220
  90.8 1.0 %copy-start.5 = (bf16[256,256]{1,0:T(8,128)(2,1)S(1)}, bf16[256,256]{1,0:T(8,128)(2,1)}, u32[]{:S(2)}) copy-start(bf16[256,256]{1,0:T(8,128)(2,1)} %get-tuple-element.17) | copy-start | bytes 393220
  90.8 1.0 %copy-start.6 = (bf16[256,256]{1,0:T(8,128)(2,1)S(1)}, bf16[256,256]{1,0:T(8,128)(2,1)}, u32[]{:S(2)}) copy-start(bf16[256,256]{1,0:T(8,128)(2,1)} %get-tuple-element.18) | copy-start | bytes 393220
  91.6 1.0 %copy-start.3 = (bf16[256,256]{1,0:T(8,128)(2,1)S(1)}, bf16[256,256]{1,0:T(8,128)(2,1)}, u32[]{:S(2)}) copy-start(bf16[256,256]{1,0:T(8,128)(2,1)} %get-tuple-element.22) | copy-start | bytes 393220
  (3 other events, 2.7 us)

commit v10 on v9

--- a/solution.py
+++ b/solution.py
@@ -25,8 +25,8 @@
     padded = jnp.pad(field, ((0, even_h - height), (0, even_w - breadth), (0, 0)))
     pairs = padded.reshape(even_h // 2, 2, even_w // 2, 2 * depth)
     zero_block = jnp.zeros((depth, depth), kernel.dtype)
-    near = jnp.zeros((out_rows * (even_w // 2), depth), jnp.float32)
-    far = jnp.zeros((out_rows * (even_w // 2), depth), jnp.float32)
+    near = jnp.zeros((out_rows, even_w // 2, depth), jnp.float32)
+    far = jnp.zeros((out_rows, even_w // 2, depth), jnp.float32)
     for row_tap in range(3):
         rows = pairs[row_tap // 2 : row_tap // 2 + out_rows, row_tap % 2]
         stacked = jnp.concatenate(
@@ -36,11 +36,9 @@
             ],
             axis=0,
         )
-        both = jnp.dot(rows.reshape(-1, 2 * depth), stacked, preferred_element_type=jnp.float32)
-        near = near + both[:, :depth]
-        far = far + both[:, depth:]
-    near = near.reshape(out_rows, even_w // 2, depth)
-    far = far.reshape(out_rows, even_w // 2, depth)
+        both = jnp.einsum("ijc,cd->ijd", rows, stacked, preferred_element_type=jnp.float32)
+        near = near + both[:, :, :depth]
+        far = far + both[:, :, depth:]
     return near[:, :out_cols] + far[:, 1 : out_cols + 1]
 
 

time: 95.1 us -> 92.1 us (0.968)
  local copies, waits for them, and re-layouts: 16.5 us -> 15.3 us
    another operation x8 -> x2, local copies, waits for them, and re-layouts: 3.13 us -> 0.38 us  [the longest x6 2.75 us: strided_valid(): rows.reshape(-1, 2 * depth)]
    unnamed x45 -> x46, local copies, waits for them, and re-layouts: 2.03 us -> 3.52 us
  transfers between devices with their start and end apart: 4 -> 4, of which waited for: 1 -> 1; matrix products, arithmetic and copies ran while one was open for 24% -> 25% of each run, Pallas kernels for 0% -> 0%
where the time goes in v10:
time: 92.1 us; the launch traced here: 90.6 us
  matrix products  31.7 us (34%)
  local copies, waits for them, and re-layouts  15.3 us (17%)
  waiting for transfers between devices  14.5 us (16%)
  starting transfers between devices  14.3 us (16%)
  other arithmetic  13.6 us (15%)
  between operations  1.29 us (1%)
    all_to_all x1, waiting for transfers between devices, body(): lax.all_to_all(outgoing, ('lat', 'lon'), split_axis=0, concat_axis=0, til...  14.5 us
    all_to_all x1, starting transfers between devices, body(): lax.all_to_all(outgoing, ('lat', 'lon'), split_axis=0, concat_axis=0, til...  11.2 us
    dot_general x1, matrix products, body(): jnp.dot(radiances, project_weight, preferred_element_type=jnp.float32)  8.82 us
    dot_general x1, matrix products, body(): jnp.dot(slot_table, arrived_rows, preferred_element_type=jnp.float32)  8.09 us
    dot_general x2, matrix products, cells(): numer = jnp.dot(weights, obs_masked, preferred_element_type=jnp.float32)  7.87 us
    reduce_sum x1, other arithmetic, body(): density = jnp.sum(masked, axis=1, dtype=jnp.float32)  6.28 us
    dot_general x1, matrix products, body(): jnp.dot(selector_all, sources, preferred_element_type=jnp.float32)  4.03 us
    unnamed x46, local copies, waits for them, and re-layouts  3.52 us
  transfers between devices with their start and end apart: 4, of which 1 were waited for; matrix products, arithmetic and copies ran while one was open for 25% of the time, Pallas kernels for 0%

profile of v10, /device:TPU:0, one launch (start us, length us, event | category | flops | bytes accessed | tf_op | source)
XLA Modules:
  0.0 90.6 jit_solution(12762961441926166745)
XLA Ops:
  0.1 0.7 broadcast_add_fusion
  2.5 3.1 %fusion.6 = pred[4096,1024]{1,0:T(32,128)(4,1)S(1)} fusion(s32[4096]{0:T(1024)S(1)} %add.119, pred[4096]{0:T(1024)(128)(4,1)S(1)} %and.61), kind=kLoop, calls=%fused_computation.9 | loop fusion | flops 8388608 | bytes 4214784 | tf_op jit(solution)/shard_map/and | solution.py:84
  5.6 1.4 %fusion.18 = pred[4096,128]{1,0:T(32,128)(4,1)S(1)} fusion(s32[4096]{0:T(1024)S(1)} %eq.99, pred[4096]{0:T(1024)(128)(4,1)S(1)} %eq.98), kind=kLoop, calls=%fused_computation.23 | loop fusion | flops 1048576 | bytes 544768 | tf_op jit(solution)/shard_map/and | solution.py:111
  7.0 8.8 %convolution_convert_fusion = bf16[1024,256]{1,0:T(8,128)(2,1)S(1)} fusion(bf16[1024,8461]{0,1:T(8,128)(2,1)} %param.8, bf16[8461,256]{1,0:T(8,128)(2,1)S(1)} %copy-done.20), kind=kOutput, calls=%fused_computation.33 | convolution fusion | flops 4436262912 | bytes 22184448 | tf_op jit(solution)/shard_map/dot_general | solution.py:86
  16.3 4.0 %fusion.7 = bf16[4096,256]{1,0:T(8,128)(2,1)} fusion(pred[4096,128]{1,0:T(32,128)(4,1)S(1)} %fusion.18, pred[4096,1024]{1,0:T(32,128)(4,1)S(1)} %fusion.6, bf16[128,256]{1,0:T(8,128)(2,1)S(1)} %fusion.34, bf16[1024,256]{1,0:T(8,128)(2,1)S(1)} %convolution_convert_fusion), kind=kOutput, calls=%fused_computation.10 | convolution fusion | flops 2422865920 | bytes 7405568 | tf_op jit(solution)/shard_map/dot_general | solution.py:114
  20.3 11.2 %all-to-all-start = ((bf16[128,32,256]{2,1,0:T(8,128)(2,1)}), bf16[128,32,256]{2,1,0:T(8,128)(2,1)S(1)}, u32[]{:S(2)}, u32[]{:S(2)}) async-start(bf16[128,32,256]{2,1,0:T(8,128)(2,1)} %bitcast.120), calls=%async_computation | async-start | bytes 4194304 | tf_op jit(solution)/shard_map/all_to_all | solution.py:118
  31.5 2.4 %slice.159 = bf16[64,3,2560]{2,1,0:T(4,128)(2,1)S(1)} slice(bf16[64,32,2560]{2,1,0:T(8,128)(2,1)} %param.13), slice={[0:64], [29:32], [0:2560]} | slice | bytes 1966080 | tf_op jit(solution)/shard_map/slice | solution.py:149
  34.6 6.3 %convert_reduce_fusion = f32[64,32]{1,0:T(8,128)S(1)} fusion(bf16[64,32,2560]{2,1,0:T(8,128)(2,1)} %param.13, pred[2560]{0:T(1024)(128)(4,1)S(1)} %iota_compare_fusion.16), kind=kLoop, calls=%fused_computation.2 | loop fusion | flops 15726592 | bytes 10496512 | tf_op jit(solution)/shard_map/reduce_sum | solution.py:137
  41.3 1.6 %reshape.160 = bf16[192,2560]{1,0:T(8,128)(2,1)} reshape(bf16[64,3,2560]{2,1,0:T(4,128)(2,1)S(1)} %slice.159) | data formatting | bytes 1966080 | tf_op jit(solution)/shard_map/reshape | solution.py:149
  43.0 2.5 %slice_bitcast_fusion.18 = (bf16[256,256]{1,0:T(8,128)(2,1)}, bf16[256,256]{1,0:T(8,128)(2,1)}, bf16[256,256]{1,0:T(8,128)(2,1)}, bf16[256,256]{1,0:T(8,128)(2,1...) fusion(bf16[3,3,256,256]{3,2,1,0:T(8,128)(2,1)} %param.14), kind=kLoop, calls=%fused_computation.159 | loop fusion | bytes 2359296 | tf_op jit(solution)/shard_map/squeeze | solution.py:34
  45.5 1.0 %slice_bitcast_fusion.9 = (bf16[256,256]{1,0:T(8,128)(2,1)}, bf16[256,256]{1,0:T(8,128)(2,1)S(1)}, bf16[256,256]{1,0:T(8,128)(2,1)}, bf16[256,256]{1,0:T(8,128)(...) fusion(bf16[3,3,256,256]{3,2,1,0:T(8,128)(2,1)S(1)} %copy-done), kind=kLoop, calls=%fused_computation.150 | loop fusion | bytes 2359296 | tf_op jit(solution)/shard_map/squeeze | solution.py:34
  46.5 14.5 %all-to-all-done = bf16[128,32,256]{2,1,0:T(8,128)(2,1)S(1)} async-done(((bf16[128,32,256]{2,1,0:T(8,128)(2,1)}), bf16[128,32,256]{2,1,0:T(8,128)(2,1)S(1)}, u32[]{:S(2)}, u32[]{:S(2)}) %all-to-all-start) | async-done | bytes 2097184 | tf_op jit(solution)/shard_map/all_to_all | solution.py:118
  61.4 8.1 %fusion.11 = bf16[2560,256]{1,0:T(8,128)(2,1)S(1)} fusion(bf16[4096,256]{1,0:T(8,128)(2,1)S(1)} %bitcast.119, s32[4096]{0:T(1024)S(1)} %sub.14, pred[2560]{0:T(1024)(128)(4,1)S(1)} %iota_compare_fusion.16), kind=kOutput, calls=%fused_computation.12 | convolution fusion | flops 5380505600 | bytes 3426816 | tf_op jit(solution)/shard_map/dot_general | solution.py:129
  70.6 0.7 collective-permute-start.1
  71.9 1.9 %collective-permute-start.2 = (bf16[64,3,256]{2,1,0:T(4,128)(2,1)S(1)}, bf16[64,3,256]{2,1,0:T(4,128)(2,1)S(1)}, u32[]{:S(2)}, u32[]{:S(2)}) collective-permute-start(bf16[64,3,256]{2,1,0:T(4,128)(2,1)S(1)} %reshape.167), channel_id=1, source_target_pairs={{0,1},{1,2},{2,3},{3,4},{4,5},{5,6},{6,7},{7,8},{8,9},{9,10},{10,1... | collective-permute-start | bytes 294920 | tf_op jit(solution)/shard_map/ppermute | solution.py:18
  73.8 7.3 %fusion.17 = bf16[2048,256]{0,1:T(8,128)(2,1)S(1)} fusion(bf16[2560,256]{1,0:T(8,128)(2,1)} %copy-done.21, bf16[2048,2560]{1,0:T(8,128)(2,1)} %bitcast.116, f32[2048]{0:T(1024)S(1)} %sqrt.22), kind=kOutput, calls=%fused_computation.21 | convolution fusion | flops 2685403136 | bytes 12853248 | tf_op jit(solution)/shard_map/dot_general | solution.py:142
  81.7 0.7 fusion.26
  83.1 0.7 copy-done.16
  83.9 0.5 fusion.41
  84.7 0.7 copy-done.13
  85.5 0.5 fusion.42
  86.1 0.6 fusion.43
  89.0 0.5 copy-done.2
  90.0 0.7 copy.47
  (107 shorter events, 8.9 us)
Async XLA Ops:
  0.0 1.6 %copy-start.19 = (s32[1024]{0:T(1024)S(1)}, s32[1024]{0:T(1024)}, u32[]{:S(2)}) copy-start(s32[1024]{0:T(1024)} %param.10) | copy-start | bytes 12292
  2.5 4.5 %copy-start.20 = (bf16[8461,256]{1,0:T(8,128)(2,1)S(1)}, bf16[8461,256]{1,0:T(8,128)(2,1)}, u32[]{:S(2)}) copy-start(bf16[8461,256]{1,0:T(8,128)(2,1)} %param.9) | copy-start | bytes 12996100
  20.3 40.6 %all-to-all-start = ((bf16[128,32,256]{2,1,0:T(8,128)(2,1)}), bf16[128,32,256]{2,1,0:T(8,128)(2,1)S(1)}, u32[]{:S(2)}, u32[]{:S(2)}) async-start(bf16[128,32,256]{2,1,0:T(8,128)(2,1)} %bitcast.120), calls=%async_computation | async-start | bytes 4194304 | tf_op jit(solution)/shard_map/all_to_all | solution.py:118
  42.9 2.6 %copy-start = (bf16[3,3,256,256]{3,2,1,0:T(8,128)(2,1)S(1)}, bf16[3,3,256,256]{3,2,1,0:T(8,128)(2,1)}, u32[]{:S(2)}) copy-start(bf16[3,3,256,256]{3,2,1,0:T(8,128)(2,1)} %param.15) | copy-start | bytes 3538948
  61.4 8.1 %slice-start = ((bf16[64,32,2560]{2,1,0:T(8,128)(2,1)}), bf16[3,32,2560]{2,1,0:T(8,128)(2,1)S(1)}, s32[]{:S(2)}) async-start(bf16[64,32,2560]{2,1,0:T(8,128)(2,1)} %param.13), calls=%async_computation.1 | async-start | bytes 983040 | tf_op jit(solution)/shard_map/slice | solution.py:148
  61.4 8.1 %copy-start.1 = (bf16[192,2560]{1,0:T(8,128)(2,1)S(1)}, bf16[192,2560]{1,0:T(8,128)(2,1)}, u32[]{:S(2)}) copy-start(bf16[192,2560]{1,0:T(8,128)(2,1)} %reshape.160) | copy-start | bytes 2949124
  69.5 1.1 %copy-start.21 = (bf16[2560,256]{1,0:T(8,128)(2,1)}, bf16[2560,256]{1,0:T(8,128)(2,1)S(1)}, u32[]{:S(2)}) copy-start(bf16[2560,256]{1,0:T(8,128)(2,1)S(1)} %fusion.11) | copy-start | bytes 3932164
  70.6 11.0 %collective-permute-start.1 = (bf16[3,32,256]{2,1,0:T(8,128)(2,1)S(1)}, bf16[3,32,256]{2,1,0:T(8,128)(2,1)S(1)}, u32[]{:S(2)}, u32[]{:S(2)}) collective-permute-start(bf16[3,32,256]{2,1,0:T(8,128)(2,1)S(1)} %bitcast.122), channel_id=1, source_target_pairs={{0,16},{16,32},{32,48},{48,64},{64,80},{80,96},{96,112},{112,0},{1... | collective-permute-start | bytes 147464 | tf_op jit(solution)/shard_map/ppermute | solution.py:18
  71.3 10.3 %collective-permute-start = (bf16[3,3,256]{2,1,0:T(4,128)(2,1)S(1)}, bf16[3,3,256]{2,1,0:T(4,128)(2,1)S(1)}, u32[]{:S(2)}, u32[]{:S(2)}) collective-permute-start(bf16[3,3,256]{2,1,0:T(4,128)(2,1)S(1)} %slice.218), channel_id=1, source_target_pairs={{0,17},{1,18},{2,19},{3,20},{4,21},{5,22},{6,23},{7,24},{8,25},{9,... | collective-permute-start | bytes 13832 | tf_op jit(solution)/shard_map/ppermute | solution.py:18
  71.9 9.8 %collective-permute-start.2 = (bf16[64,3,256]{2,1,0:T(4,128)(2,1)S(1)}, bf16[64,3,256]{2,1,0:T(4,128)(2,1)S(1)}, u32[]{:S(2)}, u32[]{:S(2)}) collective-permute-start(bf16[64,3,256]{2,1,0:T(4,128)(2,1)S(1)} %reshape.167), channel_id=1, source_target_pairs={{0,1},{1,2},{2,3},{3,4},{4,5},{5,6},{6,7},{7,8},{8,9},{9,10},{10,1... | collective-permute-start | bytes 294920 | tf_op jit(solution)/shard_map/ppermute | solution.py:18
  82.9 1.0 %copy-start.17 = (bf16[256,256]{1,0:T(8,128)(2,1)S(1)}, bf16[256,256]{1,0:T(8,128)(2,1)}, u32[]{:S(2)}) copy-start(bf16[256,256]{1,0:T(8,128)(2,1)} %get-tuple-element.34) | copy-start | bytes 393220
  82.9 1.0 %copy-start.18 = (bf16[256,256]{1,0:T(8,128)(2,1)S(1)}, bf16[256,256]{1,0:T(8,128)(2,1)}, u32[]{:S(2)}) copy-start(bf16[256,256]{1,0:T(8,128)(2,1)} %get-tuple-element.35) | copy-start | bytes 393220
  84.5 1.0 %copy-start.14 = (bf16[256,256]{1,0:T(8,128)(2,1)S(1)}, bf16[256,256]{1,0:T(8,128)(2,1)}, u32[]{:S(2)}) copy-start(bf16[256,256]{1,0:T(8,128)(2,1)} %get-tuple-element.30) | copy-start | bytes 393220
  84.5 1.0 %copy-start.15 = (bf16[256,256]{1,0:T(8,128)(2,1)S(1)}, bf16[256,256]{1,0:T(8,128)(2,1)}, u32[]{:S(2)}) copy-start(bf16[256,256]{1,0:T(8,128)(2,1)} %get-tuple-element.31) | copy-start | bytes 393220
  84.7 1.4 %copy-start.10 = (bf16[256,256]{1,0:T(8,128)(2,1)S(1)}, bf16[256,256]{1,0:T(8,128)(2,1)}, u32[]{:S(2)}) copy-start(bf16[256,256]{1,0:T(8,128)(2,1)} %get-tuple-element.27) | copy-start | bytes 393220
  84.7 1.4 %copy-start.11 = (bf16[256,256]{1,0:T(8,128)(2,1)S(1)}, bf16[256,256]{1,0:T(8,128)(2,1)}, u32[]{:S(2)}) copy-start(bf16[256,256]{1,0:T(8,128)(2,1)} %get-tuple-element.32) | copy-start | bytes 393220
  84.7 1.4 %copy-start.12 = (bf16[256,256]{1,0:T(8,128)(2,1)S(1)}, bf16[256,256]{1,0:T(8,128)(2,1)}, u32[]{:S(2)}) copy-start(bf16[256,256]{1,0:T(8,128)(2,1)} %get-tuple-element.33) | copy-start | bytes 393220
  87.4 1.0 %copy-start.8 = (bf16[256,256]{1,0:T(8,128)(2,1)S(1)}, bf16[256,256]{1,0:T(8,128)(2,1)}, u32[]{:S(2)}) copy-start(bf16[256,256]{1,0:T(8,128)(2,1)} %get-tuple-element.23) | copy-start | bytes 393220
  87.4 1.0 %copy-start.9 = (bf16[256,256]{1,0:T(8,128)(2,1)S(1)}, bf16[256,256]{1,0:T(8,128)(2,1)}, u32[]{:S(2)}) copy-start(bf16[256,256]{1,0:T(8,128)(2,1)} %get-tuple-element.24) | copy-start | bytes 393220
  87.6 1.0 %copy-start.4 = (bf16[256,256]{1,0:T(8,128)(2,1)S(1)}, bf16[256,256]{1,0:T(8,128)(2,1)}, u32[]{:S(2)}) copy-start(bf16[256,256]{1,0:T(8,128)(2,1)} %get-tuple-element.20) | copy-start | bytes 393220
  87.7 1.0 %copy-start.5 = (bf16[256,256]{1,0:T(8,128)(2,1)S(1)}, bf16[256,256]{1,0:T(8,128)(2,1)}, u32[]{:S(2)}) copy-start(bf16[256,256]{1,0:T(8,128)(2,1)} %get-tuple-element.21) | copy-start | bytes 393220
  87.7 1.0 %copy-start.6 = (bf16[256,256]{1,0:T(8,128)(2,1)S(1)}, bf16[256,256]{1,0:T(8,128)(2,1)}, u32[]{:S(2)}) copy-start(bf16[256,256]{1,0:T(8,128)(2,1)} %get-tuple-element.22) | copy-start | bytes 393220
  88.6 0.9 %copy-start.2 = (bf16[256,256]{1,0:T(8,128)(2,1)S(1)}, bf16[256,256]{1,0:T(8,128)(2,1)}, u32[]{:S(2)}) copy-start(bf16[256,256]{1,0:T(8,128)(2,1)} %get-tuple-element.25) | copy-start | bytes 393220
  88.6 1.0 %copy-start.3 = (bf16[256,256]{1,0:T(8,128)(2,1)S(1)}, bf16[256,256]{1,0:T(8,128)(2,1)}, u32[]{:S(2)}) copy-start(bf16[256,256]{1,0:T(8,128)(2,1)} %get-tuple-element.26) | copy-start | bytes 393220
  (3 other events, 2.7 us)
